TPU v7x, 32 devices: a whole 2x2x4 slice. The times are simulated.
32 devices in a mesh: grp: 4 (over y, x), rows: 8 (over z, core).
Axes of the slice: x: 2, y: 2, z: 4, core: 2. Of those that a mesh axis runs over, the one named last changes fastest.
Arguments:
- stationary: bfloat16 [81920, 512], P(('grp', 'rows')), may hold values from -6 to 6
- rotor_rows: bfloat16 [1024, 512], P(('grp', 'rows')), may hold values from -6 to 6
- owners: int32 [1024, 1], P(('grp', 'rows')), may hold values from 0 to 7; in each aligned block of 32 rows (0 to 31, 32 to 63, ...) at most 6 rows name the same one
- counts: int32 [32], P(('grp', 'rows')), may hold values from 24 to 32
- omega: bfloat16 [512, 192], replicated, may hold values from -0.25 to 0.25
Outputs:
- basis_stationary: bfloat16 [81920, 192], P(('grp', 'rows'))
- basis_rotor: bfloat16 [1536, 192], P(('grp', 'rows'))
- factor: float32 [192, 192], replicated
Inputs may be any that keep to these rules, and one draw needn't show every extreme that they name: `owners`: in the rotor rows of one device no owner is named more than 6 times.
All inputs are finite; a program needn't handle non-finite values.
Results may differ from a plain program's by a relative error of at most 0.0056.
Values may be sent and summed in bfloat16 or wider, within the bound.
No kernel may reach another device: no remote copies, remote signals or barrier semaphores. Data moves between devices by JAX's collectives and lax.ppermute only.
A program may use at most 64 MiB of HBM per device.

v0:
```python
import jax
import jax.numpy as jnp
from jax import lax
from jax.sharding import PartitionSpec as P

CAP = 6


def sketch_block(block, omega):
    return jnp.dot(block, omega, preferred_element_type=jnp.float32).astype(jnp.bfloat16)


def per_device(stationary, rotor_rows, owners, counts, omega):
    n_rows = lax.axis_size("rows")
    n_grp = lax.axis_size("grp")
    rot_dev = rotor_rows.shape[0]
    stat_dev = stationary.shape[0]
    total = n_grp * n_rows * (stat_dev + rot_dev)
    targets = owners[:, 0]
    live = lax.iota(jnp.int32, rot_dev) < counts[0]
    onehot = ((targets[:, None] == lax.iota(jnp.int32, n_rows)[None, :]) & live[:, None]).astype(
        jnp.int32
    )
    rank = jnp.sum((jnp.cumsum(onehot, axis=0) - onehot) * onehot, axis=1)
    slot = jnp.where(live, targets * CAP + rank, -1)
    select = (lax.iota(jnp.int32, n_rows * CAP)[:, None] == slot[None, :]).astype(jnp.bfloat16)
    sketch_stat = sketch_block(stationary, omega)
    outgoing = jnp.dot(select, rotor_rows, preferred_element_type=jnp.float32).astype(jnp.bfloat16)
    outgoing = outgoing.reshape(n_rows, CAP, -1)
    arrived_rows = lax.all_to_all(outgoing, "rows", split_axis=0, concat_axis=0, tiled=True)
    arrived = sketch_block(arrived_rows.reshape(n_rows * CAP, -1), omega)
    local = jnp.concatenate([sketch_stat, arrived], axis=0)
    gram = (
        lax.dot_general(local, local, (((0,), (0,)), ((), ())), preferred_element_type=jnp.float32)
        / total
    )
    lower = jnp.linalg.cholesky(lax.psum(gram, ("grp", "rows")))
    solved = lax.linalg.triangular_solve(
        lower, local.astype(jnp.float32).T, left_side=True, lower=True
    )
    basis = solved.T.astype(jnp.bfloat16)
    return (basis[:stat_dev], basis[stat_dev:], lower.T)


def solution(mesh):
    return jax.shard_map(
        per_device,
        mesh=mesh,
        in_specs=(
            P(("grp", "rows"), None),
            P(("grp", "rows"), None),
            P(("grp", "rows"), None),
            P(("grp", "rows")),
            P(),
        ),
        out_specs=(P(("grp", "rows"), None), P(("grp", "rows"), None), P()),
        check_vma=False,
    )
```

profile of v0, /device:TPU:0, one launch (start us, length us, event | category | flops | bytes accessed | tf_op | source)
XLA Modules:
  0.0 226.5 jit_solution(445382293434304383)
XLA Ops:
  8.0 0.7 fusion.12
  8.8 0.8 select_reduce_fusion.2
  9.6 0.7 add_select_fusion
  10.3 0.9 convolution_convert_fusion.2
  11.2 0.7 reshape.49
  11.8 6.4 %all-to-all-start = ((bf16[8,6,512]{2,1,0:T(8,128)(2,1)}), bf16[8,6,512]{2,1,0:T(8,128)(2,1)S(1)}, u32[]{:S(2)}, u32[]{:S(2)}) async-start(bf16[8,6,512]{2,1,0:T(8,128)(2,1)} %reshape.49), calls=%async_computation | async-start | bytes 131072 | tf_op jit(solution)/shard_map/all_to_all | solution.py:30
  18.3 2.9 %convolution_convert_fusion = bf16[2560,192]{0,1:T(8,128)(2,1)} fusion(bf16[2560,512]{1,0:T(8,128)(2,1)S(1)} %copy-done, bf16[512,192]{0,1:T(8,128)(2,1)} %param.9), kind=kOutput, calls=%fused_computation | convolution fusion | flops 503808000 | bytes 3801088 | tf_op jit(solution)/shard_map/dot_general | solution.py:10
  21.2 2.9 %all-to-all-done = bf16[8,6,512]{2,1,0:T(8,128)(2,1)S(1)} async-done(((bf16[8,6,512]{2,1,0:T(8,128)(2,1)}), bf16[8,6,512]{2,1,0:T(8,128)(2,1)S(1)}, u32[]{:S(2)}, u32[]{:S(2)}) %all-to-all-start) | async-done | bytes 49184 | tf_op jit(solution)/shard_map/all_to_all | solution.py:30
  24.1 0.2 convolution_convert_fusion.3
  24.4 2.7 %convolution_multiply_fusion = f32[192,192]{0,1:T(8,128)} fusion(bf16[48,192]{0,1:T(8,128)(2,1)S(1)} %copy.20, bf16[2560,192]{0,1:T(8,128)(2,1)} %convolution_convert_fusion), kind=kOutput, calls=%fused_computation.4 | convolution fusion | flops 194322432 | bytes 1148928 | tf_op jit(solution)/shard_map/dot_general | solution.py:34
  27.1 2.3 fusion.2
  29.4 121.9 %all-reduce.5.cloned.1.call-done = f32[192,192]{0,1:T(8,128)} async-done(((f32[192,192]{0,1:T(8,128)}), f32[192,192]{0,1:T(8,128)}) %all-reduce.5.cloned.1.call-update) | async-done | bytes 147472 | tf_op jit(solution)/shard_map/psum | solution.py:37
  151.3 1.0 copy.22
  152.3 1.0 fusion.3
  153.3 11.7 %cholesky.51 = f32[128,128]{1,0:T(8,128)S(1)} custom-call(f32[128,128]{1,0:T(8,128)S(1)} %cholesky.124), custom_call_target="Cholesky" | custom-call | tf_op jit(solution)/shard_map/jit(cholesky)/cholesky | solution.py:37
  165.0 0.6 compare_reduce_fusion.1
  165.7 9.8 %custom-call.14 = f32[1,128,128]{1,2,0:T(8,128)S(1)} custom-call(f32[1,128,128]{2,1,0:T(8,128)S(1)} %get-tuple-element.35), custom_call_target="InvertDiagBlocksLowerTriangular" | custom-call | tf_op jit(solution)/shard_map/jit(cholesky)/cholesky | solution.py:37
  175.5 0.2 constant_dynamic-update-slice_fusion.1
  175.7 0.2 convolution_subtract_fusion.1
  175.9 5.8 %cholesky.110 = f32[64,64]{1,0:T(8,128)S(1)} custom-call(f32[64,64]{1,0:T(8,128)S(1)} %convolution_subtract_fusion.1), custom_call_target="Cholesky" | custom-call | tf_op jit(solution)/shard_map/jit(cholesky)/cholesky | solution.py:37
  181.8 0.6 compare_reduce_fusion
  183.9 0.5 copy-done.2
  184.4 20.3 %custom-call.15 = f32[2,128,128]{1,2,0:T(8,128)} custom-call(f32[2,128,128]{2,1,0:T(8,128)S(1)} %pad_maximum_fusion.2), custom_call_target="InvertDiagBlocksLowerTriangular" | custom-call | tf_op jit(solution)/shard_map/triangular_solve | solution.py:38
  204.7 2.0 fusion.15
  206.7 2.4 %convolution_subtract_fusion = f32[64,2608]{1,0:T(8,128)S(1)} fusion(f32[128,2608]{0,1:T(8,128)S(1)} %get-tuple-element.41, bf16[192,2608]{1,0:T(8,128)(2,1)} %fusion.2, f32[192,192]{1,0:T(8,128)} %copy-done.2), kind=kOutput, calls=%fused_computation.1 | convolution fusion | flops 256710656 | bytes 2379776 | tf_op jit(solution)/shard_map/triangular_solve | solution.py:38
  209.1 2.2 convolution_convert_fusion.1
  211.4 2.1 copy.23
  213.5 1.3 maximum_bitcast_fusion
  214.8 0.6 slice.72
  215.4 1.1 slice.71
  216.6 0.8 copy.25
  217.4 2.3 %copy.24 = bf16[2560,192]{0,1:T(8,128)(2,1)} copy(bf16[2560,192]{1,0:T(8,128)(2,1)} %slice.71) | data formatting | bytes 1966080
  (21 shorter events, 0.5 us)
Async XLA Ops:
  7.2 11.1 %copy-start = (bf16[2560,512]{1,0:T(8,128)(2,1)S(1)}, bf16[2560,512]{1,0:T(8,128)(2,1)}, u32[]{:S(2)}) copy-start(bf16[2560,512]{1,0:T(8,128)(2,1)} %param.5) | copy-start | bytes 7864324
  11.8 12.3 %all-to-all-start = ((bf16[8,6,512]{2,1,0:T(8,128)(2,1)}), bf16[8,6,512]{2,1,0:T(8,128)(2,1)S(1)}, u32[]{:S(2)}, u32[]{:S(2)}) async-start(bf16[8,6,512]{2,1,0:T(8,128)(2,1)} %reshape.49), calls=%async_computation | async-start | bytes 131072 | tf_op jit(solution)/shard_map/all_to_all | solution.py:30
  18.2 133.1 %all-reduce.5.cloned.1.call-start = ((), (), s32[]{:S(2)}) async-start(), calls=%async_computation.1 | async-start | bytes 393216 | tf_op jit(solution)/shard_map/psum | solution.py:37
  18.2 5.9 %copy-start.1 = (bf16[512,192]{0,1:T(8,128)(2,1)S(1)}, bf16[512,192]{0,1:T(8,128)(2,1)}, u32[]{:S(2)}) copy-start(bf16[512,192]{0,1:T(8,128)(2,1)} %param.9) | copy-start | bytes 589828
  183.8 0.7 copy-start.2
Sparse Core Ops, SparseCore 0:
  27.2 124.0 all-reduce.4
where the time goes:
time: 228 us; the launch traced here: 227 us
  waiting for transfers between devices  125 us (55%)
  other arithmetic  56 us (25%)
  between operations  16.3 us (7%)
  matrix products  13.7 us (6%)
  local copies, waits for them, and re-layouts  9.36 us (4%)
  starting transfers between devices  6.39 us (3%)
    psum x1, waiting for transfers between devices, per_device(): lower = jnp.linalg.cholesky(lax.psum(gram, ('grp', 'rows')))  122 us
    another operation x7, other arithmetic, per_device(): lower = jnp.linalg.cholesky(lax.psum(gram, ('grp', 'rows')))  28.7 us
    another operation x5, other arithmetic, per_device(): lax.linalg.triangular_solve(lower, local.astype(jnp.float32).T, left_side...  20.4 us
    another operation x3, matrix products, per_device(): lax.linalg.triangular_solve(lower, local.astype(jnp.float32).T, left_side...  6.65 us
    all_to_all x1, starting transfers between devices, per_device(): lax.all_to_all(outgoing, 'rows', split_axis=0, concat_axis=0, tiled=True)  6.35 us
  transfers between devices with their start and end apart: 2, of which 2 were waited for; matrix products, arithmetic and copies ran while one was open for 2% of the time, Pallas kernels for 0%

commit v1 on v0

--- a/solution.py
+++ b/solution.py
@@ -4,10 +4,43 @@
 from jax.sharding import PartitionSpec as P
 
 CAP = 6
+AXES = ("grp", "rows")
 
 
 def sketch_block(block, omega):
     return jnp.dot(block, omega, preferred_element_type=jnp.float32).astype(jnp.bfloat16)
+
+
+def pack_sym(g):
+    h = g.shape[0] // 2
+    i = lax.broadcasted_iota(jnp.int32, (h, h), 0)
+    j = lax.broadcasted_iota(jnp.int32, (h, h), 1)
+    a, b, c = g[:h, :h], g[h:, :h], g[h:, h:]
+    m = jnp.where(i >= j, a, c)
+    diag_c = jnp.sum(jnp.where(i == j, c, 0.0), axis=0, keepdims=True)
+    return jnp.concatenate([b, m, diag_c], axis=0)
+
+
+def unpack_sym(p):
+    h = p.shape[1]
+    b, m, diag_c = p[:h], p[h : 2 * h], p[2 * h :]
+    i = lax.broadcasted_iota(jnp.int32, (h, h), 0)
+    j = lax.broadcasted_iota(jnp.int32, (h, h), 1)
+    mt = m.T
+    a = jnp.where(i >= j, m, mt)
+    c = jnp.where(i < j, m, jnp.where(i > j, mt, diag_c))
+    return jnp.concatenate(
+        [jnp.concatenate([a, b.T], axis=1), jnp.concatenate([b, c], axis=1)], axis=0
+    )
+
+
+def all_sum(x, n):
+    if n & (n - 1):
+        return lax.psum(x, AXES)
+    bits = n.bit_length() - 1
+    for b in reversed(range(bits)):
+        x = x + lax.ppermute(x, AXES, [(i, i ^ (1 << b)) for i in range(n)])
+    return x
 
 
 def per_device(stationary, rotor_rows, owners, counts, omega):
@@ -24,17 +57,24 @@
     rank = jnp.sum((jnp.cumsum(onehot, axis=0) - onehot) * onehot, axis=1)
     slot = jnp.where(live, targets * CAP + rank, -1)
     select = (lax.iota(jnp.int32, n_rows * CAP)[:, None] == slot[None, :]).astype(jnp.bfloat16)
+
     sketch_stat = sketch_block(stationary, omega)
-    outgoing = jnp.dot(select, rotor_rows, preferred_element_type=jnp.float32).astype(jnp.bfloat16)
+    sketch_rot = sketch_block(rotor_rows, omega)
+    rot_live = jnp.where(live[:, None], sketch_rot, jnp.zeros_like(sketch_rot))
+
+    dims = (((0,), (0,)), ((), ()))
+    gram = lax.dot_general(sketch_stat, sketch_stat, dims, preferred_element_type=jnp.float32)
+    gram = gram + lax.dot_general(rot_live, rot_live, dims, preferred_element_type=jnp.float32)
+    gram = gram / total
+
+    outgoing = jnp.dot(select, sketch_rot, preferred_element_type=jnp.float32).astype(jnp.bfloat16)
     outgoing = outgoing.reshape(n_rows, CAP, -1)
-    arrived_rows = lax.all_to_all(outgoing, "rows", split_axis=0, concat_axis=0, tiled=True)
-    arrived = sketch_block(arrived_rows.reshape(n_rows * CAP, -1), omega)
+    arrived = lax.all_to_all(outgoing, "rows", split_axis=0, concat_axis=0, tiled=True)
+    arrived = arrived.reshape(n_rows * CAP, -1)
+
+    gram = unpack_sym(all_sum(pack_sym(gram), n_grp * n_rows))
+    lower = jnp.linalg.cholesky(gram)
     local = jnp.concatenate([sketch_stat, arrived], axis=0)
-    gram = (
-        lax.dot_general(local, local, (((0,), (0,)), ((), ())), preferred_element_type=jnp.float32)
-        / total
-    )
-    lower = jnp.linalg.cholesky(lax.psum(gram, ("grp", "rows")))
     solved = lax.linalg.triangular_solve(
         lower, local.astype(jnp.float32).T, left_side=True, lower=True
     )

time: 228 us -> 103 us (0.45)
  waiting for transfers between devices: 125 us -> 12.9 us
  between operations: 16.3 us -> 3.01 us
  starting transfers between devices: 6.39 us -> 12.5 us
  matrix products: 13.7 us -> 10.9 us
  other arithmetic: 56 us -> 53.6 us
    psum x1 -> x0, waiting for transfers between devices: 122 us -> none  [per_device(): lower = jnp.linalg.cholesky(lax.psum(gram, ('grp', 'rows')))]
    ppermute x0 -> x5, waiting for transfers between devices: none -> 12.9 us  [all_sum(): x = x + lax.ppermute(x, AXES, [(i, i ^ 1 << b) for i in range(n)])]
    ppermute x0 -> x5, starting transfers between devices: none -> 7.59 us  [all_sum(): x = x + lax.ppermute(x, AXES, [(i, i ^ 1 << b) for i in range(n)])]
    all_to_all x1, waiting for transfers between devices: 2.88 us -> 0.01 us  [per_device(): lax.all_to_all(outgoing, 'rows', split_axis=0, concat_axis=0, tiled=True)]
    dot_general x2 -> x3, matrix products: 3.54 us -> 0.84 us  [the longest x1 0.43 us: per_device(): lax.dot_general(sketch_stat, sketch_stat, dims, preferred_element_type=jn...]
    unnamed x8 -> x10, local copies, waits for them, and re-layouts: 3.68 us -> 4.65 us
  transfers between devices with their start and end apart: 2 -> 6, of which waited for: 2 -> 3; matrix products, arithmetic and copies ran while one was open for 2% -> 4% of each run, Pallas kernels for 0% -> 0%
where the time goes in v1:
time: 103 us
  other arithmetic  53.6 us (52%)
  waiting for transfers between devices  12.9 us (13%)
  starting transfers between devices  12.5 us (12%)
  matrix products  10.9 us (11%)
  local copies, waits for them, and re-layouts  9.68 us (9%)
  between operations  3.01 us (3%)
    another operation x7, other arithmetic, per_device(): lower = jnp.linalg.cholesky(gram)  28.7 us
    another operation x5, other arithmetic, per_device(): lax.linalg.triangular_solve(lower, local.astype(jnp.float32).T, left_side...  20.4 us
    ppermute x5, waiting for transfers between devices, all_sum(): x = x + lax.ppermute(x, AXES, [(i, i ^ 1 << b) for i in range(n)])  12.9 us
    ppermute x5, starting transfers between devices, all_sum(): x = x + lax.ppermute(x, AXES, [(i, i ^ 1 << b) for i in range(n)])  7.59 us
    another operation x3, matrix products, per_device(): lax.linalg.triangular_solve(lower, local.astype(jnp.float32).T, left_side...  6.65 us
    all_to_all x1, starting transfers between devices, per_device(): lax.all_to_all(outgoing, 'rows', split_axis=0, concat_axis=0, tiled=True)  4.87 us
    unnamed x10, local copies, waits for them, and re-layouts  4.65 us
    dot_general x2, matrix products, sketch_block(): jnp.dot(block, omega, preferred_element_type=jnp.float32)  3.02 us
  transfers between devices with their start and end apart: 6, of which 3 were waited for; matrix products, arithmetic and copies ran while one was open for 4% of the time, Pallas kernels for 0%

profile of v1, /device:TPU:0, one launch (start us, length us, event | category | flops | bytes accessed | tf_op | source)
XLA Modules:
  0.0 102.5 jit_solution(2980507620838060273)
XLA Ops:
  1.5 1.1 %convolution_convert_fusion.3 = bf16[32,192]{1,0:T(8,128)(2,1)S(1)} fusion(bf16[32,512]{1,0:T(8,128)(2,1)} %param.6, bf16[512,192]{0,1:T(8,128)(2,1)} %param.9), kind=kOutput, calls=%fused_computation.8 | convolution fusion | flops 6297600 | bytes 241664 | tf_op jit(solution)/shard_map/dot_general | solution.py:11
  2.6 1.9 %convolution_convert_fusion = bf16[2560,192]{0,1:T(8,128)(2,1)S(1)} fusion(bf16[2560,512]{1,0:T(8,128)(2,1)S(1)} %copy-done, bf16[512,192]{0,1:T(8,128)(2,1)} %param.9), kind=kOutput, calls=%fused_computation | convolution fusion | flops 503808000 | bytes 3801088 | tf_op jit(solution)/shard_map/dot_general | solution.py:11
  4.5 0.9 copy-done.1
  5.5 0.4 fusion.22
  5.9 0.3 fusion
  6.3 3.1 %collective-permute-start = (f32[193,96]{1,0:T(8,128)S(1)}, f32[193,96]{1,0:T(8,128)S(1)}, u32[]{:S(2)}, u32[]{:S(2)}) collective-permute-start(f32[193,96]{1,0:T(8,128)S(1)} %pad_maximum_fusion.1), channel_id=1, source_target_pairs={{0,16},{1,17},{2,18},{3,19},{4,20},{5,21},{6,22},{7,23},{8,24},{9,... | collective-permute-start | bytes 222344 | tf_op jit(solution)/shard_map/ppermute | solution.py:42
  9.5 0.2 select_reduce_fusion.3
  9.8 0.6 reshape.49
  10.5 4.9 %all-to-all-start = ((bf16[8,6,192]{2,1,0:T(8,128)(2,1)}), bf16[8,6,192]{2,1,0:T(8,128)(2,1)S(1)}, u32[]{:S(2)}, u32[]{:S(2)}) async-start(bf16[8,6,192]{2,1,0:T(8,128)(2,1)} %reshape.49), calls=%async_computation | async-start | bytes 65536 | tf_op jit(solution)/shard_map/all_to_all | solution.py:72
  15.4 1.6 %collective-permute-start.1 = (f32[193,96]{1,0:T(8,128)S(1)}, f32[193,96]{1,0:T(8,128)S(1)}, u32[]{:S(2)}, u32[]{:S(2)}) collective-permute-start(f32[193,96]{1,0:T(8,128)S(1)} %fusion.19), channel_id=1, source_target_pairs={{0,8},{1,9},{2,10},{3,11},{4,12},{5,13},{6,14},{7,15},{8,0},{9,1},... | collective-permute-start | bytes 222344 | tf_op jit(solution)/shard_map/ppermute | solution.py:42
  16.9 3.8 %collective-permute-done.1 = f32[193,96]{1,0:T(8,128)S(1)} collective-permute-done((f32[193,96]{1,0:T(8,128)S(1)}, f32[193,96]{1,0:T(8,128)S(1)}, u32[]{:S(2)}, u32[]{:S(2)}) %collective-permute-start.1) | collective-permute-done | bytes 74144 | tf_op jit(solution)/shard_map/ppermute | solution.py:42
  20.7 2.6 %collective-permute-start.2 = (f32[193,96]{1,0:T(8,128)S(1)}, f32[193,96]{1,0:T(8,128)S(1)}, u32[]{:S(2)}, u32[]{:S(2)}) collective-permute-start(f32[193,96]{1,0:T(8,128)S(1)} %add.51), channel_id=1, source_target_pairs={{0,4},{1,5},{2,6},{3,7},{4,0},{5,1},{6,2},{7,3},{8,12},{9,13},{10,... | collective-permute-start | bytes 222344 | tf_op jit(solution)/shard_map/ppermute | solution.py:42
  23.3 5.0 %collective-permute-done.2 = f32[193,96]{1,0:T(8,128)S(1)} collective-permute-done((f32[193,96]{1,0:T(8,128)S(1)}, f32[193,96]{1,0:T(8,128)S(1)}, u32[]{:S(2)}, u32[]{:S(2)}) %collective-permute-start.2) | collective-permute-done | bytes 74144 | tf_op jit(solution)/shard_map/ppermute | solution.py:42
  28.3 0.3 collective-permute-start.3
  28.9 4.1 %collective-permute-done.3 = f32[193,96]{1,0:T(8,128)S(1)} collective-permute-done((f32[193,96]{1,0:T(8,128)S(1)}, f32[193,96]{1,0:T(8,128)S(1)}, u32[]{:S(2)}, u32[]{:S(2)}) %collective-permute-start.3) | collective-permute-done | bytes 74144 | tf_op jit(solution)/shard_map/ppermute | solution.py:42
  33.2 2.3 %maximum_bitcast_fusion.1 = bf16[192,2608]{1,0:T(8,128)(2,1)} fusion(bf16[48,192]{0,1:T(8,128)(2,1)S(1)} %copy.37, bf16[2560,192]{0,1:T(8,128)(2,1)} %copy-done.1), kind=kLoop, calls=%fused_computation.9 | loop fusion | flops 2002944 | bytes 2002944 | tf_op jit(solution)/shard_map/transpose | solution.py:79
  36.1 11.7 %cholesky.51 = f32[128,128]{1,0:T(8,128)S(1)} custom-call(f32[128,128]{1,0:T(8,128)S(1)} %cholesky.124), custom_call_target="Cholesky" | custom-call | tf_op jit(solution)/shard_map/jit(cholesky)/cholesky | solution.py:76
  47.9 0.6 compare_reduce_fusion.1
  48.5 9.8 %custom-call.14 = f32[1,128,128]{1,2,0:T(8,128)S(1)} custom-call(f32[1,128,128]{2,1,0:T(8,128)S(1)} %get-tuple-element.43), custom_call_target="InvertDiagBlocksLowerTriangular" | custom-call | tf_op jit(solution)/shard_map/jit(cholesky)/cholesky | solution.py:76
  58.7 5.8 %cholesky.110 = f32[64,64]{1,0:T(8,128)S(1)} custom-call(f32[64,64]{1,0:T(8,128)S(1)} %convolution_subtract_fusion.1), custom_call_target="Cholesky" | custom-call | tf_op jit(solution)/shard_map/jit(cholesky)/cholesky | solution.py:76
  64.6 0.6 compare_reduce_fusion
  66.7 0.5 copy-done.2
  67.3 20.3 %custom-call.15 = f32[2,128,128]{1,2,0:T(8,128)} custom-call(f32[2,128,128]{2,1,0:T(8,128)S(1)} %pad_maximum_fusion), custom_call_target="InvertDiagBlocksLowerTriangular" | custom-call | tf_op jit(solution)/shard_map/triangular_solve | solution.py:78
  87.6 2.0 %fusion.21 = (bf16[128,2608]{0,1:T(8,128)(2,1)S(1)}, f32[128,2608]{0,1:T(8,128)S(1)}) fusion(bf16[192,2608]{1,0:T(8,128)(2,1)} %maximum_bitcast_fusion.1, f32[2,128,128]{1,2,0:T(8,128)} %custom-call.15), kind=kOutput, calls=%fused_computation.68 | convolution fusion | flops 513087488 | bytes 2756608 | tf_op jit(solution)/shard_map/triangular_solve | solution.py:78
  89.5 2.4 %convolution_subtract_fusion = f32[64,2608]{1,0:T(8,128)S(1)} fusion(f32[128,2608]{0,1:T(8,128)S(1)} %get-tuple-element.49, bf16[192,2608]{1,0:T(8,128)(2,1)} %maximum_bitcast_fusion.1, f32[192,192]{1,0:T(8,128)} %copy-done.2), kind=kOutput, calls=%fused_computation.1 | convolution fusion | flops 256710656 | bytes 2379776 | tf_op jit(solution)/shard_map/triangular_solve | solution.py:78
  92.0 2.2 %convolution_convert_fusion.1 = bf16[64,2608]{1,0:T(8,128)(2,1)} fusion(f32[64,2608]{1,0:T(8,128)S(1)} %convolution_subtract_fusion, f32[2,128,128]{1,2,0:T(8,128)} %custom-call.15), kind=kOutput, calls=%fused_computation.2 | convolution fusion | flops 128355328 | bytes 1034240 | tf_op jit(solution)/shard_map/triangular_solve | solution.py:78
  94.2 2.1 %copy.38 = bf16[64,2608]{0,1:T(8,128)(2,1)} copy(bf16[64,2608]{1,0:T(8,128)(2,1)} %convolution_convert_fusion.1) | data formatting | bytes 667648 | tf_op jit(solution)/shard_map/convert.7
  96.3 1.3 %maximum_bitcast_fusion = bf16[2608,192]{1,0:T(8,128)(2,1)S(1)} fusion(bf16[64,2608]{0,1:T(8,128)(2,1)} %copy.38, bf16[128,2608]{0,1:T(8,128)(2,1)S(1)} %get-tuple-element.48), kind=kLoop, calls=%fused_computation.3 | loop fusion | flops 2002944 | bytes 2002944 | tf_op jit(solution)/shard_map/convert_element_type | solution.py:81
  97.6 0.6 slice.102
  98.3 1.1 %slice.101 = bf16[2560,192]{1,0:T(8,128)(2,1)} slice(bf16[2608,192]{1,0:T(8,128)(2,1)S(1)} %maximum_bitcast_fusion), slice={[0:2560], [0:192]} | slice | bytes 1966080 | tf_op jit(solution)/shard_map/slice | solution.py:82
  99.4 0.8 copy.40
  100.2 2.3 %copy.39 = bf16[2560,192]{0,1:T(8,128)(2,1)} copy(bf16[2560,192]{1,0:T(8,128)(2,1)} %slice.101) | data formatting | bytes 1966080
  (46 shorter events, 2.1 us)
Async XLA Ops:
  0.6 1.9 %copy-start = (bf16[2560,512]{1,0:T(8,128)(2,1)S(1)}, bf16[2560,512]{1,0:T(8,128)(2,1)}, u32[]{:S(2)}) copy-start(bf16[2560,512]{1,0:T(8,128)(2,1)} %param.5) | copy-start | bytes 7864324
  4.5 0.9 copy-start.1
  5.5 3.9 %copy-start.3 = (s32[32,1]{0,1:T(1,128)S(1)}, s32[32,1]{0,1:T(1,128)}, u32[]{:S(2)}) copy-start(s32[32,1]{0,1:T(1,128)} %param.7) | copy-start | bytes 388
  6.3 9.0 %collective-permute-start = (f32[193,96]{1,0:T(8,128)S(1)}, f32[193,96]{1,0:T(8,128)S(1)}, u32[]{:S(2)}, u32[]{:S(2)}) collective-permute-start(f32[193,96]{1,0:T(8,128)S(1)} %pad_maximum_fusion.1), channel_id=1, source_target_pairs={{0,16},{1,17},{2,18},{3,19},{4,20},{5,21},{6,22},{7,23},{8,24},{9,... | collective-permute-start | bytes 222344 | tf_op jit(solution)/shard_map/ppermute | solution.py:42
  10.5 18.3 %all-to-all-start = ((bf16[8,6,192]{2,1,0:T(8,128)(2,1)}), bf16[8,6,192]{2,1,0:T(8,128)(2,1)S(1)}, u32[]{:S(2)}, u32[]{:S(2)}) async-start(bf16[8,6,192]{2,1,0:T(8,128)(2,1)} %reshape.49), calls=%async_computation | async-start | bytes 65536 | tf_op jit(solution)/shard_map/all_to_all | solution.py:72
  15.4 5.4 %collective-permute-start.1 = (f32[193,96]{1,0:T(8,128)S(1)}, f32[193,96]{1,0:T(8,128)S(1)}, u32[]{:S(2)}, u32[]{:S(2)}) collective-permute-start(f32[193,96]{1,0:T(8,128)S(1)} %fusion.19), channel_id=1, source_target_pairs={{0,8},{1,9},{2,10},{3,11},{4,12},{5,13},{6,14},{7,15},{8,0},{9,1},... | collective-permute-start | bytes 222344 | tf_op jit(solution)/shard_map/ppermute | solution.py:42
  20.7 7.6 %collective-permute-start.2 = (f32[193,96]{1,0:T(8,128)S(1)}, f32[193,96]{1,0:T(8,128)S(1)}, u32[]{:S(2)}, u32[]{:S(2)}) collective-permute-start(f32[193,96]{1,0:T(8,128)S(1)} %add.51), channel_id=1, source_target_pairs={{0,4},{1,5},{2,6},{3,7},{4,0},{5,1},{6,2},{7,3},{8,12},{9,13},{10,... | collective-permute-start | bytes 222344 | tf_op jit(solution)/shard_map/ppermute | solution.py:42
  28.3 4.7 %collective-permute-start.3 = (f32[193,96]{1,0:T(8,128)S(1)}, f32[193,96]{1,0:T(8,128)S(1)}, u32[]{:S(2)}, u32[]{:S(2)}) collective-permute-start(f32[193,96]{1,0:T(8,128)S(1)} %add.52), channel_id=1, source_target_pairs={{0,2},{1,3},{2,0},{3,1},{4,6},{5,7},{6,4},{7,5},{8,10},{9,11},{10,... | collective-permute-start | bytes 222344 | tf_op jit(solution)/shard_map/ppermute | solution.py:42
  33.1 2.3 %collective-permute-start.4 = (f32[193,96]{1,0:T(8,128)S(1)}, f32[193,96]{1,0:T(8,128)S(1)}, u32[]{:S(2)}, u32[]{:S(2)}) collective-permute-start(f32[193,96]{1,0:T(8,128)S(1)} %add.53), channel_id=1, source_target_pairs={{0,1},{1,0},{2,3},{3,2},{4,5},{5,4},{6,7},{7,6},{8,9},{9,8},{10,11... | collective-permute-start | bytes 222344 | tf_op jit(solution)/shard_map/ppermute | solution.py:42
  66.6 0.7 copy-start.2

commit v2 on v1

--- a/solution.py
+++ b/solution.py
@@ -5,6 +5,7 @@
 
 CAP = 6
 AXES = ("grp", "rows")
+HIGHEST = lax.Precision.HIGHEST
 
 
 def sketch_block(block, omega):
@@ -43,6 +44,24 @@
     return x
 
 
+def cholesky_and_inverse(g):
+    k = g.shape[0]
+    h = k // 2
+    a11, a21, a22 = g[:h, :h], g[h:, :h], g[h:, h:]
+    eye = jnp.eye(h, dtype=jnp.float32)
+    l11 = lax.linalg.cholesky(a11, symmetrize_input=False)
+    i11 = lax.linalg.triangular_solve(l11, eye, left_side=True, lower=True)
+    l21 = jnp.dot(a21, i11.T, precision=HIGHEST)
+    s = a22 - jnp.dot(l21, l21.T, precision=HIGHEST)
+    l22 = lax.linalg.cholesky(s, symmetrize_input=False)
+    i22 = lax.linalg.triangular_solve(l22, eye, left_side=True, lower=True)
+    i21 = -jnp.dot(i22, jnp.dot(l21, i11, precision=HIGHEST), precision=HIGHEST)
+    z = jnp.zeros((h, h), jnp.float32)
+    lower = jnp.block([[l11, z], [l21, l22]])
+    inverse = jnp.block([[i11, z], [i21, i22]])
+    return lower, inverse
+
+
 def per_device(stationary, rotor_rows, owners, counts, omega):
     n_rows = lax.axis_size("rows")
     n_grp = lax.axis_size("grp")
@@ -73,13 +92,14 @@
     arrived = arrived.reshape(n_rows * CAP, -1)
 
     gram = unpack_sym(all_sum(pack_sym(gram), n_grp * n_rows))
-    lower = jnp.linalg.cholesky(gram)
-    local = jnp.concatenate([sketch_stat, arrived], axis=0)
-    solved = lax.linalg.triangular_solve(
-        lower, local.astype(jnp.float32).T, left_side=True, lower=True
+    lower, inverse = cholesky_and_inverse(gram)
+    basis_stat = jnp.dot(
+        sketch_stat.astype(jnp.float32), inverse.T, precision=HIGHEST
+    ).astype(jnp.bfloat16)
+    basis_rot = jnp.dot(arrived.astype(jnp.float32), inverse.T, precision=HIGHEST).astype(
+        jnp.bfloat16
     )
-    basis = solved.T.astype(jnp.bfloat16)
-    return (basis[:stat_dev], basis[stat_dev:], lower.T)
+    return (basis_stat, basis_rot, lower.T)
 
 
 def solution(mesh):

time: 103 us -> 82.2 us (0.80)
  other arithmetic: 53.6 us -> 35.5 us
  blocking collectives: 0 us -> 11.8 us
  local copies, waits for them, and re-layouts: 9.68 us -> 3.76 us
  starting transfers between devices: 12.5 us -> 9.95 us
  matrix products: 10.9 us -> 8.43 us
  waiting for transfers between devices: 12.9 us -> 10.9 us
  between operations: 3.01 us -> 1.58 us
    another operation x12 -> x10, other arithmetic: 49.1 us -> 34.9 us  [the longest x3 9.45 us: cholesky_and_inverse(): l22 = lax.linalg.cholesky(s, symmetrize_input=False)]
    all_to_all x0 -> x1, blocking collectives: none -> 11.8 us  [per_device(): lax.all_to_all(outgoing, 'rows', split_axis=0, concat_axis=0, tiled=True)]
    another operation x5 -> x2, matrix products: 7.01 us -> 0.51 us  [the longest x1 0.26 us: cholesky_and_inverse(): i11 = lax.linalg.triangular_solve(l11, eye, left_side=True, lower=True)]
    dot_general x0 -> x6, matrix products: none -> 5.01 us  [the longest x1 3.1 us: per_device(): jnp.dot(sketch_stat.astype(jnp.float32), inverse.T, precision=HIGHEST)]
    all_to_all x1 -> x0, starting transfers between devices: 4.87 us -> none  [per_device(): lax.all_to_all(outgoing, 'rows', split_axis=0, concat_axis=0, tiled=True)]
    ppermute x5, starting transfers between devices: 7.59 us -> 9.95 us  [all_sum(): x = x + lax.ppermute(x, AXES, [(i, i ^ 1 << b) for i in range(n)])]
    transpose x2 -> x1, other arithmetic: 2.29 us -> 0.09 us  [per_device(): return (basis_stat, basis_rot, lower.T)]
    ppermute x5, waiting for transfers between devices: 12.9 us -> 10.9 us  [all_sum(): x = x + lax.ppermute(x, AXES, [(i, i ^ 1 << b) for i in range(n)])]
  transfers between devices with their start and end apart: 6 -> 5, of which waited for: 3 -> 4; matrix products, arithmetic and copies ran while one was open for 4% -> 1% of each run, Pallas kernels for 0% -> 0%
where the time goes in v2:
time: 82.2 us; the launch traced here: 81.9 us
  other arithmetic  35.5 us (43%)
  blocking collectives  11.8 us (14%)
  waiting for transfers between devices  10.9 us (13%)
  starting transfers between devices  9.95 us (12%)
  matrix products  8.43 us (10%)
  local copies, waits for them, and re-layouts  3.76 us (5%)
  between operations  1.58 us (2%)
    all_to_all x1, blocking collectives, per_device(): lax.all_to_all(outgoing, 'rows', split_axis=0, concat_axis=0, tiled=True)  11.8 us
    ppermute x5, waiting for transfers between devices, all_sum(): x = x + lax.ppermute(x, AXES, [(i, i ^ 1 << b) for i in range(n)])  10.9 us
    ppermute x5, starting transfers between devices, all_sum(): x = x + lax.ppermute(x, AXES, [(i, i ^ 1 << b) for i in range(n)])  9.95 us
    another operation x3, other arithmetic, cholesky_and_inverse(): l22 = lax.linalg.cholesky(s, symmetrize_input=False)  9.45 us
    another operation x3, other arithmetic, cholesky_and_inverse(): l11 = lax.linalg.cholesky(a11, symmetrize_input=False)  9.45 us
    another operation x2, other arithmetic, cholesky_and_inverse(): i11 = lax.linalg.triangular_solve(l11, eye, left_side=True, lower=True)  8.01 us
    another operation x2, other arithmetic, cholesky_and_inverse(): i22 = lax.linalg.triangular_solve(l22, eye, left_side=True, lower=True)  8.01 us
    unnamed x11, local copies, waits for them, and re-layouts  3.47 us
  transfers between devices with their start and end apart: 5, of which 4 were waited for; matrix products, arithmetic and copies ran while one was open for 1% of the time, Pallas kernels for 0%

profile of v2, /device:TPU:0, one launch (start us, length us, event | category | flops | bytes accessed | tf_op | source)
XLA Modules:
  0.0 81.9 jit_solution(12670827334580957721)
XLA Ops:
  0.7 1.7 %copy-done = bf16[2560,512]{1,0:T(8,128)(2,1)S(1)} copy-done((bf16[2560,512]{1,0:T(8,128)(2,1)S(1)}, bf16[2560,512]{1,0:T(8,128)(2,1)}, u32[]{:S(2)}) %copy-start) | copy-done | bytes 2621464
  2.4 1.9 %convolution_convert_fusion.1 = bf16[2560,192]{0,1:T(8,128)(2,1)S(1)} fusion(bf16[2560,512]{1,0:T(8,128)(2,1)S(1)} %copy-done, bf16[512,192]{0,1:T(8,128)(2,1)} %param.12), kind=kOutput, calls=%fused_computation.1 | convolution fusion | flops 503808000 | bytes 3801088 | tf_op jit(solution)/shard_map/dot_general | solution.py:12
  4.3 0.9 %copy-done.1 = bf16[2560,192]{0,1:T(8,128)(2,1)} copy-done((bf16[2560,192]{0,1:T(8,128)(2,1)}, bf16[2560,192]{0,1:T(8,128)(2,1)S(1)}, u32[]{:S(2)}) %copy-start.1) | copy-done | bytes 983064
  5.3 0.4 fusion.35
  6.6 0.3 fusion
  7.0 3.1 %collective-permute-start = (f32[193,96]{1,0:T(8,128)S(1)}, f32[193,96]{1,0:T(8,128)S(1)}, u32[]{:S(2)}, u32[]{:S(2)}) collective-permute-start(f32[193,96]{1,0:T(8,128)S(1)} %pad_maximum_fusion), channel_id=1, source_target_pairs={{0,16},{1,17},{2,18},{3,19},{4,20},{5,21},{6,22},{7,23},{8,24},{9,... | collective-permute-start | bytes 222344 | tf_op jit(solution)/shard_map/ppermute | solution.py:43
  10.0 2.9 %collective-permute-done = f32[193,96]{1,0:T(8,128)S(1)} collective-permute-done((f32[193,96]{1,0:T(8,128)S(1)}, f32[193,96]{1,0:T(8,128)S(1)}, u32[]{:S(2)}, u32[]{:S(2)}) %collective-permute-start) | collective-permute-done | bytes 74144 | tf_op jit(solution)/shard_map/ppermute | solution.py:43
  12.9 1.8 %collective-permute-start.1 = (f32[193,96]{1,0:T(8,128)S(1)}, f32[193,96]{1,0:T(8,128)S(1)}, u32[]{:S(2)}, u32[]{:S(2)}) collective-permute-start(f32[193,96]{1,0:T(8,128)S(1)} %fusion.32), channel_id=1, source_target_pairs={{0,8},{1,9},{2,10},{3,11},{4,12},{5,13},{6,14},{7,15},{8,0},{9,1},... | collective-permute-start | bytes 222344 | tf_op jit(solution)/shard_map/ppermute | solution.py:43
  14.9 2.8 %collective-permute-done.1 = f32[193,96]{1,0:T(8,128)S(1)} collective-permute-done((f32[193,96]{1,0:T(8,128)S(1)}, f32[193,96]{1,0:T(8,128)S(1)}, u32[]{:S(2)}, u32[]{:S(2)}) %collective-permute-start.1) | collective-permute-done | bytes 74144 | tf_op jit(solution)/shard_map/ppermute | solution.py:43
  17.7 2.9 %collective-permute-start.2 = (f32[193,96]{1,0:T(8,128)S(1)}, f32[193,96]{1,0:T(8,128)S(1)}, u32[]{:S(2)}, u32[]{:S(2)}) collective-permute-start(f32[193,96]{1,0:T(8,128)S(1)} %add.35), channel_id=1, source_target_pairs={{0,4},{1,5},{2,6},{3,7},{4,0},{5,1},{6,2},{7,3},{8,12},{9,13},{10,... | collective-permute-start | bytes 222344 | tf_op jit(solution)/shard_map/ppermute | solution.py:43
  20.6 0.2 select_reduce_fusion.2
  20.8 2.6 %collective-permute-done.2 = f32[193,96]{1,0:T(8,128)S(1)} collective-permute-done((f32[193,96]{1,0:T(8,128)S(1)}, f32[193,96]{1,0:T(8,128)S(1)}, u32[]{:S(2)}, u32[]{:S(2)}) %collective-permute-start.2) | collective-permute-done | bytes 74144 | tf_op jit(solution)/shard_map/ppermute | solution.py:43
  23.4 2.1 %collective-permute-start.3 = (f32[193,96]{1,0:T(8,128)S(1)}, f32[193,96]{1,0:T(8,128)S(1)}, u32[]{:S(2)}, u32[]{:S(2)}) collective-permute-start(f32[193,96]{1,0:T(8,128)S(1)} %add.36), channel_id=1, source_target_pairs={{0,2},{1,3},{2,0},{3,1},{4,6},{5,7},{6,4},{7,5},{8,10},{9,11},{10,... | collective-permute-start | bytes 222344 | tf_op jit(solution)/shard_map/ppermute | solution.py:43
  25.5 2.6 %collective-permute-done.3 = f32[193,96]{1,0:T(8,128)S(1)} collective-permute-done((f32[193,96]{1,0:T(8,128)S(1)}, f32[193,96]{1,0:T(8,128)S(1)}, u32[]{:S(2)}, u32[]{:S(2)}) %collective-permute-start.3) | collective-permute-done | bytes 74144 | tf_op jit(solution)/shard_map/ppermute | solution.py:43
  28.3 11.8 %all_to_all.5 = bf16[8,6,192]{2,1,0:T(8,128)(2,1)S(1)} all-to-all(bf16[8,6,192]{2,1,0:T(8,128)(2,1)S(1)} %reshape.39), channel_id=1, replica_groups=mesh['grp'=4,'rows'=8] {'rows'}, dimensions={0} | all-to-all | bytes 36864 | tf_op jit(solution)/shard_map/all_to_all | solution.py:91
  40.3 8.8 %custom-call.8 = f32[96,96]{1,0:T(8,128)S(1)} custom-call(f32[96,96]{1,0:T(8,128)S(1)} %bitcast_select_fusion.1), custom_call_target="Cholesky" | custom-call | tf_op jit(solution)/shard_map/cholesky/custom-call.1 | solution.py:52
  49.2 0.6 compare_reduce_fusion.1
  49.8 0.7 select_bitcast_fusion.1
  50.5 7.4 %custom-call.9 = f32[1,96,96]{1,2,0:T(8,128)S(1)} custom-call(f32[1,96,96]{2,1,0:T(8,128)S(1)} %get-tuple-element.13), custom_call_target="InvertDiagBlocksLowerTriangular" | custom-call | tf_op jit(solution)/shard_map/triangular_solve/custom-call.0 | solution.py:53
  57.8 0.3 fusion.8
  58.1 0.2 fusion.10
  58.3 0.3 fusion.36
  58.7 0.3 fusion.15
  59.0 8.8 %custom-call.10 = f32[96,96]{1,0:T(8,128)S(1)} custom-call(f32[96,96]{1,0:T(8,128)S(1)} %fusion.15), custom_call_target="Cholesky" | custom-call | tf_op jit(solution)/shard_map/cholesky/custom-call.1 | solution.py:56
  67.8 0.6 compare_reduce_fusion
  68.4 0.7 select_bitcast_fusion
  69.1 7.4 %custom-call.11 = f32[1,96,96]{1,2,0:T(8,128)S(1)} custom-call(f32[1,96,96]{2,1,0:T(8,128)S(1)} %get-tuple-element.11), custom_call_target="InvertDiagBlocksLowerTriangular" | custom-call | tf_op jit(solution)/shard_map/triangular_solve/custom-call.0 | solution.py:57
  76.4 0.2 fusion.6
  76.8 0.3 convolution_negate_fusion
  77.0 3.1 %convolution_convert_fusion = bf16[2560,192]{0,1:T(8,128)(2,1)} fusion(bf16[2560,192]{0,1:T(8,128)(2,1)} %copy-done.1, f32[96,96]{1,0:T(8,128)S(1)} %fusion.8, f32[96,96]{1,0:T(8,128)S(1)} %copy.19, f32[96,96]{1,0:T(8,128)S(1)} %convolution_negate_fusion), kind=kOutput, calls=%fused_computation | convolution fusion | flops 1133101056 | bytes 2076672 | tf_op jit(solution)/shard_map/dot_general | solution.py:96
  80.1 0.9 %convolution_convert_fusion.2 = bf16[48,192]{1,0:T(8,128)(2,1)} fusion(bf16[48,192]{1,0:T(8,128)(2,1)S(1)} %reshape.40, f32[96,96]{1,0:T(8,128)S(1)} %fusion.8, f32[96,96]{1,0:T(8,128)S(1)} %copy.19, f32[96,96]{1,0:T(8,128)S(1)} %convolution_negate_fusion), kind=kOutput, calls=%fused_computation.5 | convolution fusion | flops 21390336 | bytes 147456 | tf_op jit(solution)/shard_map/dot_general | solution.py:99
  81.1 0.8 copy.21
  (34 shorter events, 1.1 us)
Async XLA Ops:
  0.6 1.7 %copy-start = (bf16[2560,512]{1,0:T(8,128)(2,1)S(1)}, bf16[2560,512]{1,0:T(8,128)(2,1)}, u32[]{:S(2)}) copy-start(bf16[2560,512]{1,0:T(8,128)(2,1)} %param.8) | copy-start | bytes 7864324
  0.6 5.1 %copy-start.2 = (bf16[512,192]{0,1:T(8,128)(2,1)S(1)}, bf16[512,192]{0,1:T(8,128)(2,1)}, u32[]{:S(2)}) copy-start(bf16[512,192]{0,1:T(8,128)(2,1)} %param.12) | copy-start | bytes 589828
  0.7 5.1 %copy-start.3 = (bf16[32,512]{1,0:T(8,128)(2,1)S(1)}, bf16[32,512]{1,0:T(8,128)(2,1)}, u32[]{:S(2)}) copy-start(bf16[32,512]{1,0:T(8,128)(2,1)} %param.9) | copy-start | bytes 98308
  4.3 1.0 %copy-start.1 = (bf16[2560,192]{0,1:T(8,128)(2,1)}, bf16[2560,192]{0,1:T(8,128)(2,1)S(1)}, u32[]{:S(2)}) copy-start(bf16[2560,192]{0,1:T(8,128)(2,1)S(1)} %convolution_convert_fusion.1) | copy-start | bytes 2949124
  5.3 9.5 %copy-start.4 = (s32[32,1]{0,1:T(1,128)S(1)}, s32[32,1]{0,1:T(1,128)}, u32[]{:S(2)}) copy-start(s32[32,1]{0,1:T(1,128)} %param.10) | copy-start | bytes 388
  7.0 5.9 %collective-permute-start = (f32[193,96]{1,0:T(8,128)S(1)}, f32[193,96]{1,0:T(8,128)S(1)}, u32[]{:S(2)}, u32[]{:S(2)}) collective-permute-start(f32[193,96]{1,0:T(8,128)S(1)} %pad_maximum_fusion), channel_id=1, source_target_pairs={{0,16},{1,17},{2,18},{3,19},{4,20},{5,21},{6,22},{7,23},{8,24},{9,... | collective-permute-start | bytes 222344 | tf_op jit(solution)/shard_map/ppermute | solution.py:43
  12.9 4.7 %collective-permute-start.1 = (f32[193,96]{1,0:T(8,128)S(1)}, f32[193,96]{1,0:T(8,128)S(1)}, u32[]{:S(2)}, u32[]{:S(2)}) collective-permute-start(f32[193,96]{1,0:T(8,128)S(1)} %fusion.32), channel_id=1, source_target_pairs={{0,8},{1,9},{2,10},{3,11},{4,12},{5,13},{6,14},{7,15},{8,0},{9,1},... | collective-permute-start | bytes 222344 | tf_op jit(solution)/shard_map/ppermute | solution.py:43
  17.7 5.7 %collective-permute-start.2 = (f32[193,96]{1,0:T(8,128)S(1)}, f32[193,96]{1,0:T(8,128)S(1)}, u32[]{:S(2)}, u32[]{:S(2)}) collective-permute-start(f32[193,96]{1,0:T(8,128)S(1)} %add.35), channel_id=1, source_target_pairs={{0,4},{1,5},{2,6},{3,7},{4,0},{5,1},{6,2},{7,3},{8,12},{9,13},{10,... | collective-permute-start | bytes 222344 | tf_op jit(solution)/shard_map/ppermute | solution.py:43
  23.4 4.7 %collective-permute-start.3 = (f32[193,96]{1,0:T(8,128)S(1)}, f32[193,96]{1,0:T(8,128)S(1)}, u32[]{:S(2)}, u32[]{:S(2)}) collective-permute-start(f32[193,96]{1,0:T(8,128)S(1)} %add.36), channel_id=1, source_target_pairs={{0,2},{1,3},{2,0},{3,1},{4,6},{5,7},{6,4},{7,5},{8,10},{9,11},{10,... | collective-permute-start | bytes 222344 | tf_op jit(solution)/shard_map/ppermute | solution.py:43
  28.1 12.1 %collective-permute-start.4 = (f32[193,96]{1,0:T(8,128)S(1)}, f32[193,96]{1,0:T(8,128)S(1)}, u32[]{:S(2)}, u32[]{:S(2)}) collective-permute-start(f32[193,96]{1,0:T(8,128)S(1)} %add.37), channel_id=1, source_target_pairs={{0,1},{1,0},{2,3},{3,2},{4,5},{5,4},{6,7},{7,6},{8,9},{9,8},{10,11... | collective-permute-start | bytes 222344 | tf_op jit(solution)/shard_map/ppermute | solution.py:43

commit v3 on v2

--- a/solution.py
+++ b/solution.py
@@ -35,13 +35,28 @@
     )
 
 
-def all_sum(x, n):
-    if n & (n - 1):
-        return lax.psum(x, AXES)
+def all_sum_and_route(x, held, n, n_rows):
     bits = n.bit_length() - 1
+    row_bits = n_rows.bit_length() - 1
+    me = lax.axis_index(AXES)
+    width = x.shape[1]
     for b in reversed(range(bits)):
-        x = x + lax.ppermute(x, AXES, [(i, i ^ (1 << b)) for i in range(n)])
-    return x
+        perm = [(i, i ^ (1 << b)) for i in range(n)]
+        if b >= row_bits:
+            x = x + lax.ppermute(x, AXES, perm)
+            continue
+        parts = held.reshape((n_rows >> (b + 1), 2, 1 << b) + held.shape[1:])
+        mine = (me >> b) & 1
+        keep = jnp.where(mine == 0, parts[:, 0], parts[:, 1])
+        away = jnp.where(mine == 0, parts[:, 1], parts[:, 0])
+        packet = jnp.concatenate([x, away.astype(jnp.float32).reshape(-1, width)], axis=0)
+        got = lax.ppermute(packet, AXES, perm)
+        x = x + got[: x.shape[0]]
+        came = got[x.shape[0] :].reshape(away.shape).astype(held.dtype)
+        lo = jnp.where(mine == 0, keep, came)
+        hi = jnp.where(mine == 0, came, keep)
+        held = jnp.stack([lo, hi], axis=1).reshape(held.shape)
+    return x, held
 
 
 def cholesky_and_inverse(g):
@@ -68,6 +83,7 @@
     rot_dev = rotor_rows.shape[0]
     stat_dev = stationary.shape[0]
     total = n_grp * n_rows * (stat_dev + rot_dev)
+    k = omega.shape[1]
     targets = owners[:, 0]
     live = lax.iota(jnp.int32, rot_dev) < counts[0]
     onehot = ((targets[:, None] == lax.iota(jnp.int32, n_rows)[None, :]) & live[:, None]).astype(
@@ -88,10 +104,15 @@
 
     outgoing = jnp.dot(select, sketch_rot, preferred_element_type=jnp.float32).astype(jnp.bfloat16)
     outgoing = outgoing.reshape(n_rows, CAP, -1)
-    arrived = lax.all_to_all(outgoing, "rows", split_axis=0, concat_axis=0, tiled=True)
+    packed = pack_sym(gram)
+    n = n_grp * n_rows
+    if n & (n - 1) or n_rows & (n_rows - 1) or (CAP * k) % packed.shape[1]:
+        arrived = lax.all_to_all(outgoing, "rows", split_axis=0, concat_axis=0, tiled=True)
+        packed = lax.psum(packed, AXES)
+    else:
+        packed, arrived = all_sum_and_route(packed, outgoing, n, n_rows)
     arrived = arrived.reshape(n_rows * CAP, -1)
-
-    gram = unpack_sym(all_sum(pack_sym(gram), n_grp * n_rows))
+    gram = unpack_sym(packed)
     lower, inverse = cholesky_and_inverse(gram)
     basis_stat = jnp.dot(
         sketch_stat.astype(jnp.float32), inverse.T, precision=HIGHEST

time: 82.2 us -> 72.8 us (0.89)
  blocking collectives: 11.8 us -> 0 us
  waiting for transfers between devices: 10.9 us -> 12.4 us
  local copies, waits for them, and re-layouts: 3.76 us -> 2.62 us
  matrix products: 8.43 us -> 9.38 us
    all_to_all x1 -> x0, blocking collectives: 11.8 us -> none  [per_device(): lax.all_to_all(outgoing, 'rows', split_axis=0, concat_axis=0, tiled=True)]
    unnamed x11 -> x7, local copies, waits for them, and re-layouts: 3.47 us -> 1.78 us
    ppermute x5, waiting for transfers between devices: 10.9 us -> 12.4 us  [the longest x3 7.22 us: all_sum_and_route(): got = lax.ppermute(packet, AXES, perm)]
    dot_general x2, matrix products: 2.07 us -> 3.02 us  [sketch_block(): jnp.dot(block, omega, preferred_element_type=jnp.float32)]
  transfers between devices with their start and end apart: 5 -> 5, of which waited for: 4 -> 5; matrix products, arithmetic and copies ran while one was open for 1% -> 1% of each run, Pallas kernels for 0% -> 0%
where the time goes in v3:
time: 72.8 us; the launch traced here: 72.3 us
  other arithmetic  35.9 us (49%)
  waiting for transfers between devices  12.4 us (17%)
  starting transfers between devices  10.2 us (14%)
  matrix products  9.38 us (13%)
  local copies, waits for them, and re-layouts  2.62 us (4%)
  between operations  1.75 us (2%)
    another operation x3, other arithmetic, cholesky_and_inverse(): l11 = lax.linalg.cholesky(a11, symmetrize_input=False)  9.45 us
    another operation x3, other arithmetic, cholesky_and_inverse(): l22 = lax.linalg.cholesky(s, symmetrize_input=False)  9.45 us
    another operation x2, other arithmetic, cholesky_and_inverse(): i11 = lax.linalg.triangular_solve(l11, eye, left_side=True, lower=True)  8.01 us
    another operation x2, other arithmetic, cholesky_and_inverse(): i22 = lax.linalg.triangular_solve(l22, eye, left_side=True, lower=True)  8.01 us
    ppermute x3, waiting for transfers between devices, all_sum_and_route(): got = lax.ppermute(packet, AXES, perm)  7.22 us
    ppermute x3, starting transfers between devices, all_sum_and_route(): got = lax.ppermute(packet, AXES, perm)  5.33 us
    ppermute x2, waiting for transfers between devices, all_sum_and_route(): x = x + lax.ppermute(x, AXES, perm)  5.23 us
    ppermute x2, starting transfers between devices, all_sum_and_route(): x = x + lax.ppermute(x, AXES, perm)  4.87 us
  transfers between devices with their start and end apart: 5, of which 5 were waited for; matrix products, arithmetic and copies ran while one was open for 1% of the time, Pallas kernels for 0%

profile of v3, /device:TPU:0, one launch (start us, length us, event | category | flops | bytes accessed | tf_op | source)
XLA Modules:
  0.0 72.3 jit_solution(2519574463297680463)
XLA Ops:
  1.5 1.1 %convolution_convert_fusion.4 = bf16[32,192]{1,0:T(8,128)(2,1)S(1)} fusion(bf16[32,512]{1,0:T(8,128)(2,1)} %param.9, bf16[512,192]{0,1:T(8,128)(2,1)} %param.12), kind=kOutput, calls=%fused_computation.7 | convolution fusion | flops 6297600 | bytes 241664 | tf_op jit(solution)/shard_map/dot_general | solution.py:12
  2.6 1.9 %convolution_convert_fusion.1 = bf16[2560,192]{0,1:T(8,128)(2,1)S(1)} fusion(bf16[2560,512]{1,0:T(8,128)(2,1)S(1)} %copy-done, bf16[512,192]{0,1:T(8,128)(2,1)} %param.12), kind=kOutput, calls=%fused_computation.1 | convolution fusion | flops 503808000 | bytes 3801088 | tf_op jit(solution)/shard_map/dot_general | solution.py:12
  4.5 0.9 %copy-done.1 = bf16[2560,192]{0,1:T(8,128)(2,1)} copy-done((bf16[2560,192]{0,1:T(8,128)(2,1)}, bf16[2560,192]{0,1:T(8,128)(2,1)S(1)}, u32[]{:S(2)}) %copy-start.1) | copy-done | bytes 983064
  5.5 0.4 fusion.38
  5.9 0.3 fusion
  6.3 3.1 %collective-permute-start = (f32[193,96]{1,0:T(8,128)S(1)}, f32[193,96]{1,0:T(8,128)S(1)}, u32[]{:S(2)}, u32[]{:S(2)}) collective-permute-start(f32[193,96]{1,0:T(8,128)S(1)} %pad_maximum_fusion.3), channel_id=1, source_target_pairs={{0,16},{1,17},{2,18},{3,19},{4,20},{5,21},{6,22},{7,23},{8,24},{9,... | collective-permute-start | bytes 222344 | tf_op jit(solution)/shard_map/ppermute | solution.py:46
  9.5 0.2 select_reduce_fusion.2
  9.9 2.4 %collective-permute-done = f32[193,96]{1,0:T(8,128)S(1)} collective-permute-done((f32[193,96]{1,0:T(8,128)S(1)}, f32[193,96]{1,0:T(8,128)S(1)}, u32[]{:S(2)}, u32[]{:S(2)}) %collective-permute-start) | collective-permute-done | bytes 74144 | tf_op jit(solution)/shard_map/ppermute | solution.py:46
  12.3 1.8 %collective-permute-start.1 = (f32[193,96]{1,0:T(8,128)S(1)}, f32[193,96]{1,0:T(8,128)S(1)}, u32[]{:S(2)}, u32[]{:S(2)}) collective-permute-start(f32[193,96]{1,0:T(8,128)S(1)} %fusion.35), channel_id=1, source_target_pairs={{0,8},{1,9},{2,10},{3,11},{4,12},{5,13},{6,14},{7,15},{8,0},{9,1},... | collective-permute-start | bytes 222344 | tf_op jit(solution)/shard_map/ppermute | solution.py:46
  14.2 2.8 %collective-permute-done.1 = f32[193,96]{1,0:T(8,128)S(1)} collective-permute-done((f32[193,96]{1,0:T(8,128)S(1)}, f32[193,96]{1,0:T(8,128)S(1)}, u32[]{:S(2)}, u32[]{:S(2)}) %collective-permute-start.1) | collective-permute-done | bytes 74144 | tf_op jit(solution)/shard_map/ppermute | solution.py:46
  17.0 2.9 %collective-permute-start.2 = (f32[241,96]{1,0:T(8,128)S(1)}, f32[241,96]{1,0:T(8,128)S(1)}, u32[]{:S(2)}, u32[]{:S(2)}) collective-permute-start(f32[241,96]{1,0:T(8,128)S(1)} %pad_maximum_fusion), channel_id=1, source_target_pairs={{0,4},{1,5},{2,6},{3,7},{4,0},{5,1},{6,2},{7,3},{8,12},{9,13},{10,... | collective-permute-start | bytes 277640 | tf_op jit(solution)/shard_map/ppermute | solution.py:53
  20.0 3.0 %collective-permute-done.2 = f32[241,96]{1,0:T(8,128)S(1)} collective-permute-done((f32[241,96]{1,0:T(8,128)S(1)}, f32[241,96]{1,0:T(8,128)S(1)}, u32[]{:S(2)}, u32[]{:S(2)}) %collective-permute-start.2) | collective-permute-done | bytes 92576 | tf_op jit(solution)/shard_map/ppermute | solution.py:53
  23.2 2.3 %collective-permute-start.3 = (f32[241,96]{1,0:T(8,128)S(1)}, f32[241,96]{1,0:T(8,128)S(1)}, u32[]{:S(2)}, u32[]{:S(2)}) collective-permute-start(f32[241,96]{1,0:T(8,128)S(1)} %pad_maximum_fusion.1), channel_id=1, source_target_pairs={{0,2},{1,3},{2,0},{3,1},{4,6},{5,7},{6,4},{7,5},{8,10},{9,11},{10,... | collective-permute-start | bytes 277640 | tf_op jit(solution)/shard_map/ppermute | solution.py:53
  25.5 2.9 %collective-permute-done.3 = f32[241,96]{1,0:T(8,128)S(1)} collective-permute-done((f32[241,96]{1,0:T(8,128)S(1)}, f32[241,96]{1,0:T(8,128)S(1)}, u32[]{:S(2)}, u32[]{:S(2)}) %collective-permute-start.3) | collective-permute-done | bytes 92576 | tf_op jit(solution)/shard_map/ppermute | solution.py:53
  28.9 1.3 %collective-permute-done.4 = f32[241,96]{1,0:T(8,128)S(1)} collective-permute-done((f32[241,96]{1,0:T(8,128)S(1)}, f32[241,96]{1,0:T(8,128)S(1)}, u32[]{:S(2)}, u32[]{:S(2)}) %collective-permute-start.4) | collective-permute-done | bytes 92576 | tf_op jit(solution)/shard_map/ppermute | solution.py:53
  30.4 8.8 %custom-call.8 = f32[96,96]{1,0:T(8,128)S(1)} custom-call(f32[96,96]{1,0:T(8,128)S(1)} %bitcast_select_fusion.1), custom_call_target="Cholesky" | custom-call | tf_op jit(solution)/shard_map/cholesky/custom-call.1 | solution.py:67
  39.2 0.6 compare_reduce_fusion.1
  39.8 0.7 select_bitcast_fusion.1
  40.5 7.4 %custom-call.9 = f32[1,96,96]{1,2,0:T(8,128)S(1)} custom-call(f32[1,96,96]{2,1,0:T(8,128)S(1)} %get-tuple-element.16), custom_call_target="InvertDiagBlocksLowerTriangular" | custom-call | tf_op jit(solution)/shard_map/triangular_solve/custom-call.0 | solution.py:68
  47.9 0.3 fusion.8
  48.1 0.2 fusion.10
  48.4 0.3 fusion.39
  49.0 0.3 fusion.15
  49.3 8.8 %custom-call.10 = f32[96,96]{1,0:T(8,128)S(1)} custom-call(f32[96,96]{1,0:T(8,128)S(1)} %fusion.15), custom_call_target="Cholesky" | custom-call | tf_op jit(solution)/shard_map/cholesky/custom-call.1 | solution.py:71
  58.1 0.6 compare_reduce_fusion
  58.7 0.7 select_bitcast_fusion
  59.4 7.4 %custom-call.11 = f32[1,96,96]{1,2,0:T(8,128)S(1)} custom-call(f32[1,96,96]{2,1,0:T(8,128)S(1)} %get-tuple-element.14), custom_call_target="InvertDiagBlocksLowerTriangular" | custom-call | tf_op jit(solution)/shard_map/triangular_solve/custom-call.0 | solution.py:72
  66.8 0.2 fusion.6
  67.1 0.3 convolution_negate_fusion
  67.4 3.1 %convolution_convert_fusion = bf16[2560,192]{0,1:T(8,128)(2,1)} fusion(bf16[2560,192]{0,1:T(8,128)(2,1)} %copy-done.1, f32[96,96]{1,0:T(8,128)S(1)} %fusion.8, f32[96,96]{1,0:T(8,128)S(1)} %copy.33, f32[96,96]{1,0:T(8,128)S(1)} %convolution_negate_fusion), kind=kOutput, calls=%fused_computation | convolution fusion | flops 1133101056 | bytes 2076672 | tf_op jit(solution)/shard_map/dot_general | solution.py:117
  70.5 0.9 %convolution_convert_fusion.2 = bf16[48,192]{1,0:T(8,128)(2,1)} fusion(bf16[48,192]{1,0:T(8,128)(2,1)S(1)} %reshape_reshape.12, f32[96,96]{1,0:T(8,128)S(1)} %fusion.8, f32[96,96]{1,0:T(8,128)S(1)} %copy.33, f32[96,96]{1,0:T(8,128)S(1)} %convolution_negate_fusion), kind=kOutput, calls=%fused_computation.5 | convolution fusion | flops 21390336 | bytes 147456 | tf_op jit(solution)/shard_map/dot_general | solution.py:120
  71.5 0.8 %copy.38 = f32[192,192]{1,0:T(8,128)} copy(f32[192,192]{0,1:T(8,128)S(1)} %fusion.1) | data formatting | bytes 294912
  (51 shorter events, 1.9 us)
Async XLA Ops:
  0.6 1.9 %copy-start = (bf16[2560,512]{1,0:T(8,128)(2,1)S(1)}, bf16[2560,512]{1,0:T(8,128)(2,1)}, u32[]{:S(2)}) copy-start(bf16[2560,512]{1,0:T(8,128)(2,1)} %param.8) | copy-start | bytes 7864324
  4.5 1.0 %copy-start.1 = (bf16[2560,192]{0,1:T(8,128)(2,1)}, bf16[2560,192]{0,1:T(8,128)(2,1)S(1)}, u32[]{:S(2)}) copy-start(bf16[2560,192]{0,1:T(8,128)(2,1)S(1)} %convolution_convert_fusion.1) | copy-start | bytes 2949124
  5.5 3.9 %copy-start.2 = (s32[32,1]{0,1:T(1,128)S(1)}, s32[32,1]{0,1:T(1,128)}, u32[]{:S(2)}) copy-start(s32[32,1]{0,1:T(1,128)} %param.10) | copy-start | bytes 388
  6.3 5.9 %collective-permute-start = (f32[193,96]{1,0:T(8,128)S(1)}, f32[193,96]{1,0:T(8,128)S(1)}, u32[]{:S(2)}, u32[]{:S(2)}) collective-permute-start(f32[193,96]{1,0:T(8,128)S(1)} %pad_maximum_fusion.3), channel_id=1, source_target_pairs={{0,16},{1,17},{2,18},{3,19},{4,20},{5,21},{6,22},{7,23},{8,24},{9,... | collective-permute-start | bytes 222344 | tf_op jit(solution)/shard_map/ppermute | solution.py:46
  12.3 4.7 %collective-permute-start.1 = (f32[193,96]{1,0:T(8,128)S(1)}, f32[193,96]{1,0:T(8,128)S(1)}, u32[]{:S(2)}, u32[]{:S(2)}) collective-permute-start(f32[193,96]{1,0:T(8,128)S(1)} %fusion.35), channel_id=1, source_target_pairs={{0,8},{1,9},{2,10},{3,11},{4,12},{5,13},{6,14},{7,15},{8,0},{9,1},... | collective-permute-start | bytes 222344 | tf_op jit(solution)/shard_map/ppermute | solution.py:46
  17.0 5.9 %collective-permute-start.2 = (f32[241,96]{1,0:T(8,128)S(1)}, f32[241,96]{1,0:T(8,128)S(1)}, u32[]{:S(2)}, u32[]{:S(2)}) collective-permute-start(f32[241,96]{1,0:T(8,128)S(1)} %pad_maximum_fusion), channel_id=1, source_target_pairs={{0,4},{1,5},{2,6},{3,7},{4,0},{5,1},{6,2},{7,3},{8,12},{9,13},{10,... | collective-permute-start | bytes 277640 | tf_op jit(solution)/shard_map/ppermute | solution.py:53
  23.2 5.3 %collective-permute-start.3 = (f32[241,96]{1,0:T(8,128)S(1)}, f32[241,96]{1,0:T(8,128)S(1)}, u32[]{:S(2)}, u32[]{:S(2)}) collective-permute-start(f32[241,96]{1,0:T(8,128)S(1)} %pad_maximum_fusion.1), channel_id=1, source_target_pairs={{0,2},{1,3},{2,0},{3,1},{4,6},{5,7},{6,4},{7,5},{8,10},{9,11},{10,... | collective-permute-start | bytes 277640 | tf_op jit(solution)/shard_map/ppermute | solution.py:53
  28.8 1.4 %collective-permute-start.4 = (f32[241,96]{1,0:T(8,128)S(1)}, f32[241,96]{1,0:T(8,128)S(1)}, u32[]{:S(2)}, u32[]{:S(2)}) collective-permute-start(f32[241,96]{1,0:T(8,128)S(1)} %pad_maximum_fusion.2), channel_id=1, source_target_pairs={{0,1},{1,0},{2,3},{3,2},{4,5},{5,4},{6,7},{7,6},{8,9},{9,8},{10,11... | collective-permute-start | bytes 277640 | tf_op jit(solution)/shard_map/ppermute | solution.py:53

commit v4 on v3

--- a/solution.py
+++ b/solution.py
@@ -1,6 +1,10 @@
+import functools
+
 import jax
 import jax.numpy as jnp
 from jax import lax
+from jax.experimental import pallas as pl
+from jax.experimental.pallas import tpu as pltpu
 from jax.sharding import PartitionSpec as P
 
 CAP = 6
@@ -59,22 +63,56 @@
     return x, held
 
 
+def _chol_kernel(g_ref, u_ref, r_ref, b_ref, *, panel):
+    k = g_ref.shape[0]
+    w = 2 * k
+    kp = ((k + 127) // 128) * 128
+    rows = lax.broadcasted_iota(jnp.int32, (k, k), 0)
+    cols = lax.broadcasted_iota(jnp.int32, (k, k), 1)
+    b_ref[:, :k] = g_ref[...]
+    b_ref[:, k:] = jnp.where(rows == cols, 1.0, 0.0).astype(jnp.float32)
+    sub = lax.broadcasted_iota(jnp.int32, (panel, w), 0)
+    lane = lax.broadcasted_iota(jnp.int32, (panel, w), 1)
+
+    def step(p, carry):
+        base = pl.multiple_of(p * panel, 8)
+        pan = b_ref[pl.ds(base, panel), :]
+        for r in range(panel):
+            row = pan[r : r + 1, :]
+            col = jnp.sum(jnp.where(lane == base + r, pan, 0.0), axis=1, keepdims=True)
+            s = lax.rsqrt(col[r : r + 1, :])
+            v = row * s
+            pan = jnp.where(sub == r, v, jnp.where(sub > r, pan - (col * s) * v, pan))
+        pan = jnp.where((lane < k) & (lane < base + sub), 0.0, pan)
+        b_ref[pl.ds(base, panel), :] = pan
+        part = jnp.where((lane >= base + panel) & (lane < k), pan, 0.0)[:, :kp]
+        upd = lax.dot_general(
+            part, pan, (((0,), (0,)), ((), ())), precision=HIGHEST, preferred_element_type=jnp.float32
+        )
+        b_ref[...] = b_ref[...] - upd[:k]
+        return carry
+
+    lax.fori_loop(0, k // panel, step, 0)
+    u_ref[...] = b_ref[:, :k]
+    r_ref[...] = b_ref[:, k:]
+
+
 def cholesky_and_inverse(g):
     k = g.shape[0]
-    h = k // 2
-    a11, a21, a22 = g[:h, :h], g[h:, :h], g[h:, h:]
-    eye = jnp.eye(h, dtype=jnp.float32)
-    l11 = lax.linalg.cholesky(a11, symmetrize_input=False)
-    i11 = lax.linalg.triangular_solve(l11, eye, left_side=True, lower=True)
-    l21 = jnp.dot(a21, i11.T, precision=HIGHEST)
-    s = a22 - jnp.dot(l21, l21.T, precision=HIGHEST)
-    l22 = lax.linalg.cholesky(s, symmetrize_input=False)
-    i22 = lax.linalg.triangular_solve(l22, eye, left_side=True, lower=True)
-    i21 = -jnp.dot(i22, jnp.dot(l21, i11, precision=HIGHEST), precision=HIGHEST)
-    z = jnp.zeros((h, h), jnp.float32)
-    lower = jnp.block([[l11, z], [l21, l22]])
-    inverse = jnp.block([[i11, z], [i21, i22]])
-    return lower, inverse
+    panel = next((p for p in (96, 64, 48, 32, 16, 8) if k % p == 0), None)
+    if panel is None:
+        lower = jnp.linalg.cholesky(g)
+        eye = jnp.eye(k, dtype=jnp.float32)
+        return lower.T, lax.linalg.triangular_solve(lower, eye, left_side=True, lower=True)
+    vmem = pl.BlockSpec(memory_space=pltpu.VMEM)
+    out = jax.ShapeDtypeStruct((k, k), jnp.float32)
+    return pl.pallas_call(
+        functools.partial(_chol_kernel, panel=panel),
+        out_shape=(out, out),
+        in_specs=[vmem],
+        out_specs=(vmem, vmem),
+        scratch_shapes=[pltpu.VMEM((k, 2 * k), jnp.float32)],
+    )(g)
 
 
 def per_device(stationary, rotor_rows, owners, counts, omega):
@@ -113,14 +151,14 @@
         packed, arrived = all_sum_and_route(packed, outgoing, n, n_rows)
     arrived = arrived.reshape(n_rows * CAP, -1)
     gram = unpack_sym(packed)
-    lower, inverse = cholesky_and_inverse(gram)
+    upper, inverse = cholesky_and_inverse(gram)
     basis_stat = jnp.dot(
         sketch_stat.astype(jnp.float32), inverse.T, precision=HIGHEST
     ).astype(jnp.bfloat16)
     basis_rot = jnp.dot(arrived.astype(jnp.float32), inverse.T, precision=HIGHEST).astype(
         jnp.bfloat16
     )
-    return (basis_stat, basis_rot, lower.T)
+    return (basis_stat, basis_rot, upper)
 
 
 def solution(mesh):

time: 72.8 us -> 58.2 us (0.80)
  other arithmetic: 35.9 us -> 2.22 us
  Pallas kernels: 0 us -> 20.8 us
  waiting for transfers between devices: 12.4 us -> 11.3 us
    another operation x10 -> x0, other arithmetic: 34.9 us -> none  [the longest x3 9.45 us: cholesky_and_inverse(): l11 = lax.linalg.cholesky(a11, symmetrize_input=False)]
    pallas_call x0 -> x1, Pallas kernels: none -> 20.8 us  [cholesky_and_inverse(): pl.pallas_call(functools.partial(_chol_kernel, panel=panel), out_shape=(o...]
    dot_general x4 -> x0, matrix products: 1.02 us -> none  [the longest x2 0.53 us: cholesky_and_inverse(): i21 = -jnp.dot(i22, jnp.dot(l21, i11, precision=HIGHEST), precision=HIGHEST)]
    dot_general x1, matrix products: 0.9 us -> 1.78 us  [per_device(): jnp.dot(arrived.astype(jnp.float32), inverse.T, precision=HIGHEST)]
    ppermute x3, waiting for transfers between devices: 7.22 us -> 6.38 us  [all_sum_and_route(): got = lax.ppermute(packet, AXES, perm)]
    unnamed x7 -> x6, local copies, waits for them, and re-layouts: 1.78 us -> 0.98 us
    concatenate x0 -> x1, other arithmetic: none -> 0.8 us  [unpack_sym(): jnp.concatenate([jnp.concatenate([a, b.T], axis=1), jnp.concatenate([b, c...]
where the time goes in v4:
time: 58.2 us; the launch traced here: 57.8 us
  Pallas kernels  20.8 us (36%)
  waiting for transfers between devices  11.3 us (19%)
  starting transfers between devices  10 us (17%)
  matrix products  8.75 us (15%)
  local copies, waits for them, and re-layouts  2.94 us (5%)
  other arithmetic  2.22 us (4%)
  between operations  1.7 us (3%)
    pallas_call x1, Pallas kernels, cholesky_and_inverse(): pl.pallas_call(functools.partial(_chol_kernel, panel=panel), out_shape=(o...  20.8 us
    ppermute x3, waiting for transfers between devices, all_sum_and_route(): got = lax.ppermute(packet, AXES, perm)  6.38 us
    ppermute x3, starting transfers between devices, all_sum_and_route(): got = lax.ppermute(packet, AXES, perm)  5.11 us
    ppermute x2, waiting for transfers between devices, all_sum_and_route(): x = x + lax.ppermute(x, AXES, perm)  4.96 us
    ppermute x2, starting transfers between devices, all_sum_and_route(): x = x + lax.ppermute(x, AXES, perm)  4.91 us
    dot_general x1, matrix products, per_device(): jnp.dot(sketch_stat.astype(jnp.float32), inverse.T, precision=HIGHEST)  3.09 us
    dot_general x2, matrix products, sketch_block(): jnp.dot(block, omega, preferred_element_type=jnp.float32)  3.02 us
    dot_general x1, matrix products, per_device(): jnp.dot(arrived.astype(jnp.float32), inverse.T, precision=HIGHEST)  1.78 us
  transfers between devices with their start and end apart: 5, of which 5 were waited for; matrix products, arithmetic and copies ran while one was open for 1% of the time, Pallas kernels for 0%

profile of v4, /device:TPU:0, one launch (start us, length us, event | category | flops | bytes accessed | tf_op | source)
XLA Modules:
  0.0 57.8 jit_solution(4627664721502413758)
XLA Ops:
  1.5 1.1 %convolution_convert_fusion.4 = bf16[32,192]{1,0:T(8,128)(2,1)S(1)} fusion(bf16[32,512]{1,0:T(8,128)(2,1)} %param.6, bf16[512,192]{0,1:T(8,128)(2,1)} %param.9), kind=kOutput, calls=%fused_computation.6 | convolution fusion | flops 6297600 | bytes 241664 | tf_op jit(solution)/shard_map/dot_general | solution.py:16
  2.6 1.9 %convolution_convert_fusion.1 = bf16[2560,192]{0,1:T(8,128)(2,1)S(1)} fusion(bf16[2560,512]{1,0:T(8,128)(2,1)S(1)} %copy-done, bf16[512,192]{0,1:T(8,128)(2,1)} %param.9), kind=kOutput, calls=%fused_computation.1 | convolution fusion | flops 503808000 | bytes 3801088 | tf_op jit(solution)/shard_map/dot_general | solution.py:16
  4.5 0.9 %copy-done.1 = bf16[2560,192]{0,1:T(8,128)(2,1)} copy-done((bf16[2560,192]{0,1:T(8,128)(2,1)}, bf16[2560,192]{0,1:T(8,128)(2,1)S(1)}, u32[]{:S(2)}) %copy-start.1) | copy-done | bytes 983064
  5.5 0.4 fusion.13
  5.9 0.3 fusion
  6.2 0.2 fusion.12
  6.4 0.1 copy.27
  6.5 0.1 pad_maximum_fusion
  6.6 3.1 %collective-permute-start = (f32[193,96]{0,1:T(8,128)S(1)}, f32[193,96]{0,1:T(8,128)S(1)}, u32[]{:S(2)}, u32[]{:S(2)}) collective-permute-start(f32[193,96]{0,1:T(8,128)S(1)} %pad_maximum_fusion), channel_id=1, source_target_pairs={{0,16},{1,17},{2,18},{3,19},{4,20},{5,21},{6,22},{7,23},{8,24},{9,... | collective-permute-start | bytes 222344 | tf_op jit(solution)/shard_map/ppermute | solution.py:50
  9.8 0.2 select_reduce_fusion.1
  10.0 0.1 convolution_convert_fusion.3
  10.2 2.3 %collective-permute-done = f32[193,96]{0,1:T(8,128)S(1)} collective-permute-done((f32[193,96]{0,1:T(8,128)S(1)}, f32[193,96]{0,1:T(8,128)S(1)}, u32[]{:S(2)}, u32[]{:S(2)}) %collective-permute-start) | collective-permute-done | bytes 74144 | tf_op jit(solution)/shard_map/ppermute | solution.py:50
  12.5 0.1 fusion.25
  12.6 1.9 %collective-permute-start.1 = (f32[193,96]{0,1:T(8,128)S(1)}, f32[193,96]{0,1:T(8,128)S(1)}, u32[]{:S(2)}, u32[]{:S(2)}) collective-permute-start(f32[193,96]{0,1:T(8,128)S(1)} %fusion.25), channel_id=1, source_target_pairs={{0,8},{1,9},{2,10},{3,11},{4,12},{5,13},{6,14},{7,15},{8,0},{9,1},... | collective-permute-start | bytes 222344 | tf_op jit(solution)/shard_map/ppermute | solution.py:50
  14.5 0.1 copy.28
  14.6 2.6 %collective-permute-done.1 = f32[193,96]{0,1:T(8,128)S(1)} collective-permute-done((f32[193,96]{0,1:T(8,128)S(1)}, f32[193,96]{0,1:T(8,128)S(1)}, u32[]{:S(2)}, u32[]{:S(2)}) %collective-permute-start.1) | collective-permute-done | bytes 74144 | tf_op jit(solution)/shard_map/ppermute | solution.py:50
  17.4 3.0 %collective-permute-start.2 = (f32[241,96]{0,1:T(8,128)S(1)}, f32[241,96]{0,1:T(8,128)S(1)}, u32[]{:S(2)}, u32[]{:S(2)}) collective-permute-start(f32[241,96]{0,1:T(8,128)S(1)} %pad_maximum_fusion.1), channel_id=1, source_target_pairs={{0,4},{1,5},{2,6},{3,7},{4,0},{5,1},{6,2},{7,3},{8,12},{9,13},{10,... | collective-permute-start | bytes 277640 | tf_op jit(solution)/shard_map/ppermute | solution.py:57
  20.3 2.6 %collective-permute-done.2 = f32[241,96]{0,1:T(8,128)S(1)} collective-permute-done((f32[241,96]{0,1:T(8,128)S(1)}, f32[241,96]{0,1:T(8,128)S(1)}, u32[]{:S(2)}, u32[]{:S(2)}) %collective-permute-start.2) | collective-permute-done | bytes 92576 | tf_op jit(solution)/shard_map/ppermute | solution.py:57
  23.1 0.1 convert_element_type.94
  23.3 0.1 copy.32
  23.5 2.1 %collective-permute-start.3 = (f32[241,96]{0,1:T(8,128)S(1)}, f32[241,96]{0,1:T(8,128)S(1)}, u32[]{:S(2)}, u32[]{:S(2)}) collective-permute-start(f32[241,96]{0,1:T(8,128)S(1)} %pad_maximum_fusion.2), channel_id=1, source_target_pairs={{0,2},{1,3},{2,0},{3,1},{4,6},{5,7},{6,4},{7,5},{8,10},{9,11},{10,... | collective-permute-start | bytes 277640 | tf_op jit(solution)/shard_map/ppermute | solution.py:57
  25.6 2.6 %collective-permute-done.3 = f32[241,96]{0,1:T(8,128)S(1)} collective-permute-done((f32[241,96]{0,1:T(8,128)S(1)}, f32[241,96]{0,1:T(8,128)S(1)}, u32[]{:S(2)}, u32[]{:S(2)}) %collective-permute-start.3) | collective-permute-done | bytes 92576 | tf_op jit(solution)/shard_map/ppermute | solution.py:57
  28.4 0.1 convert_element_type.97
  29.0 0.1 copy.36
  29.1 1.2 %collective-permute-done.4 = f32[241,96]{0,1:T(8,128)S(1)} collective-permute-done((f32[241,96]{0,1:T(8,128)S(1)}, f32[241,96]{0,1:T(8,128)S(1)}, u32[]{:S(2)}, u32[]{:S(2)}) %collective-permute-start.4) | collective-permute-done | bytes 92576 | tf_op jit(solution)/shard_map/ppermute | solution.py:57
  30.3 0.2 slice_reduce_fusion
  30.7 0.1 convert_element_type.106
  30.8 0.1 broadcast_select_fusion.1
  31.3 0.8 %maximum_maximum_fusion.g_ref = f32[192,192]{1,0:T(8,128)} fusion(f32[96,96]{1,0:T(8,128)S(1)} %get-tuple-element.11, f32[96,96]{1,0:T(8,128)S(1)} %copy.39, f32[96,96]{1,0:T(8,128)S(1)} %get-tuple-element.12, f32[96,96]{1,0:T(8,128)S(1)} %get-tuple-element.10), kind=kLoop, calls=%fused_computation.7 | loop fusion | flops 110592 | bytes 294912 | tf_op jit(solution)/shard_map/concatenate | solution.py:37
  32.1 20.8 %shard_map.76 = (f32[192,192]{1,0:T(8,128)}, f32[192,192]{1,0:T(8,128)}) custom-call(f32[192,192]{1,0:T(8,128)} %maximum_maximum_fusion.g_ref), custom_call_target="tpu_custom_call" | custom-call | tf_op jit(solution)/shard_map/pallas_call | solution.py:109
  52.9 3.1 %convolution_convert_fusion = bf16[2560,192]{0,1:T(8,128)(2,1)} fusion(bf16[2560,192]{0,1:T(8,128)(2,1)} %copy-done.1, f32[192,192]{1,0:T(8,128)} %get-tuple-element.5), kind=kOutput, calls=%fused_computation | convolution fusion | flops 1132953600 | bytes 2113536 | tf_op jit(solution)/shard_map/dot_general | solution.py:155
  56.0 1.8 %convolution_convert_fusion.2 = bf16[48,192]{1,0:T(8,128)(2,1)} fusion(bf16[48,192]{1,0:T(8,128)(2,1)S(1)} %reshape_reshape.12, f32[192,192]{1,0:T(8,128)} %get-tuple-element.5), kind=kOutput, calls=%fused_computation.4 | convolution fusion | flops 21242880 | bytes 184320 | tf_op jit(solution)/shard_map/dot_general | solution.py:158
  (43 shorter events, 2.0 us)
Async XLA Ops:
  0.6 1.9 %copy-start = (bf16[2560,512]{1,0:T(8,128)(2,1)S(1)}, bf16[2560,512]{1,0:T(8,128)(2,1)}, u32[]{:S(2)}) copy-start(bf16[2560,512]{1,0:T(8,128)(2,1)} %param.5) | copy-start | bytes 7864324
  4.5 1.0 %copy-start.1 = (bf16[2560,192]{0,1:T(8,128)(2,1)}, bf16[2560,192]{0,1:T(8,128)(2,1)S(1)}, u32[]{:S(2)}) copy-start(bf16[2560,192]{0,1:T(8,128)(2,1)S(1)} %convolution_convert_fusion.1) | copy-start | bytes 2949124
  5.5 4.2 %copy-start.2 = (s32[32,1]{0,1:T(1,128)S(1)}, s32[32,1]{0,1:T(1,128)}, u32[]{:S(2)}) copy-start(s32[32,1]{0,1:T(1,128)} %param.7) | copy-start | bytes 388
  6.6 5.9 %collective-permute-start = (f32[193,96]{0,1:T(8,128)S(1)}, f32[193,96]{0,1:T(8,128)S(1)}, u32[]{:S(2)}, u32[]{:S(2)}) collective-permute-start(f32[193,96]{0,1:T(8,128)S(1)} %pad_maximum_fusion), channel_id=1, source_target_pairs={{0,16},{1,17},{2,18},{3,19},{4,20},{5,21},{6,22},{7,23},{8,24},{9,... | collective-permute-start | bytes 222344 | tf_op jit(solution)/shard_map/ppermute | solution.py:50
  12.6 4.7 %collective-permute-start.1 = (f32[193,96]{0,1:T(8,128)S(1)}, f32[193,96]{0,1:T(8,128)S(1)}, u32[]{:S(2)}, u32[]{:S(2)}) collective-permute-start(f32[193,96]{0,1:T(8,128)S(1)} %fusion.25), channel_id=1, source_target_pairs={{0,8},{1,9},{2,10},{3,11},{4,12},{5,13},{6,14},{7,15},{8,0},{9,1},... | collective-permute-start | bytes 222344 | tf_op jit(solution)/shard_map/ppermute | solution.py:50
  17.4 5.6 %collective-permute-start.2 = (f32[241,96]{0,1:T(8,128)S(1)}, f32[241,96]{0,1:T(8,128)S(1)}, u32[]{:S(2)}, u32[]{:S(2)}) collective-permute-start(f32[241,96]{0,1:T(8,128)S(1)} %pad_maximum_fusion.1), channel_id=1, source_target_pairs={{0,4},{1,5},{2,6},{3,7},{4,0},{5,1},{6,2},{7,3},{8,12},{9,13},{10,... | collective-permute-start | bytes 277640 | tf_op jit(solution)/shard_map/ppermute | solution.py:57
  23.5 4.7 %collective-permute-start.3 = (f32[241,96]{0,1:T(8,128)S(1)}, f32[241,96]{0,1:T(8,128)S(1)}, u32[]{:S(2)}, u32[]{:S(2)}) collective-permute-start(f32[241,96]{0,1:T(8,128)S(1)} %pad_maximum_fusion.2), channel_id=1, source_target_pairs={{0,2},{1,3},{2,0},{3,1},{4,6},{5,7},{6,4},{7,5},{8,10},{9,11},{10,... | collective-permute-start | bytes 277640 | tf_op jit(solution)/shard_map/ppermute | solution.py:57
  28.9 1.4 %collective-permute-start.4 = (f32[241,96]{0,1:T(8,128)S(1)}, f32[241,96]{0,1:T(8,128)S(1)}, u32[]{:S(2)}, u32[]{:S(2)}) collective-permute-start(f32[241,96]{0,1:T(8,128)S(1)} %pad_maximum_fusion.3), channel_id=1, source_target_pairs={{0,1},{1,0},{2,3},{3,2},{4,5},{5,4},{6,7},{7,6},{8,9},{9,8},{10,11... | collective-permute-start | bytes 277640 | tf_op jit(solution)/shard_map/ppermute | solution.py:57

commit v5 on v4

--- a/solution.py
+++ b/solution.py
@@ -71,28 +71,48 @@
     cols = lax.broadcasted_iota(jnp.int32, (k, k), 1)
     b_ref[:, :k] = g_ref[...]
     b_ref[:, k:] = jnp.where(rows == cols, 1.0, 0.0).astype(jnp.float32)
-    sub = lax.broadcasted_iota(jnp.int32, (panel, w), 0)
-    lane = lax.broadcasted_iota(jnp.int32, (panel, w), 1)
-
-    def step(p, carry):
-        base = pl.multiple_of(p * panel, 8)
-        pan = b_ref[pl.ds(base, panel), :]
-        for r in range(panel):
-            row = pan[r : r + 1, :]
-            col = jnp.sum(jnp.where(lane == base + r, pan, 0.0), axis=1, keepdims=True)
-            s = lax.rsqrt(col[r : r + 1, :])
-            v = row * s
-            pan = jnp.where(sub == r, v, jnp.where(sub > r, pan - (col * s) * v, pan))
-        pan = jnp.where((lane < k) & (lane < base + sub), 0.0, pan)
-        b_ref[pl.ds(base, panel), :] = pan
-        part = jnp.where((lane >= base + panel) & (lane < k), pan, 0.0)[:, :kp]
-        upd = lax.dot_general(
-            part, pan, (((0,), (0,)), ((), ())), precision=HIGHEST, preferred_element_type=jnp.float32
-        )
-        b_ref[...] = b_ref[...] - upd[:k]
-        return carry
-
-    lax.fori_loop(0, k // panel, step, 0)
+    for p in range(k // panel):
+        base = p * panel
+        end = base + panel
+        pan = b_ref[base:end, :]
+        for r in range(0, panel, 2):
+            piv = base + r
+            t0 = (piv // 128) * 128
+            s0 = (r // 8) * 8
+            top, low = pan[:s0], pan[s0:]
+            m = panel - s0
+            i0, i1 = r - s0, r + 1 - s0
+            row0, row1 = low[i0 : i0 + 1], low[i1 : i1 + 1]
+            lane = lax.broadcasted_iota(jnp.int32, (m, 128), 1) + t0
+            blk = low[:, t0 : t0 + 128]
+            c0 = jnp.sum(jnp.where(lane == piv, blk, 0.0), axis=1, keepdims=True)
+            c1 = jnp.sum(jnp.where(lane == piv + 1, blk, 0.0), axis=1, keepdims=True)
+            s1 = lax.rsqrt(c0[i0 : i0 + 1])
+            v1 = row0 * s1
+            coef1 = c0 * s1
+            l = coef1[i1 : i1 + 1]
+            c1p = c1 - coef1 * l
+            s2 = lax.rsqrt(c1p[i1 : i1 + 1])
+            v2 = (row1 - l * v1) * s2
+            coef2 = c1p * s2
+            sub = lax.broadcasted_iota(jnp.int32, (m, w), 0) + s0
+            low = jnp.where(
+                sub > r + 1,
+                low - coef1 * v1 - coef2 * v2,
+                jnp.where(sub == r, v1, jnp.where(sub == r + 1, v2, low)),
+            )
+            pan = jnp.concatenate([top, low], axis=0) if s0 else low
+        sub = lax.broadcasted_iota(jnp.int32, pan.shape, 0) + base
+        lane = lax.broadcasted_iota(jnp.int32, pan.shape, 1)
+        pan = jnp.where((lane < k) & (lane < sub), 0.0, pan)
+        b_ref[base:end, :] = pan
+        if end < k:
+            part = jnp.where((lane >= end) & (lane < k), pan, 0.0)[:, :kp]
+            upd = lax.dot_general(
+                part, pan, (((0,), (0,)), ((), ())), precision=HIGHEST,
+                preferred_element_type=jnp.float32,
+            )
+            b_ref[end:, :] = b_ref[end:, :] - upd[end:k]
     u_ref[...] = b_ref[:, :k]
     r_ref[...] = b_ref[:, k:]
 

time: 58.2 us -> 49.9 us (0.86)
  Pallas kernels: 20.8 us -> 12.6 us
    pallas_call x1, Pallas kernels: 20.8 us -> 12.6 us  [cholesky_and_inverse(): pl.pallas_call(functools.partial(_chol_kernel, panel=panel), out_shape=(o...]
  transfers between devices with their start and end apart: 5 -> 5, of which waited for: 5 -> 5; matrix products, arithmetic and copies ran while one was open for 1% -> 2% of each run, Pallas kernels for 0% -> 0%
where the time goes in v5:
time: 49.9 us; the launch traced here: 49.6 us
  Pallas kernels  12.6 us (25%)
  waiting for transfers between devices  11.3 us (23%)
  starting transfers between devices  10 us (20%)
  matrix products  8.75 us (18%)
  local copies, waits for them, and re-layouts  2.94 us (6%)
  other arithmetic  2.22 us (4%)
  between operations  1.7 us (3%)
    pallas_call x1, Pallas kernels, cholesky_and_inverse(): pl.pallas_call(functools.partial(_chol_kernel, panel=panel), out_shape=(o...  12.6 us
    ppermute x3, waiting for transfers between devices, all_sum_and_route(): got = lax.ppermute(packet, AXES, perm)  6.38 us
    ppermute x3, starting transfers between devices, all_sum_and_route(): got = lax.ppermute(packet, AXES, perm)  5.11 us
    ppermute x2, waiting for transfers between devices, all_sum_and_route(): x = x + lax.ppermute(x, AXES, perm)  4.96 us
    ppermute x2, starting transfers between devices, all_sum_and_route(): x = x + lax.ppermute(x, AXES, perm)  4.91 us
    dot_general x1, matrix products, per_device(): jnp.dot(sketch_stat.astype(jnp.float32), inverse.T, precision=HIGHEST)  3.09 us
    dot_general x2, matrix products, sketch_block(): jnp.dot(block, omega, preferred_element_type=jnp.float32)  3.02 us
    dot_general x1, matrix products, per_device(): jnp.dot(arrived.astype(jnp.float32), inverse.T, precision=HIGHEST)  1.78 us
  transfers between devices with their start and end apart: 5, of which 5 were waited for; matrix products, arithmetic and copies ran while one was open for 2% of the time, Pallas kernels for 0%

profile of v5, /device:TPU:0, one launch (start us, length us, event | category | flops | bytes accessed | tf_op | source)
XLA Modules:
  0.0 49.6 jit_solution(11907849372742040602)
XLA Ops:
  1.5 1.1 %convolution_convert_fusion.4 = bf16[32,192]{1,0:T(8,128)(2,1)S(1)} fusion(bf16[32,512]{1,0:T(8,128)(2,1)} %param.6, bf16[512,192]{0,1:T(8,128)(2,1)} %param.9), kind=kOutput, calls=%fused_computation.6 | convolution fusion | flops 6297600 | bytes 241664 | tf_op jit(solution)/shard_map/dot_general | solution.py:16
  2.6 1.9 %convolution_convert_fusion.1 = bf16[2560,192]{0,1:T(8,128)(2,1)S(1)} fusion(bf16[2560,512]{1,0:T(8,128)(2,1)S(1)} %copy-done, bf16[512,192]{0,1:T(8,128)(2,1)} %param.9), kind=kOutput, calls=%fused_computation.1 | convolution fusion | flops 503808000 | bytes 3801088 | tf_op jit(solution)/shard_map/dot_general | solution.py:16
  4.5 0.9 %copy-done.1 = bf16[2560,192]{0,1:T(8,128)(2,1)} copy-done((bf16[2560,192]{0,1:T(8,128)(2,1)}, bf16[2560,192]{0,1:T(8,128)(2,1)S(1)}, u32[]{:S(2)}) %copy-start.1) | copy-done | bytes 983064
  5.5 0.4 fusion.13
  5.9 0.3 fusion
  6.2 0.2 fusion.12
  6.4 0.1 copy.27
  6.5 0.1 pad_maximum_fusion
  6.6 3.1 %collective-permute-start = (f32[193,96]{0,1:T(8,128)S(1)}, f32[193,96]{0,1:T(8,128)S(1)}, u32[]{:S(2)}, u32[]{:S(2)}) collective-permute-start(f32[193,96]{0,1:T(8,128)S(1)} %pad_maximum_fusion), channel_id=1, source_target_pairs={{0,16},{1,17},{2,18},{3,19},{4,20},{5,21},{6,22},{7,23},{8,24},{9,... | collective-permute-start | bytes 222344 | tf_op jit(solution)/shard_map/ppermute | solution.py:50
  9.8 0.2 select_reduce_fusion.1
  10.0 0.1 convolution_convert_fusion.3
  10.2 2.3 %collective-permute-done = f32[193,96]{0,1:T(8,128)S(1)} collective-permute-done((f32[193,96]{0,1:T(8,128)S(1)}, f32[193,96]{0,1:T(8,128)S(1)}, u32[]{:S(2)}, u32[]{:S(2)}) %collective-permute-start) | collective-permute-done | bytes 74144 | tf_op jit(solution)/shard_map/ppermute | solution.py:50
  12.5 0.1 fusion.25
  12.6 1.9 %collective-permute-start.1 = (f32[193,96]{0,1:T(8,128)S(1)}, f32[193,96]{0,1:T(8,128)S(1)}, u32[]{:S(2)}, u32[]{:S(2)}) collective-permute-start(f32[193,96]{0,1:T(8,128)S(1)} %fusion.25), channel_id=1, source_target_pairs={{0,8},{1,9},{2,10},{3,11},{4,12},{5,13},{6,14},{7,15},{8,0},{9,1},... | collective-permute-start | bytes 222344 | tf_op jit(solution)/shard_map/ppermute | solution.py:50
  14.5 0.1 copy.28
  14.6 2.6 %collective-permute-done.1 = f32[193,96]{0,1:T(8,128)S(1)} collective-permute-done((f32[193,96]{0,1:T(8,128)S(1)}, f32[193,96]{0,1:T(8,128)S(1)}, u32[]{:S(2)}, u32[]{:S(2)}) %collective-permute-start.1) | collective-permute-done | bytes 74144 | tf_op jit(solution)/shard_map/ppermute | solution.py:50
  17.4 3.0 %collective-permute-start.2 = (f32[241,96]{0,1:T(8,128)S(1)}, f32[241,96]{0,1:T(8,128)S(1)}, u32[]{:S(2)}, u32[]{:S(2)}) collective-permute-start(f32[241,96]{0,1:T(8,128)S(1)} %pad_maximum_fusion.1), channel_id=1, source_target_pairs={{0,4},{1,5},{2,6},{3,7},{4,0},{5,1},{6,2},{7,3},{8,12},{9,13},{10,... | collective-permute-start | bytes 277640 | tf_op jit(solution)/shard_map/ppermute | solution.py:57
  20.3 2.6 %collective-permute-done.2 = f32[241,96]{0,1:T(8,128)S(1)} collective-permute-done((f32[241,96]{0,1:T(8,128)S(1)}, f32[241,96]{0,1:T(8,128)S(1)}, u32[]{:S(2)}, u32[]{:S(2)}) %collective-permute-start.2) | collective-permute-done | bytes 92576 | tf_op jit(solution)/shard_map/ppermute | solution.py:57
  23.1 0.1 convert_element_type.94
  23.5 2.1 %collective-permute-start.3 = (f32[241,96]{0,1:T(8,128)S(1)}, f32[241,96]{0,1:T(8,128)S(1)}, u32[]{:S(2)}, u32[]{:S(2)}) collective-permute-start(f32[241,96]{0,1:T(8,128)S(1)} %pad_maximum_fusion.2), channel_id=1, source_target_pairs={{0,2},{1,3},{2,0},{3,1},{4,6},{5,7},{6,4},{7,5},{8,10},{9,11},{10,... | collective-permute-start | bytes 277640 | tf_op jit(solution)/shard_map/ppermute | solution.py:57
  25.6 2.6 %collective-permute-done.3 = f32[241,96]{0,1:T(8,128)S(1)} collective-permute-done((f32[241,96]{0,1:T(8,128)S(1)}, f32[241,96]{0,1:T(8,128)S(1)}, u32[]{:S(2)}, u32[]{:S(2)}) %collective-permute-start.3) | collective-permute-done | bytes 92576 | tf_op jit(solution)/shard_map/ppermute | solution.py:57
  28.4 0.1 convert_element_type.97
  28.7 0.1 copy.35
  29.0 0.1 copy.36
  29.1 1.2 %collective-permute-done.4 = f32[241,96]{0,1:T(8,128)S(1)} collective-permute-done((f32[241,96]{0,1:T(8,128)S(1)}, f32[241,96]{0,1:T(8,128)S(1)}, u32[]{:S(2)}, u32[]{:S(2)}) %collective-permute-start.4) | collective-permute-done | bytes 92576 | tf_op jit(solution)/shard_map/ppermute | solution.py:57
  30.3 0.2 slice_reduce_fusion
  30.7 0.1 convert_element_type.106
  30.8 0.1 broadcast_select_fusion.1
  31.3 0.8 %maximum_maximum_fusion.g_ref = f32[192,192]{1,0:T(8,128)} fusion(f32[96,96]{1,0:T(8,128)S(1)} %get-tuple-element.11, f32[96,96]{1,0:T(8,128)S(1)} %copy.39, f32[96,96]{1,0:T(8,128)S(1)} %get-tuple-element.12, f32[96,96]{1,0:T(8,128)S(1)} %get-tuple-element.10), kind=kLoop, calls=%fused_computation.7 | loop fusion | flops 110592 | bytes 294912 | tf_op jit(solution)/shard_map/concatenate | solution.py:37
  32.1 12.6 %shard_map.76 = (f32[192,192]{1,0:T(8,128)}, f32[192,192]{1,0:T(8,128)}) custom-call(f32[192,192]{1,0:T(8,128)} %maximum_maximum_fusion.g_ref), custom_call_target="tpu_custom_call" | custom-call | tf_op jit(solution)/shard_map/pallas_call | solution.py:129
  44.7 3.1 %convolution_convert_fusion = bf16[2560,192]{0,1:T(8,128)(2,1)} fusion(bf16[2560,192]{0,1:T(8,128)(2,1)} %copy-done.1, f32[192,192]{1,0:T(8,128)} %get-tuple-element.5), kind=kOutput, calls=%fused_computation | convolution fusion | flops 1132953600 | bytes 2113536 | tf_op jit(solution)/shard_map/dot_general | solution.py:175
  47.8 1.8 %convolution_convert_fusion.2 = bf16[48,192]{1,0:T(8,128)(2,1)} fusion(bf16[48,192]{1,0:T(8,128)(2,1)S(1)} %reshape_reshape.12, f32[192,192]{1,0:T(8,128)} %get-tuple-element.5), kind=kOutput, calls=%fused_computation.4 | convolution fusion | flops 21242880 | bytes 184320 | tf_op jit(solution)/shard_map/dot_general | solution.py:178
  (43 shorter events, 2.0 us)
Async XLA Ops:
  0.6 1.9 %copy-start = (bf16[2560,512]{1,0:T(8,128)(2,1)S(1)}, bf16[2560,512]{1,0:T(8,128)(2,1)}, u32[]{:S(2)}) copy-start(bf16[2560,512]{1,0:T(8,128)(2,1)} %param.5) | copy-start | bytes 7864324
  4.5 1.0 %copy-start.1 = (bf16[2560,192]{0,1:T(8,128)(2,1)}, bf16[2560,192]{0,1:T(8,128)(2,1)S(1)}, u32[]{:S(2)}) copy-start(bf16[2560,192]{0,1:T(8,128)(2,1)S(1)} %convolution_convert_fusion.1) | copy-start | bytes 2949124
  5.5 4.2 %copy-start.2 = (s32[32,1]{0,1:T(1,128)S(1)}, s32[32,1]{0,1:T(1,128)}, u32[]{:S(2)}) copy-start(s32[32,1]{0,1:T(1,128)} %param.7) | copy-start | bytes 388
  6.6 5.9 %collective-permute-start = (f32[193,96]{0,1:T(8,128)S(1)}, f32[193,96]{0,1:T(8,128)S(1)}, u32[]{:S(2)}, u32[]{:S(2)}) collective-permute-start(f32[193,96]{0,1:T(8,128)S(1)} %pad_maximum_fusion), channel_id=1, source_target_pairs={{0,16},{1,17},{2,18},{3,19},{4,20},{5,21},{6,22},{7,23},{8,24},{9,... | collective-permute-start | bytes 222344 | tf_op jit(solution)/shard_map/ppermute | solution.py:50
  12.6 4.7 %collective-permute-start.1 = (f32[193,96]{0,1:T(8,128)S(1)}, f32[193,96]{0,1:T(8,128)S(1)}, u32[]{:S(2)}, u32[]{:S(2)}) collective-permute-start(f32[193,96]{0,1:T(8,128)S(1)} %fusion.25), channel_id=1, source_target_pairs={{0,8},{1,9},{2,10},{3,11},{4,12},{5,13},{6,14},{7,15},{8,0},{9,1},... | collective-permute-start | bytes 222344 | tf_op jit(solution)/shard_map/ppermute | solution.py:50
  17.4 5.6 %collective-permute-start.2 = (f32[241,96]{0,1:T(8,128)S(1)}, f32[241,96]{0,1:T(8,128)S(1)}, u32[]{:S(2)}, u32[]{:S(2)}) collective-permute-start(f32[241,96]{0,1:T(8,128)S(1)} %pad_maximum_fusion.1), channel_id=1, source_target_pairs={{0,4},{1,5},{2,6},{3,7},{4,0},{5,1},{6,2},{7,3},{8,12},{9,13},{10,... | collective-permute-start | bytes 277640 | tf_op jit(solution)/shard_map/ppermute | solution.py:57
  23.5 4.7 %collective-permute-start.3 = (f32[241,96]{0,1:T(8,128)S(1)}, f32[241,96]{0,1:T(8,128)S(1)}, u32[]{:S(2)}, u32[]{:S(2)}) collective-permute-start(f32[241,96]{0,1:T(8,128)S(1)} %pad_maximum_fusion.2), channel_id=1, source_target_pairs={{0,2},{1,3},{2,0},{3,1},{4,6},{5,7},{6,4},{7,5},{8,10},{9,11},{10,... | collective-permute-start | bytes 277640 | tf_op jit(solution)/shard_map/ppermute | solution.py:57
  28.9 1.4 %collective-permute-start.4 = (f32[241,96]{0,1:T(8,128)S(1)}, f32[241,96]{0,1:T(8,128)S(1)}, u32[]{:S(2)}, u32[]{:S(2)}) collective-permute-start(f32[241,96]{0,1:T(8,128)S(1)} %pad_maximum_fusion.3), channel_id=1, source_target_pairs={{0,1},{1,0},{2,3},{3,2},{4,5},{5,4},{6,7},{7,6},{8,9},{9,8},{10,11... | collective-permute-start | bytes 277640 | tf_op jit(solution)/shard_map/ppermute | solution.py:57

commit v6 on v5

--- a/solution.py
+++ b/solution.py
@@ -10,6 +10,7 @@
 CAP = 6
 AXES = ("grp", "rows")
 HIGHEST = lax.Precision.HIGHEST
+GROUP = 8
 
 
 def sketch_block(block, omega):
@@ -75,33 +76,35 @@
         base = p * panel
         end = base + panel
         pan = b_ref[base:end, :]
-        for r in range(0, panel, 2):
+        for r in range(0, panel, GROUP):
             piv = base + r
             t0 = (piv // 128) * 128
-            s0 = (r // 8) * 8
-            top, low = pan[:s0], pan[s0:]
-            m = panel - s0
-            i0, i1 = r - s0, r + 1 - s0
-            row0, row1 = low[i0 : i0 + 1], low[i1 : i1 + 1]
+            top, low = pan[:r], pan[r:]
+            m = panel - r
             lane = lax.broadcasted_iota(jnp.int32, (m, 128), 1) + t0
             blk = low[:, t0 : t0 + 128]
-            c0 = jnp.sum(jnp.where(lane == piv, blk, 0.0), axis=1, keepdims=True)
-            c1 = jnp.sum(jnp.where(lane == piv + 1, blk, 0.0), axis=1, keepdims=True)
-            s1 = lax.rsqrt(c0[i0 : i0 + 1])
-            v1 = row0 * s1
-            coef1 = c0 * s1
-            l = coef1[i1 : i1 + 1]
-            c1p = c1 - coef1 * l
-            s2 = lax.rsqrt(c1p[i1 : i1 + 1])
-            v2 = (row1 - l * v1) * s2
-            coef2 = c1p * s2
-            sub = lax.broadcasted_iota(jnp.int32, (m, w), 0) + s0
-            low = jnp.where(
-                sub > r + 1,
-                low - coef1 * v1 - coef2 * v2,
-                jnp.where(sub == r, v1, jnp.where(sub == r + 1, v2, low)),
-            )
-            pan = jnp.concatenate([top, low], axis=0) if s0 else low
+            cs = [
+                jnp.sum(jnp.where(lane == piv + t, blk, 0.0), axis=1, keepdims=True)
+                for t in range(GROUP)
+            ]
+            coefs, vs = [], []
+            for t in range(GROUP):
+                c, row = cs[t], low[t : t + 1]
+                for u in range(t):
+                    lu = coefs[u][t : t + 1]
+                    c = c - coefs[u] * lu
+                    row = row - lu * vs[u]
+                s = lax.rsqrt(c[t : t + 1])
+                vs.append(row * s)
+                coefs.append(c * s)
+            sub = lax.broadcasted_iota(jnp.int32, (m, w), 0)
+            upd = low
+            for t in range(GROUP):
+                upd = upd - coefs[t] * vs[t]
+            low = jnp.where(sub >= GROUP, upd, low)
+            for t in range(GROUP):
+                low = jnp.where(sub == t, vs[t], low)
+            pan = jnp.concatenate([top, low], axis=0) if r else low
         sub = lax.broadcasted_iota(jnp.int32, pan.shape, 0) + base
         lane = lax.broadcasted_iota(jnp.int32, pan.shape, 1)
         pan = jnp.where((lane < k) & (lane < sub), 0.0, pan)

time: 49.9 us -> 45.3 us (0.908)
  Pallas kernels: 12.6 us -> 7.99 us
    pallas_call x1, Pallas kernels: 12.6 us -> 7.99 us  [cholesky_and_inverse(): pl.pallas_call(functools.partial(_chol_kernel, panel=panel), out_shape=(o...]
where the time goes in v6:
time: 45.3 us; the launch traced here: 45 us
  waiting for transfers between devices  11.3 us (25%)
  starting transfers between devices  10 us (22%)
  matrix products  8.75 us (19%)
  Pallas kernels  7.99 us (18%)
  local copies, waits for them, and re-layouts  2.94 us (6%)
  other arithmetic  2.22 us (5%)
  between operations  1.7 us (4%)
    pallas_call x1, Pallas kernels, cholesky_and_inverse(): pl.pallas_call(functools.partial(_chol_kernel, panel=panel), out_shape=(o...  7.99 us
    ppermute x3, waiting for transfers between devices, all_sum_and_route(): got = lax.ppermute(packet, AXES, perm)  6.38 us
    ppermute x3, starting transfers between devices, all_sum_and_route(): got = lax.ppermute(packet, AXES, perm)  5.11 us
    ppermute x2, waiting for transfers between devices, all_sum_and_route(): x = x + lax.ppermute(x, AXES, perm)  4.96 us
    ppermute x2, starting transfers between devices, all_sum_and_route(): x = x + lax.ppermute(x, AXES, perm)  4.91 us
    dot_general x1, matrix products, per_device(): jnp.dot(sketch_stat.astype(jnp.float32), inverse.T, precision=HIGHEST)  3.09 us
    dot_general x2, matrix products, sketch_block(): jnp.dot(block, omega, preferred_element_type=jnp.float32)  3.02 us
    dot_general x1, matrix products, per_device(): jnp.dot(arrived.astype(jnp.float32), inverse.T, precision=HIGHEST)  1.78 us
  transfers between devices with their start and end apart: 5, of which 5 were waited for; matrix products, arithmetic and copies ran while one was open for 2% of the time, Pallas kernels for 0%

profile of v6, /device:TPU:0, one launch (start us, length us, event | category | flops | bytes accessed | tf_op | source)
XLA Modules:
  0.0 45.0 jit_solution(7323679490949039770)
XLA Ops:
  1.5 1.1 %convolution_convert_fusion.4 = bf16[32,192]{1,0:T(8,128)(2,1)S(1)} fusion(bf16[32,512]{1,0:T(8,128)(2,1)} %param.6, bf16[512,192]{0,1:T(8,128)(2,1)} %param.9), kind=kOutput, calls=%fused_computation.6 | convolution fusion | flops 6297600 | bytes 241664 | tf_op jit(solution)/shard_map/dot_general | solution.py:17
  2.6 1.9 %convolution_convert_fusion.1 = bf16[2560,192]{0,1:T(8,128)(2,1)S(1)} fusion(bf16[2560,512]{1,0:T(8,128)(2,1)S(1)} %copy-done, bf16[512,192]{0,1:T(8,128)(2,1)} %param.9), kind=kOutput, calls=%fused_computation.1 | convolution fusion | flops 503808000 | bytes 3801088 | tf_op jit(solution)/shard_map/dot_general | solution.py:17
  4.5 0.9 %copy-done.1 = bf16[2560,192]{0,1:T(8,128)(2,1)} copy-done((bf16[2560,192]{0,1:T(8,128)(2,1)}, bf16[2560,192]{0,1:T(8,128)(2,1)S(1)}, u32[]{:S(2)}) %copy-start.1) | copy-done | bytes 983064
  5.5 0.4 fusion.13
  5.9 0.3 fusion
  6.2 0.2 fusion.12
  6.4 0.1 copy.27
  6.5 0.1 pad_maximum_fusion
  6.6 3.1 %collective-permute-start = (f32[193,96]{0,1:T(8,128)S(1)}, f32[193,96]{0,1:T(8,128)S(1)}, u32[]{:S(2)}, u32[]{:S(2)}) collective-permute-start(f32[193,96]{0,1:T(8,128)S(1)} %pad_maximum_fusion), channel_id=1, source_target_pairs={{0,16},{1,17},{2,18},{3,19},{4,20},{5,21},{6,22},{7,23},{8,24},{9,... | collective-permute-start | bytes 222344 | tf_op jit(solution)/shard_map/ppermute | solution.py:51
  9.8 0.2 select_reduce_fusion.1
  10.0 0.1 convolution_convert_fusion.3
  10.2 2.3 %collective-permute-done = f32[193,96]{0,1:T(8,128)S(1)} collective-permute-done((f32[193,96]{0,1:T(8,128)S(1)}, f32[193,96]{0,1:T(8,128)S(1)}, u32[]{:S(2)}, u32[]{:S(2)}) %collective-permute-start) | collective-permute-done | bytes 74144 | tf_op jit(solution)/shard_map/ppermute | solution.py:51
  12.5 0.1 fusion.25
  12.6 1.9 %collective-permute-start.1 = (f32[193,96]{0,1:T(8,128)S(1)}, f32[193,96]{0,1:T(8,128)S(1)}, u32[]{:S(2)}, u32[]{:S(2)}) collective-permute-start(f32[193,96]{0,1:T(8,128)S(1)} %fusion.25), channel_id=1, source_target_pairs={{0,8},{1,9},{2,10},{3,11},{4,12},{5,13},{6,14},{7,15},{8,0},{9,1},... | collective-permute-start | bytes 222344 | tf_op jit(solution)/shard_map/ppermute | solution.py:51
  14.5 0.1 copy.28
  14.6 2.6 %collective-permute-done.1 = f32[193,96]{0,1:T(8,128)S(1)} collective-permute-done((f32[193,96]{0,1:T(8,128)S(1)}, f32[193,96]{0,1:T(8,128)S(1)}, u32[]{:S(2)}, u32[]{:S(2)}) %collective-permute-start.1) | collective-permute-done | bytes 74144 | tf_op jit(solution)/shard_map/ppermute | solution.py:51
  17.4 3.0 %collective-permute-start.2 = (f32[241,96]{0,1:T(8,128)S(1)}, f32[241,96]{0,1:T(8,128)S(1)}, u32[]{:S(2)}, u32[]{:S(2)}) collective-permute-start(f32[241,96]{0,1:T(8,128)S(1)} %pad_maximum_fusion.1), channel_id=1, source_target_pairs={{0,4},{1,5},{2,6},{3,7},{4,0},{5,1},{6,2},{7,3},{8,12},{9,13},{10,... | collective-permute-start | bytes 277640 | tf_op jit(solution)/shard_map/ppermute | solution.py:58
  20.3 2.6 %collective-permute-done.2 = f32[241,96]{0,1:T(8,128)S(1)} collective-permute-done((f32[241,96]{0,1:T(8,128)S(1)}, f32[241,96]{0,1:T(8,128)S(1)}, u32[]{:S(2)}, u32[]{:S(2)}) %collective-permute-start.2) | collective-permute-done | bytes 92576 | tf_op jit(solution)/shard_map/ppermute | solution.py:58
  23.1 0.1 convert_element_type.94
  23.3 0.1 copy.32
  23.5 2.1 %collective-permute-start.3 = (f32[241,96]{0,1:T(8,128)S(1)}, f32[241,96]{0,1:T(8,128)S(1)}, u32[]{:S(2)}, u32[]{:S(2)}) collective-permute-start(f32[241,96]{0,1:T(8,128)S(1)} %pad_maximum_fusion.2), channel_id=1, source_target_pairs={{0,2},{1,3},{2,0},{3,1},{4,6},{5,7},{6,4},{7,5},{8,10},{9,11},{10,... | collective-permute-start | bytes 277640 | tf_op jit(solution)/shard_map/ppermute | solution.py:58
  25.6 2.6 %collective-permute-done.3 = f32[241,96]{0,1:T(8,128)S(1)} collective-permute-done((f32[241,96]{0,1:T(8,128)S(1)}, f32[241,96]{0,1:T(8,128)S(1)}, u32[]{:S(2)}, u32[]{:S(2)}) %collective-permute-start.3) | collective-permute-done | bytes 92576 | tf_op jit(solution)/shard_map/ppermute | solution.py:58
  28.4 0.1 convert_element_type.97
  29.0 0.1 copy.36
  29.1 1.2 %collective-permute-done.4 = f32[241,96]{0,1:T(8,128)S(1)} collective-permute-done((f32[241,96]{0,1:T(8,128)S(1)}, f32[241,96]{0,1:T(8,128)S(1)}, u32[]{:S(2)}, u32[]{:S(2)}) %collective-permute-start.4) | collective-permute-done | bytes 92576 | tf_op jit(solution)/shard_map/ppermute | solution.py:58
  30.3 0.2 slice_reduce_fusion
  30.7 0.1 convert_element_type.106
  30.8 0.1 broadcast_select_fusion.1
  31.3 0.8 %maximum_maximum_fusion.g_ref = f32[192,192]{1,0:T(8,128)} fusion(f32[96,96]{1,0:T(8,128)S(1)} %get-tuple-element.11, f32[96,96]{1,0:T(8,128)S(1)} %copy.39, f32[96,96]{1,0:T(8,128)S(1)} %get-tuple-element.12, f32[96,96]{1,0:T(8,128)S(1)} %get-tuple-element.10), kind=kLoop, calls=%fused_computation.7 | loop fusion | flops 110592 | bytes 294912 | tf_op jit(solution)/shard_map/concatenate | solution.py:38
  32.1 8.0 %shard_map.76 = (f32[192,192]{1,0:T(8,128)}, f32[192,192]{1,0:T(8,128)}) custom-call(f32[192,192]{1,0:T(8,128)} %maximum_maximum_fusion.g_ref), custom_call_target="tpu_custom_call" | custom-call | tf_op jit(solution)/shard_map/pallas_call | solution.py:132
  40.1 3.1 %convolution_convert_fusion = bf16[2560,192]{0,1:T(8,128)(2,1)} fusion(bf16[2560,192]{0,1:T(8,128)(2,1)} %copy-done.1, f32[192,192]{1,0:T(8,128)} %get-tuple-element.5), kind=kOutput, calls=%fused_computation | convolution fusion | flops 1132953600 | bytes 2113536 | tf_op jit(solution)/shard_map/dot_general | solution.py:178
  43.2 1.8 %convolution_convert_fusion.2 = bf16[48,192]{1,0:T(8,128)(2,1)} fusion(bf16[48,192]{1,0:T(8,128)(2,1)S(1)} %reshape_reshape.12, f32[192,192]{1,0:T(8,128)} %get-tuple-element.5), kind=kOutput, calls=%fused_computation.4 | convolution fusion | flops 21242880 | bytes 184320 | tf_op jit(solution)/shard_map/dot_general | solution.py:181
  (43 shorter events, 2.0 us)
Async XLA Ops:
  0.6 1.9 %copy-start = (bf16[2560,512]{1,0:T(8,128)(2,1)S(1)}, bf16[2560,512]{1,0:T(8,128)(2,1)}, u32[]{:S(2)}) copy-start(bf16[2560,512]{1,0:T(8,128)(2,1)} %param.5) | copy-start | bytes 7864324
  4.5 1.0 %copy-start.1 = (bf16[2560,192]{0,1:T(8,128)(2,1)}, bf16[2560,192]{0,1:T(8,128)(2,1)S(1)}, u32[]{:S(2)}) copy-start(bf16[2560,192]{0,1:T(8,128)(2,1)S(1)} %convolution_convert_fusion.1) | copy-start | bytes 2949124
  5.5 4.2 %copy-start.2 = (s32[32,1]{0,1:T(1,128)S(1)}, s32[32,1]{0,1:T(1,128)}, u32[]{:S(2)}) copy-start(s32[32,1]{0,1:T(1,128)} %param.7) | copy-start | bytes 388
  6.6 5.9 %collective-permute-start = (f32[193,96]{0,1:T(8,128)S(1)}, f32[193,96]{0,1:T(8,128)S(1)}, u32[]{:S(2)}, u32[]{:S(2)}) collective-permute-start(f32[193,96]{0,1:T(8,128)S(1)} %pad_maximum_fusion), channel_id=1, source_target_pairs={{0,16},{1,17},{2,18},{3,19},{4,20},{5,21},{6,22},{7,23},{8,24},{9,... | collective-permute-start | bytes 222344 | tf_op jit(solution)/shard_map/ppermute | solution.py:51
  12.6 4.7 %collective-permute-start.1 = (f32[193,96]{0,1:T(8,128)S(1)}, f32[193,96]{0,1:T(8,128)S(1)}, u32[]{:S(2)}, u32[]{:S(2)}) collective-permute-start(f32[193,96]{0,1:T(8,128)S(1)} %fusion.25), channel_id=1, source_target_pairs={{0,8},{1,9},{2,10},{3,11},{4,12},{5,13},{6,14},{7,15},{8,0},{9,1},... | collective-permute-start | bytes 222344 | tf_op jit(solution)/shard_map/ppermute | solution.py:51
  17.4 5.6 %collective-permute-start.2 = (f32[241,96]{0,1:T(8,128)S(1)}, f32[241,96]{0,1:T(8,128)S(1)}, u32[]{:S(2)}, u32[]{:S(2)}) collective-permute-start(f32[241,96]{0,1:T(8,128)S(1)} %pad_maximum_fusion.1), channel_id=1, source_target_pairs={{0,4},{1,5},{2,6},{3,7},{4,0},{5,1},{6,2},{7,3},{8,12},{9,13},{10,... | collective-permute-start | bytes 277640 | tf_op jit(solution)/shard_map/ppermute | solution.py:58
  23.5 4.7 %collective-permute-start.3 = (f32[241,96]{0,1:T(8,128)S(1)}, f32[241,96]{0,1:T(8,128)S(1)}, u32[]{:S(2)}, u32[]{:S(2)}) collective-permute-start(f32[241,96]{0,1:T(8,128)S(1)} %pad_maximum_fusion.2), channel_id=1, source_target_pairs={{0,2},{1,3},{2,0},{3,1},{4,6},{5,7},{6,4},{7,5},{8,10},{9,11},{10,... | collective-permute-start | bytes 277640 | tf_op jit(solution)/shard_map/ppermute | solution.py:58
  28.9 1.4 %collective-permute-start.4 = (f32[241,96]{0,1:T(8,128)S(1)}, f32[241,96]{0,1:T(8,128)S(1)}, u32[]{:S(2)}, u32[]{:S(2)}) collective-permute-start(f32[241,96]{0,1:T(8,128)S(1)} %pad_maximum_fusion.3), channel_id=1, source_target_pairs={{0,1},{1,0},{2,3},{3,2},{4,5},{5,4},{6,7},{7,6},{8,9},{9,8},{10,11... | collective-permute-start | bytes 277640 | tf_op jit(solution)/shard_map/ppermute | solution.py:58

commit v7 on v6

--- a/solution.py
+++ b/solution.py
@@ -64,7 +64,7 @@
     return x, held
 
 
-def _chol_kernel(g_ref, u_ref, r_ref, b_ref, *, panel):
+def _chol_kernel(g_ref, u_ref, hi_ref, mid_ref, lo_ref, b_ref, *, panel):
     k = g_ref.shape[0]
     w = 2 * k
     kp = ((k + 127) // 128) * 128
@@ -117,7 +117,11 @@
             )
             b_ref[end:, :] = b_ref[end:, :] - upd[end:k]
     u_ref[...] = b_ref[:, :k]
-    r_ref[...] = b_ref[:, k:]
+    rest = b_ref[:, k:]
+    for part in (hi_ref, mid_ref, lo_ref):
+        term = rest.astype(jnp.bfloat16)
+        part[...] = term
+        rest = rest - term.astype(jnp.float32)
 
 
 def cholesky_and_inverse(g):
@@ -126,16 +130,30 @@
     if panel is None:
         lower = jnp.linalg.cholesky(g)
         eye = jnp.eye(k, dtype=jnp.float32)
-        return lower.T, lax.linalg.triangular_solve(lower, eye, left_side=True, lower=True)
+        inverse = lax.linalg.triangular_solve(lower, eye, left_side=True, lower=True)
+        return lower.T, (inverse,)
     vmem = pl.BlockSpec(memory_space=pltpu.VMEM)
-    out = jax.ShapeDtypeStruct((k, k), jnp.float32)
-    return pl.pallas_call(
+    half = jax.ShapeDtypeStruct((k, k), jnp.bfloat16)
+    upper, *parts = pl.pallas_call(
         functools.partial(_chol_kernel, panel=panel),
-        out_shape=(out, out),
+        out_shape=(jax.ShapeDtypeStruct((k, k), jnp.float32), half, half, half),
         in_specs=[vmem],
-        out_specs=(vmem, vmem),
+        out_specs=(vmem, vmem, vmem, vmem),
         scratch_shapes=[pltpu.VMEM((k, 2 * k), jnp.float32)],
     )(g)
+    return upper, tuple(parts)
+
+
+def apply_inverse(y, parts):
+    dims = (((1,), (1,)), ((), ()))
+    out = None
+    for part in parts:
+        if part.dtype == jnp.float32:
+            term = jnp.dot(y.astype(jnp.float32), part.T, precision=HIGHEST)
+        else:
+            term = lax.dot_general(y, part, dims, preferred_element_type=jnp.float32)
+        out = term if out is None else out + term
+    return out.astype(jnp.bfloat16)
 
 
 def per_device(stationary, rotor_rows, owners, counts, omega):
@@ -174,13 +192,9 @@
         packed, arrived = all_sum_and_route(packed, outgoing, n, n_rows)
     arrived = arrived.reshape(n_rows * CAP, -1)
     gram = unpack_sym(packed)
-    upper, inverse = cholesky_and_inverse(gram)
-    basis_stat = jnp.dot(
-        sketch_stat.astype(jnp.float32), inverse.T, precision=HIGHEST
-    ).astype(jnp.bfloat16)
-    basis_rot = jnp.dot(arrived.astype(jnp.float32), inverse.T, precision=HIGHEST).astype(
-        jnp.bfloat16
-    )
+    upper, parts = cholesky_and_inverse(gram)
+    basis_stat = apply_inverse(sketch_stat, parts)
+    basis_rot = apply_inverse(arrived, parts)
     return (basis_stat, basis_rot, upper)
 
 

time: 45.3 us -> 45.7 us (level)
  local copies, waits for them, and re-layouts: 2.94 us -> 3.43 us
    unnamed x6 -> x14, local copies, waits for them, and re-layouts: 0.98 us -> 1.47 us
    dot_general x2 -> x6, matrix products: 4.87 us -> 4.6 us  [apply_inverse(): term = lax.dot_general(y, part, dims, preferred_element_type=jnp.float32)]
where the time goes in v7:
time: 45.7 us; the launch traced here: 45.3 us
  waiting for transfers between devices  11.3 us (25%)
  starting transfers between devices  10 us (22%)
  matrix products  8.48 us (19%)
  Pallas kernels  8.05 us (18%)
  local copies, waits for them, and re-layouts  3.43 us (8%)
  other arithmetic  2.22 us (5%)
  between operations  1.76 us (4%)
    pallas_call x1, Pallas kernels, cholesky_and_inverse(): pl.pallas_call(functools.partial(_chol_kernel, panel=panel), out_shape=(j...  8.05 us
    ppermute x3, waiting for transfers between devices, all_sum_and_route(): got = lax.ppermute(packet, AXES, perm)  6.38 us
    ppermute x3, starting transfers between devices, all_sum_and_route(): got = lax.ppermute(packet, AXES, perm)  5.11 us
    ppermute x2, waiting for transfers between devices, all_sum_and_route(): x = x + lax.ppermute(x, AXES, perm)  4.96 us
    ppermute x2, starting transfers between devices, all_sum_and_route(): x = x + lax.ppermute(x, AXES, perm)  4.91 us
    dot_general x6, matrix products, apply_inverse(): term = lax.dot_general(y, part, dims, preferred_element_type=jnp.float32)  4.6 us
    dot_general x2, matrix products, sketch_block(): jnp.dot(block, omega, preferred_element_type=jnp.float32)  3.02 us
    unnamed x14, local copies, waits for them, and re-layouts  1.47 us
  transfers between devices with their start and end apart: 5, of which 5 were waited for; matrix products, arithmetic and copies ran while one was open for 2% of the time, Pallas kernels for 0%

profile of v7, /device:TPU:0, one launch (start us, length us, event | category | flops | bytes accessed | tf_op | source)
XLA Modules:
  0.0 45.3 jit_solution(7716717599489366934)
XLA Ops:
  1.5 1.1 %convolution_convert_fusion.2 = bf16[32,192]{1,0:T(8,128)(2,1)S(1)} fusion(bf16[32,512]{1,0:T(8,128)(2,1)} %param.6, bf16[512,192]{0,1:T(8,128)(2,1)} %param.9), kind=kOutput, calls=%fused_computation.10 | convolution fusion | flops 6297600 | bytes 241664 | tf_op jit(solution)/shard_map/dot_general | solution.py:17
  2.6 1.9 %convolution_convert_fusion = bf16[2560,192]{0,1:T(8,128)(2,1)S(1)} fusion(bf16[2560,512]{1,0:T(8,128)(2,1)S(1)} %copy-done, bf16[512,192]{0,1:T(8,128)(2,1)} %param.9), kind=kOutput, calls=%fused_computation.3 | convolution fusion | flops 503808000 | bytes 3801088 | tf_op jit(solution)/shard_map/dot_general | solution.py:17
  4.5 0.9 %copy-done.1 = bf16[2560,192]{0,1:T(8,128)(2,1)} copy-done((bf16[2560,192]{0,1:T(8,128)(2,1)}, bf16[2560,192]{0,1:T(8,128)(2,1)S(1)}, u32[]{:S(2)}) %copy-start.1) | copy-done | bytes 983064
  5.5 0.4 fusion.15
  5.9 0.3 fusion.1
  6.2 0.2 fusion.14
  6.4 0.1 copy.27
  6.5 0.1 pad_maximum_fusion
  6.6 3.1 %collective-permute-start = (f32[193,96]{0,1:T(8,128)S(1)}, f32[193,96]{0,1:T(8,128)S(1)}, u32[]{:S(2)}, u32[]{:S(2)}) collective-permute-start(f32[193,96]{0,1:T(8,128)S(1)} %pad_maximum_fusion), channel_id=1, source_target_pairs={{0,16},{1,17},{2,18},{3,19},{4,20},{5,21},{6,22},{7,23},{8,24},{9,... | collective-permute-start | bytes 222344 | tf_op jit(solution)/shard_map/ppermute | solution.py:51
  9.8 0.2 select_reduce_fusion.1
  10.0 0.1 convolution_convert_fusion.1
  10.2 2.3 %collective-permute-done = f32[193,96]{0,1:T(8,128)S(1)} collective-permute-done((f32[193,96]{0,1:T(8,128)S(1)}, f32[193,96]{0,1:T(8,128)S(1)}, u32[]{:S(2)}, u32[]{:S(2)}) %collective-permute-start) | collective-permute-done | bytes 74144 | tf_op jit(solution)/shard_map/ppermute | solution.py:51
  12.5 0.1 fusion.37
  12.6 1.9 %collective-permute-start.1 = (f32[193,96]{0,1:T(8,128)S(1)}, f32[193,96]{0,1:T(8,128)S(1)}, u32[]{:S(2)}, u32[]{:S(2)}) collective-permute-start(f32[193,96]{0,1:T(8,128)S(1)} %fusion.37), channel_id=1, source_target_pairs={{0,8},{1,9},{2,10},{3,11},{4,12},{5,13},{6,14},{7,15},{8,0},{9,1},... | collective-permute-start | bytes 222344 | tf_op jit(solution)/shard_map/ppermute | solution.py:51
  14.6 2.6 %collective-permute-done.1 = f32[193,96]{0,1:T(8,128)S(1)} collective-permute-done((f32[193,96]{0,1:T(8,128)S(1)}, f32[193,96]{0,1:T(8,128)S(1)}, u32[]{:S(2)}, u32[]{:S(2)}) %collective-permute-start.1) | collective-permute-done | bytes 74144 | tf_op jit(solution)/shard_map/ppermute | solution.py:51
  17.4 3.0 %collective-permute-start.2 = (f32[241,96]{0,1:T(8,128)S(1)}, f32[241,96]{0,1:T(8,128)S(1)}, u32[]{:S(2)}, u32[]{:S(2)}) collective-permute-start(f32[241,96]{0,1:T(8,128)S(1)} %pad_maximum_fusion.1), channel_id=1, source_target_pairs={{0,4},{1,5},{2,6},{3,7},{4,0},{5,1},{6,2},{7,3},{8,12},{9,13},{10,... | collective-permute-start | bytes 277640 | tf_op jit(solution)/shard_map/ppermute | solution.py:58
  20.3 2.6 %collective-permute-done.2 = f32[241,96]{0,1:T(8,128)S(1)} collective-permute-done((f32[241,96]{0,1:T(8,128)S(1)}, f32[241,96]{0,1:T(8,128)S(1)}, u32[]{:S(2)}, u32[]{:S(2)}) %collective-permute-start.2) | collective-permute-done | bytes 92576 | tf_op jit(solution)/shard_map/ppermute | solution.py:58
  23.5 2.1 %collective-permute-start.3 = (f32[241,96]{0,1:T(8,128)S(1)}, f32[241,96]{0,1:T(8,128)S(1)}, u32[]{:S(2)}, u32[]{:S(2)}) collective-permute-start(f32[241,96]{0,1:T(8,128)S(1)} %pad_maximum_fusion.2), channel_id=1, source_target_pairs={{0,2},{1,3},{2,0},{3,1},{4,6},{5,7},{6,4},{7,5},{8,10},{9,11},{10,... | collective-permute-start | bytes 277640 | tf_op jit(solution)/shard_map/ppermute | solution.py:58
  25.6 2.6 %collective-permute-done.3 = f32[241,96]{0,1:T(8,128)S(1)} collective-permute-done((f32[241,96]{0,1:T(8,128)S(1)}, f32[241,96]{0,1:T(8,128)S(1)}, u32[]{:S(2)}, u32[]{:S(2)}) %collective-permute-start.3) | collective-permute-done | bytes 92576 | tf_op jit(solution)/shard_map/ppermute | solution.py:58
  29.0 0.1 copy.36
  29.1 1.2 %collective-permute-done.4 = f32[241,96]{0,1:T(8,128)S(1)} collective-permute-done((f32[241,96]{0,1:T(8,128)S(1)}, f32[241,96]{0,1:T(8,128)S(1)}, u32[]{:S(2)}, u32[]{:S(2)}) %collective-permute-start.4) | collective-permute-done | bytes 92576 | tf_op jit(solution)/shard_map/ppermute | solution.py:58
  30.3 0.2 slice_reduce_fusion
  30.7 0.1 convert_element_type.104
  31.3 0.8 %maximum_maximum_fusion.g_ref = f32[192,192]{1,0:T(8,128)} fusion(f32[96,96]{1,0:T(8,128)S(1)} %get-tuple-element.15, f32[96,96]{1,0:T(8,128)S(1)} %copy.39, f32[96,96]{1,0:T(8,128)S(1)} %get-tuple-element.16, f32[96,96]{1,0:T(8,128)S(1)} %get-tuple-element.14), kind=kLoop, calls=%fused_computation.11 | loop fusion | flops 110592 | bytes 294912 | tf_op jit(solution)/shard_map/concatenate | solution.py:38
  32.1 8.1 %shard_map.76 = (f32[192,192]{1,0:T(8,128)}, bf16[192,192]{1,0:T(8,128)(2,1)}, bf16[192,192]{1,0:T(8,128)(2,1)}, bf16[192,192]{1,0:T(8,128)(2,1)}) custom-call(f32[192,192]{1,0:T(8,128)} %maximum_maximum_fusion.g_ref), custom_call_target="tpu_custom_call" | custom-call | tf_op jit(solution)/shard_map/pallas_call | solution.py:137
  40.2 1.7 %fusion.17 = f32[2560,192]{0,1:T(8,128)S(1)} fusion(bf16[192,192]{1,0:T(8,128)(2,1)} %get-tuple-element.7, bf16[2560,192]{0,1:T(8,128)(2,1)} %copy-done.1), kind=kOutput, calls=%fused_computation.68 | convolution fusion | flops 188743680 | bytes 3022848 | tf_op jit(solution)/shard_map/dot_general | solution.py:154
  41.9 0.1 fusion.16
  42.1 0.2 convolution_add_fusion.4
  42.3 0.4 convolution_add_fusion.1
  42.7 0.5 %copy-done.5 = bf16[192,192]{1,0:T(8,128)(2,1)S(1)} copy-done((bf16[192,192]{1,0:T(8,128)(2,1)S(1)}, bf16[192,192]{1,0:T(8,128)(2,1)}, u32[]{:S(2)}) %copy-start.5) | copy-done | bytes 73752
  43.2 0.8 %fusion.2 = bf16[48,192]{1,0:T(8,128)(2,1)} fusion(f32[48,192]{1,0:T(8,128)S(1)} %convolution_add_fusion.4, bf16[48,192]{1,0:T(8,128)(2,1)S(1)} %reshape_reshape.12, bf16[192,192]{1,0:T(8,128)(2,1)S(1)} %copy-done.5), kind=kOutput, calls=%fused_computation.8 | convolution fusion | flops 3557376 | bytes 147456 | tf_op jit(solution)/shard_map/dot_general | solution.py:154
  43.9 1.4 %fusion = bf16[2560,192]{0,1:T(8,128)(2,1)} fusion(f32[2560,192]{0,1:T(8,128)S(1)} %convolution_add_fusion.1, bf16[192,192]{1,0:T(8,128)(2,1)S(1)} %copy-done.5, bf16[2560,192]{0,1:T(8,128)(2,1)S(1)} %copy-done.2), kind=kOutput, calls=%fused_computation.2 | convolution fusion | flops 189726720 | bytes 4005888 | tf_op jit(solution)/shard_map/dot_general | solution.py:154
  (55 shorter events, 2.5 us)
Async XLA Ops:
  0.6 1.9 %copy-start = (bf16[2560,512]{1,0:T(8,128)(2,1)S(1)}, bf16[2560,512]{1,0:T(8,128)(2,1)}, u32[]{:S(2)}) copy-start(bf16[2560,512]{1,0:T(8,128)(2,1)} %param.5) | copy-start | bytes 7864324
  4.5 0.9 %copy-start.1 = (bf16[2560,192]{0,1:T(8,128)(2,1)}, bf16[2560,192]{0,1:T(8,128)(2,1)S(1)}, u32[]{:S(2)}) copy-start(bf16[2560,192]{0,1:T(8,128)(2,1)S(1)} %convolution_convert_fusion) | copy-start | bytes 2949124
  5.5 4.2 %copy-start.6 = (s32[32,1]{0,1:T(1,128)S(1)}, s32[32,1]{0,1:T(1,128)}, u32[]{:S(2)}) copy-start(s32[32,1]{0,1:T(1,128)} %param.7) | copy-start | bytes 388
  6.6 5.9 %collective-permute-start = (f32[193,96]{0,1:T(8,128)S(1)}, f32[193,96]{0,1:T(8,128)S(1)}, u32[]{:S(2)}, u32[]{:S(2)}) collective-permute-start(f32[193,96]{0,1:T(8,128)S(1)} %pad_maximum_fusion), channel_id=1, source_target_pairs={{0,16},{1,17},{2,18},{3,19},{4,20},{5,21},{6,22},{7,23},{8,24},{9,... | collective-permute-start | bytes 222344 | tf_op jit(solution)/shard_map/ppermute | solution.py:51
  12.6 4.7 %collective-permute-start.1 = (f32[193,96]{0,1:T(8,128)S(1)}, f32[193,96]{0,1:T(8,128)S(1)}, u32[]{:S(2)}, u32[]{:S(2)}) collective-permute-start(f32[193,96]{0,1:T(8,128)S(1)} %fusion.37), channel_id=1, source_target_pairs={{0,8},{1,9},{2,10},{3,11},{4,12},{5,13},{6,14},{7,15},{8,0},{9,1},... | collective-permute-start | bytes 222344 | tf_op jit(solution)/shard_map/ppermute | solution.py:51
  17.4 5.6 %collective-permute-start.2 = (f32[241,96]{0,1:T(8,128)S(1)}, f32[241,96]{0,1:T(8,128)S(1)}, u32[]{:S(2)}, u32[]{:S(2)}) collective-permute-start(f32[241,96]{0,1:T(8,128)S(1)} %pad_maximum_fusion.1), channel_id=1, source_target_pairs={{0,4},{1,5},{2,6},{3,7},{4,0},{5,1},{6,2},{7,3},{8,12},{9,13},{10,... | collective-permute-start | bytes 277640 | tf_op jit(solution)/shard_map/ppermute | solution.py:58
  23.5 4.7 %collective-permute-start.3 = (f32[241,96]{0,1:T(8,128)S(1)}, f32[241,96]{0,1:T(8,128)S(1)}, u32[]{:S(2)}, u32[]{:S(2)}) collective-permute-start(f32[241,96]{0,1:T(8,128)S(1)} %pad_maximum_fusion.2), channel_id=1, source_target_pairs={{0,2},{1,3},{2,0},{3,1},{4,6},{5,7},{6,4},{7,5},{8,10},{9,11},{10,... | collective-permute-start | bytes 277640 | tf_op jit(solution)/shard_map/ppermute | solution.py:58
  28.9 1.4 %collective-permute-start.4 = (f32[241,96]{0,1:T(8,128)S(1)}, f32[241,96]{0,1:T(8,128)S(1)}, u32[]{:S(2)}, u32[]{:S(2)}) collective-permute-start(f32[241,96]{0,1:T(8,128)S(1)} %pad_maximum_fusion.3), channel_id=1, source_target_pairs={{0,1},{1,0},{2,3},{3,2},{4,5},{5,4},{6,7},{7,6},{8,9},{9,8},{10,11... | collective-permute-start | bytes 277640 | tf_op jit(solution)/shard_map/ppermute | solution.py:58
  40.2 1.8 %copy-start.3 = (bf16[192,192]{1,0:T(8,128)(2,1)S(1)}, bf16[192,192]{1,0:T(8,128)(2,1)}, u32[]{:S(2)}) copy-start(bf16[192,192]{1,0:T(8,128)(2,1)} %get-tuple-element.7) | copy-start | bytes 221188
  40.2 1.9 %copy-start.4 = (bf16[192,192]{1,0:T(8,128)(2,1)S(1)}, bf16[192,192]{1,0:T(8,128)(2,1)}, u32[]{:S(2)}) copy-start(bf16[192,192]{1,0:T(8,128)(2,1)} %get-tuple-element.8) | copy-start | bytes 221188
  40.2 2.1 %copy-start.2 = (bf16[2560,192]{0,1:T(8,128)(2,1)S(1)}, bf16[2560,192]{0,1:T(8,128)(2,1)}, u32[]{:S(2)}) copy-start(bf16[2560,192]{0,1:T(8,128)(2,1)} %copy-done.1) | copy-start | bytes 2949124
  42.3 0.9 %copy-start.5 = (bf16[192,192]{1,0:T(8,128)(2,1)S(1)}, bf16[192,192]{1,0:T(8,128)(2,1)}, u32[]{:S(2)}) copy-start(bf16[192,192]{1,0:T(8,128)(2,1)} %get-tuple-element.9) | copy-start | bytes 221188

commit v8 on v6

--- a/solution.py
+++ b/solution.py
@@ -64,7 +64,7 @@
     return x, held
 
 
-def _chol_kernel(g_ref, u_ref, r_ref, b_ref, *, panel):
+def _chol_kernel(g_ref, ys_ref, yr_ref, u_ref, bs_ref, br_ref, b_ref, *, panel):
     k = g_ref.shape[0]
     w = 2 * k
     kp = ((k + 127) // 128) * 128
@@ -117,25 +117,49 @@
             )
             b_ref[end:, :] = b_ref[end:, :] - upd[end:k]
     u_ref[...] = b_ref[:, :k]
-    r_ref[...] = b_ref[:, k:]
-
-
-def cholesky_and_inverse(g):
+    rest = b_ref[:, k:]
+    parts = []
+    for _ in range(3):
+        term = rest.astype(jnp.bfloat16)
+        parts.append(term)
+        rest = rest - term.astype(jnp.float32)
+    dims = (((1,), (1,)), ((), ()))
+    for y_ref, o_ref in ((ys_ref, bs_ref), (yr_ref, br_ref)):
+        n = y_ref.shape[0]
+        step = 512 if n % 512 == 0 else n
+        for i in range(0, n, step):
+            y = y_ref[i : i + step, :]
+            acc = None
+            for part in parts:
+                t = lax.dot_general(y, part, dims, preferred_element_type=jnp.float32)
+                acc = t if acc is None else acc + t
+            o_ref[i : i + step, :] = acc.astype(o_ref.dtype)
+
+
+def factor_and_basis(g, y_stat, y_rot):
     k = g.shape[0]
     panel = next((p for p in (96, 64, 48, 32, 16, 8) if k % p == 0), None)
     if panel is None:
         lower = jnp.linalg.cholesky(g)
         eye = jnp.eye(k, dtype=jnp.float32)
-        return lower.T, lax.linalg.triangular_solve(lower, eye, left_side=True, lower=True)
+        inverse = lax.linalg.triangular_solve(lower, eye, left_side=True, lower=True)
+        basis = [
+            jnp.dot(y.astype(jnp.float32), inverse.T, precision=HIGHEST).astype(jnp.bfloat16)
+            for y in (y_stat, y_rot)
+        ]
+        return lower.T, basis[0], basis[1]
     vmem = pl.BlockSpec(memory_space=pltpu.VMEM)
-    out = jax.ShapeDtypeStruct((k, k), jnp.float32)
     return pl.pallas_call(
         functools.partial(_chol_kernel, panel=panel),
-        out_shape=(out, out),
-        in_specs=[vmem],
-        out_specs=(vmem, vmem),
+        out_shape=(
+            jax.ShapeDtypeStruct((k, k), jnp.float32),
+            jax.ShapeDtypeStruct(y_stat.shape, jnp.bfloat16),
+            jax.ShapeDtypeStruct(y_rot.shape, jnp.bfloat16),
+        ),
+        in_specs=[vmem, vmem, vmem],
+        out_specs=(vmem, vmem, vmem),
         scratch_shapes=[pltpu.VMEM((k, 2 * k), jnp.float32)],
-    )(g)
+    )(g, y_stat, y_rot)
 
 
 def per_device(stationary, rotor_rows, owners, counts, omega):
@@ -174,13 +198,7 @@
         packed, arrived = all_sum_and_route(packed, outgoing, n, n_rows)
     arrived = arrived.reshape(n_rows * CAP, -1)
     gram = unpack_sym(packed)
-    upper, inverse = cholesky_and_inverse(gram)
-    basis_stat = jnp.dot(
-        sketch_stat.astype(jnp.float32), inverse.T, precision=HIGHEST
-    ).astype(jnp.bfloat16)
-    basis_rot = jnp.dot(arrived.astype(jnp.float32), inverse.T, precision=HIGHEST).astype(
-        jnp.bfloat16
-    )
+    upper, basis_stat, basis_rot = factor_and_basis(gram, sketch_stat, arrived)
     return (basis_stat, basis_rot, upper)
 
 

time: 45.3 us -> 44.7 us (0.987)
  matrix products: 8.75 us -> 3.91 us
  local copies, waits for them, and re-layouts: 2.94 us -> 5.05 us
  Pallas kernels: 7.99 us -> 10.1 us
    dot_general x2 -> x0, matrix products: 4.87 us -> none  [the longest x1 3.09 us: per_device(): jnp.dot(sketch_stat.astype(jnp.float32), inverse.T, precision=HIGHEST)]
    pallas_call x1, Pallas kernels: 7.99 us -> 10.1 us  [factor_and_basis(): pl.pallas_call(functools.partial(_chol_kernel, panel=panel), out_shape=(j...]
    unnamed x6 -> x7, local copies, waits for them, and re-layouts: 0.98 us -> 2.49 us
    another operation x1, local copies, waits for them, and re-layouts: 0.02 us -> 0.63 us  [per_device(): arrived = arrived.reshape(n_rows * CAP, -1)]
where the time goes in v8:
time: 44.7 us; the launch traced here: 44.3 us
  waiting for transfers between devices  11.3 us (25%)
  Pallas kernels  10.1 us (23%)
  starting transfers between devices  10 us (22%)
  local copies, waits for them, and re-layouts  5.05 us (11%)
  matrix products  3.91 us (9%)
  other arithmetic  2.22 us (5%)
  between operations  1.7 us (4%)
    pallas_call x1, Pallas kernels, factor_and_basis(): pl.pallas_call(functools.partial(_chol_kernel, panel=panel), out_shape=(j...  10.1 us
    ppermute x3, waiting for transfers between devices, all_sum_and_route(): got = lax.ppermute(packet, AXES, perm)  6.38 us
    ppermute x3, starting transfers between devices, all_sum_and_route(): got = lax.ppermute(packet, AXES, perm)  5.11 us
    ppermute x2, waiting for transfers between devices, all_sum_and_route(): x = x + lax.ppermute(x, AXES, perm)  4.95 us
    ppermute x2, starting transfers between devices, all_sum_and_route(): x = x + lax.ppermute(x, AXES, perm)  4.93 us
    dot_general x2, matrix products, sketch_block(): jnp.dot(block, omega, preferred_element_type=jnp.float32)  2.87 us
    unnamed x7, local copies, waits for them, and re-layouts  2.49 us
  transfers between devices with their start and end apart: 5, of which 5 were waited for; matrix products, arithmetic and copies ran while one was open for 2% of the time, Pallas kernels for 0%

profile of v8, /device:TPU:0, one launch (start us, length us, event | category | flops | bytes accessed | tf_op | source)
XLA Modules:
  0.0 44.3 jit_solution(16784859340455476129)
XLA Ops:
  1.5 1.1 %convolution_convert_fusion.2 = bf16[32,192]{1,0:T(8,128)(2,1)S(1)} fusion(bf16[32,512]{1,0:T(8,128)(2,1)} %param.6, bf16[512,192]{0,1:T(8,128)(2,1)} %param.9), kind=kOutput, calls=%fused_computation.4 | convolution fusion | flops 6297600 | bytes 241664 | tf_op jit(solution)/shard_map/dot_general | solution.py:17
  2.6 1.8 %convolution_convert_fusion.ys_ref = bf16[2560,192]{1,0:T(8,128)(2,1)S(1)} fusion(bf16[2560,512]{1,0:T(8,128)(2,1)S(1)} %copy-done, bf16[512,192]{0,1:T(8,128)(2,1)} %param.9), kind=kOutput, calls=%fused_computation | convolution fusion | flops 503808000 | bytes 3801088 | tf_op jit(solution)/shard_map/dot_general | solution.py:17
  4.4 0.3 fusion.5
  4.7 0.6 %fusion = f32[192,192]{0,1:T(8,128)S(1)} fusion(f32[192,192]{0,1:T(8,128)S(1)} %fusion.5, bf16[2560,192]{1,0:T(8,128)(2,1)S(1)} %convolution_convert_fusion.ys_ref), kind=kOutput, calls=%fused_computation.2 | convolution fusion | flops 188817408 | bytes 1277952 | tf_op jit(solution)/shard_map/dot_general | solution.py:186
  5.3 0.1 copy-done.1
  5.4 0.2 fusion.13
  5.6 0.1 copy.32
  5.7 0.1 pad_maximum_fusion
  5.8 3.1 %collective-permute-start = (f32[193,96]{0,1:T(8,128)S(1)}, f32[193,96]{0,1:T(8,128)S(1)}, u32[]{:S(2)}, u32[]{:S(2)}) collective-permute-start(f32[193,96]{0,1:T(8,128)S(1)} %pad_maximum_fusion), channel_id=1, source_target_pairs={{0,16},{1,17},{2,18},{3,19},{4,20},{5,21},{6,22},{7,23},{8,24},{9,... | collective-permute-start | bytes 222344 | tf_op jit(solution)/shard_map/ppermute | solution.py:51
  9.0 0.2 select_reduce_fusion.1
  9.2 0.1 convolution_convert_fusion.1
  9.4 2.3 %collective-permute-done = f32[193,96]{0,1:T(8,128)S(1)} collective-permute-done((f32[193,96]{0,1:T(8,128)S(1)}, f32[193,96]{0,1:T(8,128)S(1)}, u32[]{:S(2)}, u32[]{:S(2)}) %collective-permute-start) | collective-permute-done | bytes 74144 | tf_op jit(solution)/shard_map/ppermute | solution.py:51
  11.7 0.1 fusion.21
  11.8 1.9 %collective-permute-start.1 = (f32[193,96]{0,1:T(8,128)S(1)}, f32[193,96]{0,1:T(8,128)S(1)}, u32[]{:S(2)}, u32[]{:S(2)}) collective-permute-start(f32[193,96]{0,1:T(8,128)S(1)} %fusion.21), channel_id=1, source_target_pairs={{0,8},{1,9},{2,10},{3,11},{4,12},{5,13},{6,14},{7,15},{8,0},{9,1},... | collective-permute-start | bytes 222344 | tf_op jit(solution)/shard_map/ppermute | solution.py:51
  13.8 0.1 copy.33
  13.9 2.6 %collective-permute-done.1 = f32[193,96]{0,1:T(8,128)S(1)} collective-permute-done((f32[193,96]{0,1:T(8,128)S(1)}, f32[193,96]{0,1:T(8,128)S(1)}, u32[]{:S(2)}, u32[]{:S(2)}) %collective-permute-start.1) | collective-permute-done | bytes 74144 | tf_op jit(solution)/shard_map/ppermute | solution.py:51
  16.6 3.0 %collective-permute-start.2 = (f32[241,96]{0,1:T(8,128)S(1)}, f32[241,96]{0,1:T(8,128)S(1)}, u32[]{:S(2)}, u32[]{:S(2)}) collective-permute-start(f32[241,96]{0,1:T(8,128)S(1)} %pad_maximum_fusion.1), channel_id=1, source_target_pairs={{0,4},{1,5},{2,6},{3,7},{4,0},{5,1},{6,2},{7,3},{8,12},{9,13},{10,... | collective-permute-start | bytes 277640 | tf_op jit(solution)/shard_map/ppermute | solution.py:58
  19.5 2.6 %collective-permute-done.2 = f32[241,96]{0,1:T(8,128)S(1)} collective-permute-done((f32[241,96]{0,1:T(8,128)S(1)}, f32[241,96]{0,1:T(8,128)S(1)}, u32[]{:S(2)}, u32[]{:S(2)}) %collective-permute-start.2) | collective-permute-done | bytes 92576 | tf_op jit(solution)/shard_map/ppermute | solution.py:58
  22.3 0.1 convert_element_type.86
  22.6 0.1 copy.37
  22.7 2.1 %collective-permute-start.3 = (f32[241,96]{0,1:T(8,128)S(1)}, f32[241,96]{0,1:T(8,128)S(1)}, u32[]{:S(2)}, u32[]{:S(2)}) collective-permute-start(f32[241,96]{0,1:T(8,128)S(1)} %pad_maximum_fusion.2), channel_id=1, source_target_pairs={{0,2},{1,3},{2,0},{3,1},{4,6},{5,7},{6,4},{7,5},{8,10},{9,11},{10,... | collective-permute-start | bytes 277640 | tf_op jit(solution)/shard_map/ppermute | solution.py:58
  24.8 2.6 %collective-permute-done.3 = f32[241,96]{0,1:T(8,128)S(1)} collective-permute-done((f32[241,96]{0,1:T(8,128)S(1)}, f32[241,96]{0,1:T(8,128)S(1)}, u32[]{:S(2)}, u32[]{:S(2)}) %collective-permute-start.3) | collective-permute-done | bytes 92576 | tf_op jit(solution)/shard_map/ppermute | solution.py:58
  27.6 0.1 convert_element_type.89
  28.2 0.1 copy.41
  28.3 1.2 %collective-permute-done.4 = f32[241,96]{0,1:T(8,128)S(1)} collective-permute-done((f32[241,96]{0,1:T(8,128)S(1)}, f32[241,96]{0,1:T(8,128)S(1)}, u32[]{:S(2)}, u32[]{:S(2)}) %collective-permute-start.4) | collective-permute-done | bytes 92576 | tf_op jit(solution)/shard_map/ppermute | solution.py:58
  29.5 0.2 slice_reduce_fusion
  29.9 0.1 convert_element_type.96
  30.0 0.1 broadcast_select_fusion.1
  30.2 0.6 %reshape_reshape.12.yr_ref = bf16[48,192]{1,0:T(8,128)(2,1)} reshape(bf16[4,2,1,6,192]{4,3,1,0,2:T(8,128)(2,1)S(1)} %copy.48) | data formatting | bytes 36864 | tf_op jit(solution)/shard_map/reshape;reshape | solution.py:199
  31.1 0.8 %maximum_maximum_fusion.g_ref = f32[192,192]{1,0:T(8,128)} fusion(f32[96,96]{1,0:T(8,128)S(1)} %get-tuple-element.22, f32[96,96]{1,0:T(8,128)S(1)} %copy.44, f32[96,96]{1,0:T(8,128)S(1)} %get-tuple-element.23, f32[96,96]{1,0:T(8,128)S(1)} %get-tuple-element.21), kind=kLoop, calls=%fused_computation.5 | loop fusion | flops 110592 | bytes 294912 | tf_op jit(solution)/shard_map/concatenate | solution.py:38
  31.9 10.1 %shard_map.76 = (f32[192,192]{1,0:T(8,128)}, bf16[2560,192]{1,0:T(8,128)(2,1)}, bf16[48,192]{1,0:T(8,128)(2,1)}) custom-call(f32[192,192]{1,0:T(8,128)} %maximum_maximum_fusion.g_ref, bf16[2560,192]{1,0:T(8,128)(2,1)} %copy-done.1, bf16[48,192]{1,0:T(8,128)(2,1)} %reshape_reshape.12.yr_ref), custom_call_target="tpu_custom_call" | custom-call | tf_op jit(solution)/shard_map/pallas_call | solution.py:152
  42.0 2.3 %copy.49 = bf16[2560,192]{0,1:T(8,128)(2,1)} copy(bf16[2560,192]{1,0:T(8,128)(2,1)} %get-tuple-element.15) | data formatting | bytes 1966080
  (42 shorter events, 2.0 us)
Async XLA Ops:
  0.6 1.9 %copy-start = (bf16[2560,512]{1,0:T(8,128)(2,1)S(1)}, bf16[2560,512]{1,0:T(8,128)(2,1)}, u32[]{:S(2)}) copy-start(bf16[2560,512]{1,0:T(8,128)(2,1)} %param.5) | copy-start | bytes 7864324
  4.4 1.1 %copy-start.1 = (bf16[2560,192]{1,0:T(8,128)(2,1)}, bf16[2560,192]{1,0:T(8,128)(2,1)S(1)}, u32[]{:S(2)}) copy-start(bf16[2560,192]{1,0:T(8,128)(2,1)S(1)} %convolution_convert_fusion.ys_ref) | copy-start | bytes 2949124
  4.7 4.2 %copy-start.2 = (s32[32,1]{0,1:T(1,128)S(1)}, s32[32,1]{0,1:T(1,128)}, u32[]{:S(2)}) copy-start(s32[32,1]{0,1:T(1,128)} %param.7) | copy-start | bytes 388
  5.8 5.9 %collective-permute-start = (f32[193,96]{0,1:T(8,128)S(1)}, f32[193,96]{0,1:T(8,128)S(1)}, u32[]{:S(2)}, u32[]{:S(2)}) collective-permute-start(f32[193,96]{0,1:T(8,128)S(1)} %pad_maximum_fusion), channel_id=1, source_target_pairs={{0,16},{1,17},{2,18},{3,19},{4,20},{5,21},{6,22},{7,23},{8,24},{9,... | collective-permute-start | bytes 222344 | tf_op jit(solution)/shard_map/ppermute | solution.py:51
  11.8 4.7 %collective-permute-start.1 = (f32[193,96]{0,1:T(8,128)S(1)}, f32[193,96]{0,1:T(8,128)S(1)}, u32[]{:S(2)}, u32[]{:S(2)}) collective-permute-start(f32[193,96]{0,1:T(8,128)S(1)} %fusion.21), channel_id=1, source_target_pairs={{0,8},{1,9},{2,10},{3,11},{4,12},{5,13},{6,14},{7,15},{8,0},{9,1},... | collective-permute-start | bytes 222344 | tf_op jit(solution)/shard_map/ppermute | solution.py:51
  16.6 5.6 %collective-permute-start.2 = (f32[241,96]{0,1:T(8,128)S(1)}, f32[241,96]{0,1:T(8,128)S(1)}, u32[]{:S(2)}, u32[]{:S(2)}) collective-permute-start(f32[241,96]{0,1:T(8,128)S(1)} %pad_maximum_fusion.1), channel_id=1, source_target_pairs={{0,4},{1,5},{2,6},{3,7},{4,0},{5,1},{6,2},{7,3},{8,12},{9,13},{10,... | collective-permute-start | bytes 277640 | tf_op jit(solution)/shard_map/ppermute | solution.py:58
  22.7 4.7 %collective-permute-start.3 = (f32[241,96]{0,1:T(8,128)S(1)}, f32[241,96]{0,1:T(8,128)S(1)}, u32[]{:S(2)}, u32[]{:S(2)}) collective-permute-start(f32[241,96]{0,1:T(8,128)S(1)} %pad_maximum_fusion.2), channel_id=1, source_target_pairs={{0,2},{1,3},{2,0},{3,1},{4,6},{5,7},{6,4},{7,5},{8,10},{9,11},{10,... | collective-permute-start | bytes 277640 | tf_op jit(solution)/shard_map/ppermute | solution.py:58
  28.1 1.4 %collective-permute-start.4 = (f32[241,96]{0,1:T(8,128)S(1)}, f32[241,96]{0,1:T(8,128)S(1)}, u32[]{:S(2)}, u32[]{:S(2)}) collective-permute-start(f32[241,96]{0,1:T(8,128)S(1)} %pad_maximum_fusion.3), channel_id=1, source_target_pairs={{0,1},{1,0},{2,3},{3,2},{4,5},{5,4},{6,7},{7,6},{8,9},{9,8},{10,11... | collective-permute-start | bytes 277640 | tf_op jit(solution)/shard_map/ppermute | solution.py:58

commit v9 on v8

--- a/solution.py
+++ b/solution.py
@@ -124,16 +124,20 @@
         parts.append(term)
         rest = rest - term.astype(jnp.float32)
     dims = (((1,), (1,)), ((), ()))
-    for y_ref, o_ref in ((ys_ref, bs_ref), (yr_ref, br_ref)):
+    for y_ref, o_ref, flip in ((ys_ref, bs_ref, True), (yr_ref, br_ref, False)):
         n = y_ref.shape[0]
         step = 512 if n % 512 == 0 else n
         for i in range(0, n, step):
             y = y_ref[i : i + step, :]
             acc = None
             for part in parts:
-                t = lax.dot_general(y, part, dims, preferred_element_type=jnp.float32)
+                pair = (part, y) if flip else (y, part)
+                t = lax.dot_general(*pair, dims, preferred_element_type=jnp.float32)
                 acc = t if acc is None else acc + t
-            o_ref[i : i + step, :] = acc.astype(o_ref.dtype)
+            if flip:
+                o_ref[:, i : i + step] = acc.astype(o_ref.dtype)
+            else:
+                o_ref[i : i + step, :] = acc.astype(o_ref.dtype)
 
 
 def factor_and_basis(g, y_stat, y_rot):
@@ -149,17 +153,18 @@
         ]
         return lower.T, basis[0], basis[1]
     vmem = pl.BlockSpec(memory_space=pltpu.VMEM)
-    return pl.pallas_call(
+    upper, basis_stat_t, basis_rot = pl.pallas_call(
         functools.partial(_chol_kernel, panel=panel),
         out_shape=(
             jax.ShapeDtypeStruct((k, k), jnp.float32),
-            jax.ShapeDtypeStruct(y_stat.shape, jnp.bfloat16),
+            jax.ShapeDtypeStruct(y_stat.shape[::-1], jnp.bfloat16),
             jax.ShapeDtypeStruct(y_rot.shape, jnp.bfloat16),
         ),
         in_specs=[vmem, vmem, vmem],
         out_specs=(vmem, vmem, vmem),
         scratch_shapes=[pltpu.VMEM((k, 2 * k), jnp.float32)],
     )(g, y_stat, y_rot)
+    return upper, basis_stat_t.T, basis_rot
 
 
 def per_device(stationary, rotor_rows, owners, counts, omega):

time: 44.7 us -> 42.3 us (0.946)
  local copies, waits for them, and re-layouts: 5.05 us -> 2.73 us
    unnamed x7 -> x6, local copies, waits for them, and re-layouts: 2.49 us -> 0.16 us
where the time goes in v9:
time: 42.3 us; the launch traced here: 42 us
  waiting for transfers between devices  11.3 us (27%)
  Pallas kernels  10.1 us (24%)
  starting transfers between devices  10 us (24%)
  matrix products  3.91 us (9%)
  local copies, waits for them, and re-layouts  2.73 us (6%)
  other arithmetic  2.24 us (5%)
  between operations  1.7 us (4%)
    pallas_call x1, Pallas kernels, factor_and_basis(): pl.pallas_call(functools.partial(_chol_kernel, panel=panel), out_shape=(j...  10.1 us
    ppermute x3, waiting for transfers between devices, all_sum_and_route(): got = lax.ppermute(packet, AXES, perm)  6.38 us
    ppermute x3, starting transfers between devices, all_sum_and_route(): got = lax.ppermute(packet, AXES, perm)  5.11 us
    ppermute x2, waiting for transfers between devices, all_sum_and_route(): x = x + lax.ppermute(x, AXES, perm)  4.95 us
    ppermute x2, starting transfers between devices, all_sum_and_route(): x = x + lax.ppermute(x, AXES, perm)  4.93 us
    dot_general x2, matrix products, sketch_block(): jnp.dot(block, omega, preferred_element_type=jnp.float32)  2.87 us
  transfers between devices with their start and end apart: 5, of which 5 were waited for; matrix products, arithmetic and copies ran while one was open for 2% of the time, Pallas kernels for 0%

profile of v9, /device:TPU:0, one launch (start us, length us, event | category | flops | bytes accessed | tf_op | source)
XLA Modules:
  0.0 42.0 jit_solution(12848434040948019994)
XLA Ops:
  1.5 1.1 %convolution_convert_fusion.2 = bf16[32,192]{1,0:T(8,128)(2,1)S(1)} fusion(bf16[32,512]{1,0:T(8,128)(2,1)} %param.6, bf16[512,192]{0,1:T(8,128)(2,1)} %param.9), kind=kOutput, calls=%fused_computation.4 | convolution fusion | flops 6297600 | bytes 241664 | tf_op jit(solution)/shard_map/dot_general | solution.py:17
  2.6 1.8 %convolution_convert_fusion.ys_ref = bf16[2560,192]{1,0:T(8,128)(2,1)S(1)} fusion(bf16[2560,512]{1,0:T(8,128)(2,1)S(1)} %copy-done, bf16[512,192]{0,1:T(8,128)(2,1)} %param.9), kind=kOutput, calls=%fused_computation | convolution fusion | flops 503808000 | bytes 3801088 | tf_op jit(solution)/shard_map/dot_general | solution.py:17
  4.4 0.3 fusion.5
  4.7 0.6 %fusion = f32[192,192]{0,1:T(8,128)S(1)} fusion(f32[192,192]{0,1:T(8,128)S(1)} %fusion.5, bf16[2560,192]{1,0:T(8,128)(2,1)S(1)} %convolution_convert_fusion.ys_ref), kind=kOutput, calls=%fused_computation.2 | convolution fusion | flops 188817408 | bytes 1277952 | tf_op jit(solution)/shard_map/dot_general | solution.py:191
  5.3 0.1 copy-done.1
  5.4 0.2 fusion.13
  5.6 0.1 copy.30
  5.7 0.1 pad_maximum_fusion
  5.8 3.1 %collective-permute-start = (f32[193,96]{0,1:T(8,128)S(1)}, f32[193,96]{0,1:T(8,128)S(1)}, u32[]{:S(2)}, u32[]{:S(2)}) collective-permute-start(f32[193,96]{0,1:T(8,128)S(1)} %pad_maximum_fusion), channel_id=1, source_target_pairs={{0,16},{1,17},{2,18},{3,19},{4,20},{5,21},{6,22},{7,23},{8,24},{9,... | collective-permute-start | bytes 222344 | tf_op jit(solution)/shard_map/ppermute | solution.py:51
  9.0 0.2 select_reduce_fusion.1
  9.2 0.1 convolution_convert_fusion.1
  9.4 2.3 %collective-permute-done = f32[193,96]{0,1:T(8,128)S(1)} collective-permute-done((f32[193,96]{0,1:T(8,128)S(1)}, f32[193,96]{0,1:T(8,128)S(1)}, u32[]{:S(2)}, u32[]{:S(2)}) %collective-permute-start) | collective-permute-done | bytes 74144 | tf_op jit(solution)/shard_map/ppermute | solution.py:51
  11.7 0.1 fusion.21
  11.8 1.9 %collective-permute-start.1 = (f32[193,96]{0,1:T(8,128)S(1)}, f32[193,96]{0,1:T(8,128)S(1)}, u32[]{:S(2)}, u32[]{:S(2)}) collective-permute-start(f32[193,96]{0,1:T(8,128)S(1)} %fusion.21), channel_id=1, source_target_pairs={{0,8},{1,9},{2,10},{3,11},{4,12},{5,13},{6,14},{7,15},{8,0},{9,1},... | collective-permute-start | bytes 222344 | tf_op jit(solution)/shard_map/ppermute | solution.py:51
  13.8 0.1 copy.31
  13.9 2.6 %collective-permute-done.1 = f32[193,96]{0,1:T(8,128)S(1)} collective-permute-done((f32[193,96]{0,1:T(8,128)S(1)}, f32[193,96]{0,1:T(8,128)S(1)}, u32[]{:S(2)}, u32[]{:S(2)}) %collective-permute-start.1) | collective-permute-done | bytes 74144 | tf_op jit(solution)/shard_map/ppermute | solution.py:51
  16.6 3.0 %collective-permute-start.2 = (f32[241,96]{0,1:T(8,128)S(1)}, f32[241,96]{0,1:T(8,128)S(1)}, u32[]{:S(2)}, u32[]{:S(2)}) collective-permute-start(f32[241,96]{0,1:T(8,128)S(1)} %pad_maximum_fusion.1), channel_id=1, source_target_pairs={{0,4},{1,5},{2,6},{3,7},{4,0},{5,1},{6,2},{7,3},{8,12},{9,13},{10,... | collective-permute-start | bytes 277640 | tf_op jit(solution)/shard_map/ppermute | solution.py:58
  19.5 2.6 %collective-permute-done.2 = f32[241,96]{0,1:T(8,128)S(1)} collective-permute-done((f32[241,96]{0,1:T(8,128)S(1)}, f32[241,96]{0,1:T(8,128)S(1)}, u32[]{:S(2)}, u32[]{:S(2)}) %collective-permute-start.2) | collective-permute-done | bytes 92576 | tf_op jit(solution)/shard_map/ppermute | solution.py:58
  22.3 0.1 convert_element_type.86
  22.6 0.1 copy.35
  22.7 2.1 %collective-permute-start.3 = (f32[241,96]{0,1:T(8,128)S(1)}, f32[241,96]{0,1:T(8,128)S(1)}, u32[]{:S(2)}, u32[]{:S(2)}) collective-permute-start(f32[241,96]{0,1:T(8,128)S(1)} %pad_maximum_fusion.2), channel_id=1, source_target_pairs={{0,2},{1,3},{2,0},{3,1},{4,6},{5,7},{6,4},{7,5},{8,10},{9,11},{10,... | collective-permute-start | bytes 277640 | tf_op jit(solution)/shard_map/ppermute | solution.py:58
  24.8 2.6 %collective-permute-done.3 = f32[241,96]{0,1:T(8,128)S(1)} collective-permute-done((f32[241,96]{0,1:T(8,128)S(1)}, f32[241,96]{0,1:T(8,128)S(1)}, u32[]{:S(2)}, u32[]{:S(2)}) %collective-permute-start.3) | collective-permute-done | bytes 92576 | tf_op jit(solution)/shard_map/ppermute | solution.py:58
  27.6 0.1 convert_element_type.89
  27.9 0.1 copy.38
  28.2 0.1 copy.39
  28.3 1.2 %collective-permute-done.4 = f32[241,96]{0,1:T(8,128)S(1)} collective-permute-done((f32[241,96]{0,1:T(8,128)S(1)}, f32[241,96]{0,1:T(8,128)S(1)}, u32[]{:S(2)}, u32[]{:S(2)}) %collective-permute-start.4) | collective-permute-done | bytes 92576 | tf_op jit(solution)/shard_map/ppermute | solution.py:58
  29.5 0.2 slice_reduce_fusion
  29.9 0.1 convert_element_type.96
  30.0 0.1 broadcast_select_fusion.1
  30.2 0.6 %reshape_reshape.12.yr_ref = bf16[48,192]{1,0:T(8,128)(2,1)} reshape(bf16[4,2,1,6,192]{4,3,1,0,2:T(8,128)(2,1)S(1)} %copy.46) | data formatting | bytes 36864 | tf_op jit(solution)/shard_map/reshape;reshape | solution.py:204
  31.1 0.8 %maximum_maximum_fusion.g_ref = f32[192,192]{1,0:T(8,128)} fusion(f32[96,96]{1,0:T(8,128)S(1)} %get-tuple-element.13, f32[96,96]{1,0:T(8,128)S(1)} %copy.42, f32[96,96]{1,0:T(8,128)S(1)} %get-tuple-element.14, f32[96,96]{1,0:T(8,128)S(1)} %get-tuple-element.12), kind=kLoop, calls=%fused_computation.5 | loop fusion | flops 110592 | bytes 294912 | tf_op jit(solution)/shard_map/concatenate | solution.py:38
  31.9 10.1 %shard_map.76 = (f32[192,192]{1,0:T(8,128)}, bf16[192,2560]{1,0:T(8,128)(2,1)}, bf16[48,192]{1,0:T(8,128)(2,1)}) custom-call(f32[192,192]{1,0:T(8,128)} %maximum_maximum_fusion.g_ref, bf16[2560,192]{1,0:T(8,128)(2,1)} %copy-done.1, bf16[48,192]{1,0:T(8,128)(2,1)} %reshape_reshape.12.yr_ref), custom_call_target="tpu_custom_call" | custom-call | tf_op jit(solution)/shard_map/pallas_call | solution.py:156
  (41 shorter events, 1.9 us)
Async XLA Ops:
  0.6 1.9 %copy-start = (bf16[2560,512]{1,0:T(8,128)(2,1)S(1)}, bf16[2560,512]{1,0:T(8,128)(2,1)}, u32[]{:S(2)}) copy-start(bf16[2560,512]{1,0:T(8,128)(2,1)} %param.5) | copy-start | bytes 7864324
  4.4 1.1 %copy-start.1 = (bf16[2560,192]{1,0:T(8,128)(2,1)}, bf16[2560,192]{1,0:T(8,128)(2,1)S(1)}, u32[]{:S(2)}) copy-start(bf16[2560,192]{1,0:T(8,128)(2,1)S(1)} %convolution_convert_fusion.ys_ref) | copy-start | bytes 2949124
  4.7 4.2 %copy-start.2 = (s32[32,1]{0,1:T(1,128)S(1)}, s32[32,1]{0,1:T(1,128)}, u32[]{:S(2)}) copy-start(s32[32,1]{0,1:T(1,128)} %param.7) | copy-start | bytes 388
  5.8 5.9 %collective-permute-start = (f32[193,96]{0,1:T(8,128)S(1)}, f32[193,96]{0,1:T(8,128)S(1)}, u32[]{:S(2)}, u32[]{:S(2)}) collective-permute-start(f32[193,96]{0,1:T(8,128)S(1)} %pad_maximum_fusion), channel_id=1, source_target_pairs={{0,16},{1,17},{2,18},{3,19},{4,20},{5,21},{6,22},{7,23},{8,24},{9,... | collective-permute-start | bytes 222344 | tf_op jit(solution)/shard_map/ppermute | solution.py:51
  11.8 4.7 %collective-permute-start.1 = (f32[193,96]{0,1:T(8,128)S(1)}, f32[193,96]{0,1:T(8,128)S(1)}, u32[]{:S(2)}, u32[]{:S(2)}) collective-permute-start(f32[193,96]{0,1:T(8,128)S(1)} %fusion.21), channel_id=1, source_target_pairs={{0,8},{1,9},{2,10},{3,11},{4,12},{5,13},{6,14},{7,15},{8,0},{9,1},... | collective-permute-start | bytes 222344 | tf_op jit(solution)/shard_map/ppermute | solution.py:51
  16.6 5.6 %collective-permute-start.2 = (f32[241,96]{0,1:T(8,128)S(1)}, f32[241,96]{0,1:T(8,128)S(1)}, u32[]{:S(2)}, u32[]{:S(2)}) collective-permute-start(f32[241,96]{0,1:T(8,128)S(1)} %pad_maximum_fusion.1), channel_id=1, source_target_pairs={{0,4},{1,5},{2,6},{3,7},{4,0},{5,1},{6,2},{7,3},{8,12},{9,13},{10,... | collective-permute-start | bytes 277640 | tf_op jit(solution)/shard_map/ppermute | solution.py:58
  22.7 4.7 %collective-permute-start.3 = (f32[241,96]{0,1:T(8,128)S(1)}, f32[241,96]{0,1:T(8,128)S(1)}, u32[]{:S(2)}, u32[]{:S(2)}) collective-permute-start(f32[241,96]{0,1:T(8,128)S(1)} %pad_maximum_fusion.2), channel_id=1, source_target_pairs={{0,2},{1,3},{2,0},{3,1},{4,6},{5,7},{6,4},{7,5},{8,10},{9,11},{10,... | collective-permute-start | bytes 277640 | tf_op jit(solution)/shard_map/ppermute | solution.py:58
  28.1 1.4 %collective-permute-start.4 = (f32[241,96]{0,1:T(8,128)S(1)}, f32[241,96]{0,1:T(8,128)S(1)}, u32[]{:S(2)}, u32[]{:S(2)}) collective-permute-start(f32[241,96]{0,1:T(8,128)S(1)} %pad_maximum_fusion.3), channel_id=1, source_target_pairs={{0,1},{1,0},{2,3},{3,2},{4,5},{5,4},{6,7},{7,6},{8,9},{9,8},{10,11... | collective-permute-start | bytes 277640 | tf_op jit(solution)/shard_map/ppermute | solution.py:58

commit v10 on v9

--- a/solution.py
+++ b/solution.py
@@ -10,7 +10,7 @@
 CAP = 6
 AXES = ("grp", "rows")
 HIGHEST = lax.Precision.HIGHEST
-GROUP = 8
+GROUP = 16
 
 
 def sketch_block(block, omega):
@@ -142,7 +142,7 @@
 
 def factor_and_basis(g, y_stat, y_rot):
     k = g.shape[0]
-    panel = next((p for p in (96, 64, 48, 32, 16, 8) if k % p == 0), None)
+    panel = next((p for p in (96, 64, 48, 32, 16) if k % p == 0 and p % GROUP == 0), None)
     if panel is None:
         lower = jnp.linalg.cholesky(g)
         eye = jnp.eye(k, dtype=jnp.float32)

time: 42.3 us -> 42.9 us (1.014)
  Pallas kernels: 10.1 us -> 10.6 us
    pallas_call x1, Pallas kernels: 10.1 us -> 10.6 us  [factor_and_basis(): pl.pallas_call(functools.partial(_chol_kernel, panel=panel), out_shape=(j...]
where the time goes in v10:
time: 42.9 us; the launch traced here: 42.6 us
  waiting for transfers between devices  11.3 us (26%)
  Pallas kernels  10.6 us (25%)
  starting transfers between devices  10 us (23%)
  matrix products  3.91 us (9%)
  local copies, waits for them, and re-layouts  2.73 us (6%)
  other arithmetic  2.24 us (5%)
  between operations  1.7 us (4%)
    pallas_call x1, Pallas kernels, factor_and_basis(): pl.pallas_call(functools.partial(_chol_kernel, panel=panel), out_shape=(j...  10.6 us
    ppermute x3, waiting for transfers between devices, all_sum_and_route(): got = lax.ppermute(packet, AXES, perm)  6.38 us
    ppermute x3, starting transfers between devices, all_sum_and_route(): got = lax.ppermute(packet, AXES, perm)  5.11 us
    ppermute x2, waiting for transfers between devices, all_sum_and_route(): x = x + lax.ppermute(x, AXES, perm)  4.95 us
    ppermute x2, starting transfers between devices, all_sum_and_route(): x = x + lax.ppermute(x, AXES, perm)  4.93 us
    dot_general x2, matrix products, sketch_block(): jnp.dot(block, omega, preferred_element_type=jnp.float32)  2.87 us
  transfers between devices with their start and end apart: 5, of which 5 were waited for; matrix products, arithmetic and copies ran while one was open for 2% of the time, Pallas kernels for 0%

profile of v10, /device:TPU:0, one launch (start us, length us, event | category | flops | bytes accessed | tf_op | source)
XLA Modules:
  0.0 42.6 jit_solution(1766659702226908926)
XLA Ops:
  1.5 1.1 %convolution_convert_fusion.2 = bf16[32,192]{1,0:T(8,128)(2,1)S(1)} fusion(bf16[32,512]{1,0:T(8,128)(2,1)} %param.6, bf16[512,192]{0,1:T(8,128)(2,1)} %param.9), kind=kOutput, calls=%fused_computation.4 | convolution fusion | flops 6297600 | bytes 241664 | tf_op jit(solution)/shard_map/dot_general | solution.py:17
  2.6 1.8 %convolution_convert_fusion.ys_ref = bf16[2560,192]{1,0:T(8,128)(2,1)S(1)} fusion(bf16[2560,512]{1,0:T(8,128)(2,1)S(1)} %copy-done, bf16[512,192]{0,1:T(8,128)(2,1)} %param.9), kind=kOutput, calls=%fused_computation | convolution fusion | flops 503808000 | bytes 3801088 | tf_op jit(solution)/shard_map/dot_general | solution.py:17
  4.4 0.3 fusion.5
  4.7 0.6 %fusion = f32[192,192]{0,1:T(8,128)S(1)} fusion(f32[192,192]{0,1:T(8,128)S(1)} %fusion.5, bf16[2560,192]{1,0:T(8,128)(2,1)S(1)} %convolution_convert_fusion.ys_ref), kind=kOutput, calls=%fused_computation.2 | convolution fusion | flops 188817408 | bytes 1277952 | tf_op jit(solution)/shard_map/dot_general | solution.py:191
  5.3 0.1 copy-done.1
  5.4 0.2 fusion.13
  5.6 0.1 copy.30
  5.7 0.1 pad_maximum_fusion
  5.8 3.1 %collective-permute-start = (f32[193,96]{0,1:T(8,128)S(1)}, f32[193,96]{0,1:T(8,128)S(1)}, u32[]{:S(2)}, u32[]{:S(2)}) collective-permute-start(f32[193,96]{0,1:T(8,128)S(1)} %pad_maximum_fusion), channel_id=1, source_target_pairs={{0,16},{1,17},{2,18},{3,19},{4,20},{5,21},{6,22},{7,23},{8,24},{9,... | collective-permute-start | bytes 222344 | tf_op jit(solution)/shard_map/ppermute | solution.py:51
  9.0 0.2 select_reduce_fusion.1
  9.2 0.1 convolution_convert_fusion.1
  9.4 2.3 %collective-permute-done = f32[193,96]{0,1:T(8,128)S(1)} collective-permute-done((f32[193,96]{0,1:T(8,128)S(1)}, f32[193,96]{0,1:T(8,128)S(1)}, u32[]{:S(2)}, u32[]{:S(2)}) %collective-permute-start) | collective-permute-done | bytes 74144 | tf_op jit(solution)/shard_map/ppermute | solution.py:51
  11.7 0.1 fusion.21
  11.8 1.9 %collective-permute-start.1 = (f32[193,96]{0,1:T(8,128)S(1)}, f32[193,96]{0,1:T(8,128)S(1)}, u32[]{:S(2)}, u32[]{:S(2)}) collective-permute-start(f32[193,96]{0,1:T(8,128)S(1)} %fusion.21), channel_id=1, source_target_pairs={{0,8},{1,9},{2,10},{3,11},{4,12},{5,13},{6,14},{7,15},{8,0},{9,1},... | collective-permute-start | bytes 222344 | tf_op jit(solution)/shard_map/ppermute | solution.py:51
  13.8 0.1 copy.31
  13.9 2.6 %collective-permute-done.1 = f32[193,96]{0,1:T(8,128)S(1)} collective-permute-done((f32[193,96]{0,1:T(8,128)S(1)}, f32[193,96]{0,1:T(8,128)S(1)}, u32[]{:S(2)}, u32[]{:S(2)}) %collective-permute-start.1) | collective-permute-done | bytes 74144 | tf_op jit(solution)/shard_map/ppermute | solution.py:51
  16.6 3.0 %collective-permute-start.2 = (f32[241,96]{0,1:T(8,128)S(1)}, f32[241,96]{0,1:T(8,128)S(1)}, u32[]{:S(2)}, u32[]{:S(2)}) collective-permute-start(f32[241,96]{0,1:T(8,128)S(1)} %pad_maximum_fusion.1), channel_id=1, source_target_pairs={{0,4},{1,5},{2,6},{3,7},{4,0},{5,1},{6,2},{7,3},{8,12},{9,13},{10,... | collective-permute-start | bytes 277640 | tf_op jit(solution)/shard_map/ppermute | solution.py:58
  19.5 2.6 %collective-permute-done.2 = f32[241,96]{0,1:T(8,128)S(1)} collective-permute-done((f32[241,96]{0,1:T(8,128)S(1)}, f32[241,96]{0,1:T(8,128)S(1)}, u32[]{:S(2)}, u32[]{:S(2)}) %collective-permute-start.2) | collective-permute-done | bytes 92576 | tf_op jit(solution)/shard_map/ppermute | solution.py:58
  22.3 0.1 convert_element_type.86
  22.6 0.1 copy.35
  22.7 2.1 %collective-permute-start.3 = (f32[241,96]{0,1:T(8,128)S(1)}, f32[241,96]{0,1:T(8,128)S(1)}, u32[]{:S(2)}, u32[]{:S(2)}) collective-permute-start(f32[241,96]{0,1:T(8,128)S(1)} %pad_maximum_fusion.2), channel_id=1, source_target_pairs={{0,2},{1,3},{2,0},{3,1},{4,6},{5,7},{6,4},{7,5},{8,10},{9,11},{10,... | collective-permute-start | bytes 277640 | tf_op jit(solution)/shard_map/ppermute | solution.py:58
  24.8 2.6 %collective-permute-done.3 = f32[241,96]{0,1:T(8,128)S(1)} collective-permute-done((f32[241,96]{0,1:T(8,128)S(1)}, f32[241,96]{0,1:T(8,128)S(1)}, u32[]{:S(2)}, u32[]{:S(2)}) %collective-permute-start.3) | collective-permute-done | bytes 92576 | tf_op jit(solution)/shard_map/ppermute | solution.py:58
  27.6 0.1 convert_element_type.89
  27.9 0.1 copy.38
  28.2 0.1 copy.39
  28.3 1.2 %collective-permute-done.4 = f32[241,96]{0,1:T(8,128)S(1)} collective-permute-done((f32[241,96]{0,1:T(8,128)S(1)}, f32[241,96]{0,1:T(8,128)S(1)}, u32[]{:S(2)}, u32[]{:S(2)}) %collective-permute-start.4) | collective-permute-done | bytes 92576 | tf_op jit(solution)/shard_map/ppermute | solution.py:58
  29.5 0.2 slice_reduce_fusion
  29.9 0.1 convert_element_type.96
  30.0 0.1 broadcast_select_fusion.1
  30.2 0.6 %reshape_reshape.12.yr_ref = bf16[48,192]{1,0:T(8,128)(2,1)} reshape(bf16[4,2,1,6,192]{4,3,1,0,2:T(8,128)(2,1)S(1)} %copy.46) | data formatting | bytes 36864 | tf_op jit(solution)/shard_map/reshape;reshape | solution.py:204
  31.1 0.8 %maximum_maximum_fusion.g_ref = f32[192,192]{1,0:T(8,128)} fusion(f32[96,96]{1,0:T(8,128)S(1)} %get-tuple-element.13, f32[96,96]{1,0:T(8,128)S(1)} %copy.42, f32[96,96]{1,0:T(8,128)S(1)} %get-tuple-element.14, f32[96,96]{1,0:T(8,128)S(1)} %get-tuple-element.12), kind=kLoop, calls=%fused_computation.5 | loop fusion | flops 110592 | bytes 294912 | tf_op jit(solution)/shard_map/concatenate | solution.py:38
  31.9 10.6 %shard_map.76 = (f32[192,192]{1,0:T(8,128)}, bf16[192,2560]{1,0:T(8,128)(2,1)}, bf16[48,192]{1,0:T(8,128)(2,1)}) custom-call(f32[192,192]{1,0:T(8,128)} %maximum_maximum_fusion.g_ref, bf16[2560,192]{1,0:T(8,128)(2,1)} %copy-done.1, bf16[48,192]{1,0:T(8,128)(2,1)} %reshape_reshape.12.yr_ref), custom_call_target="tpu_custom_call" | custom-call | tf_op jit(solution)/shard_map/pallas_call | solution.py:156
  (41 shorter events, 1.9 us)
Async XLA Ops:
  0.6 1.9 %copy-start = (bf16[2560,512]{1,0:T(8,128)(2,1)S(1)}, bf16[2560,512]{1,0:T(8,128)(2,1)}, u32[]{:S(2)}) copy-start(bf16[2560,512]{1,0:T(8,128)(2,1)} %param.5) | copy-start | bytes 7864324
  4.4 1.1 %copy-start.1 = (bf16[2560,192]{1,0:T(8,128)(2,1)}, bf16[2560,192]{1,0:T(8,128)(2,1)S(1)}, u32[]{:S(2)}) copy-start(bf16[2560,192]{1,0:T(8,128)(2,1)S(1)} %convolution_convert_fusion.ys_ref) | copy-start | bytes 2949124
  4.7 4.2 %copy-start.2 = (s32[32,1]{0,1:T(1,128)S(1)}, s32[32,1]{0,1:T(1,128)}, u32[]{:S(2)}) copy-start(s32[32,1]{0,1:T(1,128)} %param.7) | copy-start | bytes 388
  5.8 5.9 %collective-permute-start = (f32[193,96]{0,1:T(8,128)S(1)}, f32[193,96]{0,1:T(8,128)S(1)}, u32[]{:S(2)}, u32[]{:S(2)}) collective-permute-start(f32[193,96]{0,1:T(8,128)S(1)} %pad_maximum_fusion), channel_id=1, source_target_pairs={{0,16},{1,17},{2,18},{3,19},{4,20},{5,21},{6,22},{7,23},{8,24},{9,... | collective-permute-start | bytes 222344 | tf_op jit(solution)/shard_map/ppermute | solution.py:51
  11.8 4.7 %collective-permute-start.1 = (f32[193,96]{0,1:T(8,128)S(1)}, f32[193,96]{0,1:T(8,128)S(1)}, u32[]{:S(2)}, u32[]{:S(2)}) collective-permute-start(f32[193,96]{0,1:T(8,128)S(1)} %fusion.21), channel_id=1, source_target_pairs={{0,8},{1,9},{2,10},{3,11},{4,12},{5,13},{6,14},{7,15},{8,0},{9,1},... | collective-permute-start | bytes 222344 | tf_op jit(solution)/shard_map/ppermute | solution.py:51
  16.6 5.6 %collective-permute-start.2 = (f32[241,96]{0,1:T(8,128)S(1)}, f32[241,96]{0,1:T(8,128)S(1)}, u32[]{:S(2)}, u32[]{:S(2)}) collective-permute-start(f32[241,96]{0,1:T(8,128)S(1)} %pad_maximum_fusion.1), channel_id=1, source_target_pairs={{0,4},{1,5},{2,6},{3,7},{4,0},{5,1},{6,2},{7,3},{8,12},{9,13},{10,... | collective-permute-start | bytes 277640 | tf_op jit(solution)/shard_map/ppermute | solution.py:58
  22.7 4.7 %collective-permute-start.3 = (f32[241,96]{0,1:T(8,128)S(1)}, f32[241,96]{0,1:T(8,128)S(1)}, u32[]{:S(2)}, u32[]{:S(2)}) collective-permute-start(f32[241,96]{0,1:T(8,128)S(1)} %pad_maximum_fusion.2), channel_id=1, source_target_pairs={{0,2},{1,3},{2,0},{3,1},{4,6},{5,7},{6,4},{7,5},{8,10},{9,11},{10,... | collective-permute-start | bytes 277640 | tf_op jit(solution)/shard_map/ppermute | solution.py:58
  28.1 1.4 %collective-permute-start.4 = (f32[241,96]{0,1:T(8,128)S(1)}, f32[241,96]{0,1:T(8,128)S(1)}, u32[]{:S(2)}, u32[]{:S(2)}) collective-permute-start(f32[241,96]{0,1:T(8,128)S(1)} %pad_maximum_fusion.3), channel_id=1, source_target_pairs={{0,1},{1,0},{2,3},{3,2},{4,5},{5,4},{6,7},{7,6},{8,9},{9,8},{10,11... | collective-permute-start | bytes 277640 | tf_op jit(solution)/shard_map/ppermute | solution.py:58

commit v11 on v9

--- a/solution.py
+++ b/solution.py
@@ -15,6 +15,44 @@
 
 def sketch_block(block, omega):
     return jnp.dot(block, omega, preferred_element_type=jnp.float32).astype(jnp.bfloat16)
+
+
+def _sketch_kernel(x_ref, w_ref, s_ref, g_ref):
+    @pl.when(pl.program_id(0) == 0)
+    def _():
+        g_ref[...] = jnp.zeros_like(g_ref)
+
+    s = jnp.dot(x_ref[...], w_ref[...], preferred_element_type=jnp.float32).astype(jnp.bfloat16)
+    s_ref[...] = s
+    g_ref[...] += lax.dot_general(
+        s, s, (((0,), (0,)), ((), ())), preferred_element_type=jnp.float32
+    )
+
+
+def sketch_and_gram(x, w):
+    n, k = x.shape[0], w.shape[1]
+    step = next((c for c in (512, 256, 128, 64, 32, 16) if n % c == 0), None)
+    if step is None:
+        s = sketch_block(x, w)
+        dims = (((0,), (0,)), ((), ()))
+        return s, lax.dot_general(s, s, dims, preferred_element_type=jnp.float32)
+    return pl.pallas_call(
+        _sketch_kernel,
+        grid=(n // step,),
+        in_specs=[
+            pl.BlockSpec((step, x.shape[1]), lambda i: (i, 0)),
+            pl.BlockSpec(w.shape, lambda i: (0, 0)),
+        ],
+        out_specs=(
+            pl.BlockSpec((step, k), lambda i: (i, 0)),
+            pl.BlockSpec((k, k), lambda i: (0, 0)),
+        ),
+        out_shape=(
+            jax.ShapeDtypeStruct((n, k), jnp.bfloat16),
+            jax.ShapeDtypeStruct((k, k), jnp.float32),
+        ),
+        compiler_params=pltpu.CompilerParams(dimension_semantics=("arbitrary",)),
+    )(x, w)
 
 
 def pack_sym(g):
@@ -183,13 +221,12 @@
     slot = jnp.where(live, targets * CAP + rank, -1)
     select = (lax.iota(jnp.int32, n_rows * CAP)[:, None] == slot[None, :]).astype(jnp.bfloat16)
 
-    sketch_stat = sketch_block(stationary, omega)
+    sketch_stat, gram_stat = sketch_and_gram(stationary, omega)
     sketch_rot = sketch_block(rotor_rows, omega)
     rot_live = jnp.where(live[:, None], sketch_rot, jnp.zeros_like(sketch_rot))
 
     dims = (((0,), (0,)), ((), ()))
-    gram = lax.dot_general(sketch_stat, sketch_stat, dims, preferred_element_type=jnp.float32)
-    gram = gram + lax.dot_general(rot_live, rot_live, dims, preferred_element_type=jnp.float32)
+    gram = gram_stat + lax.dot_general(rot_live, rot_live, dims, preferred_element_type=jnp.float32)
     gram = gram / total
 
     outgoing = jnp.dot(select, sketch_rot, preferred_element_type=jnp.float32).astype(jnp.bfloat16)

time: 42.3 us -> 48.2 us (1.14)
  Pallas kernels: 10.1 us -> 15.7 us
  local copies, waits for them, and re-layouts: 2.73 us -> 5.39 us
  matrix products: 3.91 us -> 1.5 us
    pallas_call x0 -> x1, Pallas kernels: none -> 5.65 us  [sketch_and_gram(): pl.pallas_call(_sketch_kernel, grid=(n // step,), in_specs=[pl.BlockSpec(...]
    dot_general x2 -> x1, matrix products: 2.87 us -> 1.06 us  [sketch_block(): jnp.dot(block, omega, preferred_element_type=jnp.float32)]
    unnamed x6 -> x5, local copies, waits for them, and re-layouts: 0.16 us -> 1.78 us
    pallas_call x0 -> x1, local copies, waits for them, and re-layouts: none -> 1.04 us  [sketch_and_gram(): pl.pallas_call(_sketch_kernel, grid=(n // step,), in_specs=[pl.BlockSpec(...]
    dot_general x1 -> x0, matrix products: 0.62 us -> none  [per_device(): lax.dot_general(sketch_stat, sketch_stat, dims, preferred_element_type=jn...]
where the time goes in v11:
time: 48.2 us; the launch traced here: 47.7 us
  Pallas kernels  15.7 us (33%)
  waiting for transfers between devices  11.3 us (23%)
  starting transfers between devices  10 us (21%)
  local copies, waits for them, and re-layouts  5.39 us (11%)
  other arithmetic  2.24 us (5%)
  between operations  1.55 us (3%)
  matrix products  1.5 us (3%)
    pallas_call x1, Pallas kernels, factor_and_basis(): pl.pallas_call(functools.partial(_chol_kernel, panel=panel), out_shape=(j...  10.1 us
    ppermute x3, waiting for transfers between devices, all_sum_and_route(): got = lax.ppermute(packet, AXES, perm)  6.38 us
    pallas_call x1, Pallas kernels, sketch_and_gram(): pl.pallas_call(_sketch_kernel, grid=(n // step,), in_specs=[pl.BlockSpec(...  5.65 us
    ppermute x3, starting transfers between devices, all_sum_and_route(): got = lax.ppermute(packet, AXES, perm)  5.11 us
    ppermute x2, waiting for transfers between devices, all_sum_and_route(): x = x + lax.ppermute(x, AXES, perm)  4.95 us
    ppermute x2, starting transfers between devices, all_sum_and_route(): x = x + lax.ppermute(x, AXES, perm)  4.93 us
    unnamed x5, local copies, waits for them, and re-layouts  1.78 us
    dot_general x1, matrix products, sketch_block(): jnp.dot(block, omega, preferred_element_type=jnp.float32)  1.06 us
  transfers between devices with their start and end apart: 5, of which 5 were waited for; matrix products, arithmetic and copies ran while one was open for 2% of the time, Pallas kernels for 0%

profile of v11, /device:TPU:0, one launch (start us, length us, event | category | flops | bytes accessed | tf_op | source)
XLA Modules:
  0.0 47.7 jit_solution(2648267377424620991)
XLA Ops:
  1.3 1.8 %copy.31.w_ref = bf16[512,192]{1,0:T(8,128)(2,1)} copy(bf16[512,192]{0,1:T(8,128)(2,1)} %param.9) | data formatting | bytes 393216 | tf_op args[4]
  3.1 1.1 %convolution_convert_fusion.1 = bf16[32,192]{1,0:T(8,128)(2,1)S(1)} fusion(bf16[32,512]{1,0:T(8,128)(2,1)S(1)} %copy-done, bf16[512,192]{0,1:T(8,128)(2,1)} %param.9), kind=kOutput, calls=%fused_computation.3 | convolution fusion | flops 6297600 | bytes 241664 | tf_op jit(solution)/shard_map/dot_general | solution.py:17
  4.2 5.6 %shard_map.76 = (bf16[2560,192]{1,0:T(8,128)(2,1)}, f32[192,192]{1,0:T(8,128)}) custom-call(bf16[2560,512]{1,0:T(8,128)(2,1)} %x_ref.1, bf16[512,192]{1,0:T(8,128)(2,1)} %copy.31.w_ref), custom_call_target="tpu_custom_call" | custom-call | tf_op jit(solution)/shard_map/pallas_call | solution.py:39
  9.8 1.0 %copy.32 = f32[192,192]{0,1:T(8,128)S(1)} copy(f32[192,192]{1,0:T(8,128)} %get-tuple-element.8) | data formatting | bytes 294912 | tf_op jit(solution)/shard_map/pallas_call | solution.py:39
  10.9 0.3 fusion
  11.2 0.2 fusion.12
  11.4 0.1 copy.33
  11.5 0.1 pad_maximum_fusion
  11.6 3.1 %collective-permute-start = (f32[193,96]{0,1:T(8,128)S(1)}, f32[193,96]{0,1:T(8,128)S(1)}, u32[]{:S(2)}, u32[]{:S(2)}) collective-permute-start(f32[193,96]{0,1:T(8,128)S(1)} %pad_maximum_fusion), channel_id=1, source_target_pairs={{0,16},{1,17},{2,18},{3,19},{4,20},{5,21},{6,22},{7,23},{8,24},{9,... | collective-permute-start | bytes 222344 | tf_op jit(solution)/shard_map/ppermute | solution.py:89
  14.8 0.2 select_reduce_fusion.1
  15.0 0.1 convolution_convert_fusion
  15.1 2.3 %collective-permute-done = f32[193,96]{0,1:T(8,128)S(1)} collective-permute-done((f32[193,96]{0,1:T(8,128)S(1)}, f32[193,96]{0,1:T(8,128)S(1)}, u32[]{:S(2)}, u32[]{:S(2)}) %collective-permute-start) | collective-permute-done | bytes 74144 | tf_op jit(solution)/shard_map/ppermute | solution.py:89
  17.4 0.1 fusion.16
  17.5 1.9 %collective-permute-start.1 = (f32[193,96]{0,1:T(8,128)S(1)}, f32[193,96]{0,1:T(8,128)S(1)}, u32[]{:S(2)}, u32[]{:S(2)}) collective-permute-start(f32[193,96]{0,1:T(8,128)S(1)} %fusion.16), channel_id=1, source_target_pairs={{0,8},{1,9},{2,10},{3,11},{4,12},{5,13},{6,14},{7,15},{8,0},{9,1},... | collective-permute-start | bytes 222344 | tf_op jit(solution)/shard_map/ppermute | solution.py:89
  19.5 0.1 copy.34
  19.6 2.6 %collective-permute-done.1 = f32[193,96]{0,1:T(8,128)S(1)} collective-permute-done((f32[193,96]{0,1:T(8,128)S(1)}, f32[193,96]{0,1:T(8,128)S(1)}, u32[]{:S(2)}, u32[]{:S(2)}) %collective-permute-start.1) | collective-permute-done | bytes 74144 | tf_op jit(solution)/shard_map/ppermute | solution.py:89
  22.3 3.0 %collective-permute-start.2 = (f32[241,96]{0,1:T(8,128)S(1)}, f32[241,96]{0,1:T(8,128)S(1)}, u32[]{:S(2)}, u32[]{:S(2)}) collective-permute-start(f32[241,96]{0,1:T(8,128)S(1)} %pad_maximum_fusion.1), channel_id=1, source_target_pairs={{0,4},{1,5},{2,6},{3,7},{4,0},{5,1},{6,2},{7,3},{8,12},{9,13},{10,... | collective-permute-start | bytes 277640 | tf_op jit(solution)/shard_map/ppermute | solution.py:96
  25.3 2.6 %collective-permute-done.2 = f32[241,96]{0,1:T(8,128)S(1)} collective-permute-done((f32[241,96]{0,1:T(8,128)S(1)}, f32[241,96]{0,1:T(8,128)S(1)}, u32[]{:S(2)}, u32[]{:S(2)}) %collective-permute-start.2) | collective-permute-done | bytes 92576 | tf_op jit(solution)/shard_map/ppermute | solution.py:96
  28.1 0.1 convert_element_type.82
  28.3 0.1 copy.38
  28.5 2.1 %collective-permute-start.3 = (f32[241,96]{0,1:T(8,128)S(1)}, f32[241,96]{0,1:T(8,128)S(1)}, u32[]{:S(2)}, u32[]{:S(2)}) collective-permute-start(f32[241,96]{0,1:T(8,128)S(1)} %pad_maximum_fusion.2), channel_id=1, source_target_pairs={{0,2},{1,3},{2,0},{3,1},{4,6},{5,7},{6,4},{7,5},{8,10},{9,11},{10,... | collective-permute-start | bytes 277640 | tf_op jit(solution)/shard_map/ppermute | solution.py:96
  30.6 2.6 %collective-permute-done.3 = f32[241,96]{0,1:T(8,128)S(1)} collective-permute-done((f32[241,96]{0,1:T(8,128)S(1)}, f32[241,96]{0,1:T(8,128)S(1)}, u32[]{:S(2)}, u32[]{:S(2)}) %collective-permute-start.3) | collective-permute-done | bytes 92576 | tf_op jit(solution)/shard_map/ppermute | solution.py:96
  33.3 0.1 convert_element_type.85
  33.7 0.1 copy.41
  34.0 0.1 copy.42
  34.1 1.2 %collective-permute-done.4 = f32[241,96]{0,1:T(8,128)S(1)} collective-permute-done((f32[241,96]{0,1:T(8,128)S(1)}, f32[241,96]{0,1:T(8,128)S(1)}, u32[]{:S(2)}, u32[]{:S(2)}) %collective-permute-start.4) | collective-permute-done | bytes 92576 | tf_op jit(solution)/shard_map/ppermute | solution.py:96
  35.3 0.2 slice_reduce_fusion
  35.7 0.1 convert_element_type.92
  35.8 0.1 broadcast_select_fusion.1
  36.0 0.6 %reshape_reshape.12.yr_ref = bf16[48,192]{1,0:T(8,128)(2,1)} reshape(bf16[4,2,1,6,192]{4,3,1,0,2:T(8,128)(2,1)S(1)} %copy.49) | data formatting | bytes 36864 | tf_op jit(solution)/shard_map/reshape;reshape | solution.py:241
  36.9 0.8 %maximum_maximum_fusion.g_ref = f32[192,192]{1,0:T(8,128)} fusion(f32[96,96]{1,0:T(8,128)S(1)} %get-tuple-element.17, f32[96,96]{1,0:T(8,128)S(1)} %copy.45, f32[96,96]{1,0:T(8,128)S(1)} %get-tuple-element.18, f32[96,96]{1,0:T(8,128)S(1)} %get-tuple-element.16), kind=kLoop, calls=%fused_computation.4 | loop fusion | flops 110592 | bytes 294912 | tf_op jit(solution)/shard_map/concatenate | solution.py:76
  37.7 10.1 %shard_map.77 = (f32[192,192]{1,0:T(8,128)}, bf16[192,2560]{1,0:T(8,128)(2,1)}, bf16[48,192]{1,0:T(8,128)(2,1)}) custom-call(f32[192,192]{1,0:T(8,128)} %maximum_maximum_fusion.g_ref, bf16[2560,192]{1,0:T(8,128)(2,1)} %get-tuple-element.9.ys_ref, bf16[48,192]{1,0:T(8,128)(2,1)} %reshape_reshape.12.yr_ref), custom_call_target="tpu_custom_call" | custom-call | tf_op jit(solution)/shard_map/pallas_call | solution.py:194
  (40 shorter events, 1.8 us)
Async XLA Ops:
  0.6 2.5 %copy-start = (bf16[32,512]{1,0:T(8,128)(2,1)S(1)}, bf16[32,512]{1,0:T(8,128)(2,1)}, u32[]{:S(2)}) copy-start(bf16[32,512]{1,0:T(8,128)(2,1)} %param.6) | copy-start | bytes 98308
  0.6 14.0 %copy-start.1 = (s32[32,1]{0,1:T(1,128)S(1)}, s32[32,1]{0,1:T(1,128)}, u32[]{:S(2)}) copy-start(s32[32,1]{0,1:T(1,128)} %param.7) | copy-start | bytes 388
  11.6 5.9 %collective-permute-start = (f32[193,96]{0,1:T(8,128)S(1)}, f32[193,96]{0,1:T(8,128)S(1)}, u32[]{:S(2)}, u32[]{:S(2)}) collective-permute-start(f32[193,96]{0,1:T(8,128)S(1)} %pad_maximum_fusion), channel_id=1, source_target_pairs={{0,16},{1,17},{2,18},{3,19},{4,20},{5,21},{6,22},{7,23},{8,24},{9,... | collective-permute-start | bytes 222344 | tf_op jit(solution)/shard_map/ppermute | solution.py:89
  17.5 4.7 %collective-permute-start.1 = (f32[193,96]{0,1:T(8,128)S(1)}, f32[193,96]{0,1:T(8,128)S(1)}, u32[]{:S(2)}, u32[]{:S(2)}) collective-permute-start(f32[193,96]{0,1:T(8,128)S(1)} %fusion.16), channel_id=1, source_target_pairs={{0,8},{1,9},{2,10},{3,11},{4,12},{5,13},{6,14},{7,15},{8,0},{9,1},... | collective-permute-start | bytes 222344 | tf_op jit(solution)/shard_map/ppermute | solution.py:89
  22.3 5.6 %collective-permute-start.2 = (f32[241,96]{0,1:T(8,128)S(1)}, f32[241,96]{0,1:T(8,128)S(1)}, u32[]{:S(2)}, u32[]{:S(2)}) collective-permute-start(f32[241,96]{0,1:T(8,128)S(1)} %pad_maximum_fusion.1), channel_id=1, source_target_pairs={{0,4},{1,5},{2,6},{3,7},{4,0},{5,1},{6,2},{7,3},{8,12},{9,13},{10,... | collective-permute-start | bytes 277640 | tf_op jit(solution)/shard_map/ppermute | solution.py:96
  28.5 4.7 %collective-permute-start.3 = (f32[241,96]{0,1:T(8,128)S(1)}, f32[241,96]{0,1:T(8,128)S(1)}, u32[]{:S(2)}, u32[]{:S(2)}) collective-permute-start(f32[241,96]{0,1:T(8,128)S(1)} %pad_maximum_fusion.2), channel_id=1, source_target_pairs={{0,2},{1,3},{2,0},{3,1},{4,6},{5,7},{6,4},{7,5},{8,10},{9,11},{10,... | collective-permute-start | bytes 277640 | tf_op jit(solution)/shard_map/ppermute | solution.py:96
  33.9 1.4 %collective-permute-start.4 = (f32[241,96]{0,1:T(8,128)S(1)}, f32[241,96]{0,1:T(8,128)S(1)}, u32[]{:S(2)}, u32[]{:S(2)}) collective-permute-start(f32[241,96]{0,1:T(8,128)S(1)} %pad_maximum_fusion.3), channel_id=1, source_target_pairs={{0,1},{1,0},{2,3},{3,2},{4,5},{5,4},{6,7},{7,6},{8,9},{9,8},{10,11... | collective-permute-start | bytes 277640 | tf_op jit(solution)/shard_map/ppermute | solution.py:96

commit v12 on v9

--- a/solution.py
+++ b/solution.py
@@ -65,12 +65,21 @@
 
 
 def _chol_kernel(g_ref, ys_ref, yr_ref, u_ref, bs_ref, br_ref, b_ref, *, panel):
-    k = g_ref.shape[0]
+    k = g_ref.shape[1] * 2
     w = 2 * k
     kp = ((k + 127) // 128) * 128
     rows = lax.broadcasted_iota(jnp.int32, (k, k), 0)
     cols = lax.broadcasted_iota(jnp.int32, (k, k), 1)
-    b_ref[:, :k] = g_ref[...]
+    h = k // 2
+    packed = g_ref[...]
+    lower_b, mixed, diag_c = packed[:h], packed[h : 2 * h], packed[2 * h : 2 * h + 1]
+    i = lax.broadcasted_iota(jnp.int32, (h, h), 0)
+    j = lax.broadcasted_iota(jnp.int32, (h, h), 1)
+    mixed_t = mixed.T
+    a = jnp.where(i >= j, mixed, mixed_t)
+    c = jnp.where(i < j, mixed, jnp.where(i > j, mixed_t, diag_c))
+    top = jnp.concatenate([a, lower_b.T], axis=1)
+    b_ref[:, :k] = jnp.concatenate([top, jnp.concatenate([lower_b, c], axis=1)], axis=0)
     b_ref[:, k:] = jnp.where(rows == cols, 1.0, 0.0).astype(jnp.float32)
     for p in range(k // panel):
         base = p * panel
@@ -140,11 +149,11 @@
                 o_ref[i : i + step, :] = acc.astype(o_ref.dtype)
 
 
-def factor_and_basis(g, y_stat, y_rot):
-    k = g.shape[0]
+def factor_and_basis(packed, y_stat, y_rot):
+    k = packed.shape[1] * 2
     panel = next((p for p in (96, 64, 48, 32, 16, 8) if k % p == 0), None)
     if panel is None:
-        lower = jnp.linalg.cholesky(g)
+        lower = jnp.linalg.cholesky(unpack_sym(packed))
         eye = jnp.eye(k, dtype=jnp.float32)
         inverse = lax.linalg.triangular_solve(lower, eye, left_side=True, lower=True)
         basis = [
@@ -163,7 +172,7 @@
         in_specs=[vmem, vmem, vmem],
         out_specs=(vmem, vmem, vmem),
         scratch_shapes=[pltpu.VMEM((k, 2 * k), jnp.float32)],
-    )(g, y_stat, y_rot)
+    )(packed, y_stat, y_rot)
     return upper, basis_stat_t.T, basis_rot
 
 
@@ -202,8 +211,7 @@
     else:
         packed, arrived = all_sum_and_route(packed, outgoing, n, n_rows)
     arrived = arrived.reshape(n_rows * CAP, -1)
-    gram = unpack_sym(packed)
-    upper, basis_stat, basis_rot = factor_and_basis(gram, sketch_stat, arrived)
+    upper, basis_stat, basis_rot = factor_and_basis(packed, sketch_stat, arrived)
     return (basis_stat, basis_rot, upper)
 
 

time: 42.3 us -> 42 us (level)
  local copies, waits for them, and re-layouts: 2.73 us -> 1.46 us
  waiting for transfers between devices: 11.3 us -> 12.4 us
  other arithmetic: 2.24 us -> 1.48 us
    ppermute x3, waiting for transfers between devices: 6.38 us -> 7.22 us  [all_sum_and_route(): got = lax.ppermute(packet, AXES, perm)]
    concatenate x1 -> x0, other arithmetic: 0.82 us -> none  [unpack_sym(): jnp.concatenate([jnp.concatenate([a, b.T], axis=1), jnp.concatenate([b, c...]
    add x3, other arithmetic: 0.04 us -> 0.68 us  [all_sum_and_route(): x = x + got[:x.shape[0]]]
    slice x6 -> x3, local copies, waits for them, and re-layouts: 0.47 us -> 0.02 us  [all_sum_and_route(): came = got[x.shape[0]:].reshape(away.shape).astype(held.dtype)]
  transfers between devices with their start and end apart: 5 -> 5, of which waited for: 5 -> 5; matrix products, arithmetic and copies ran while one was open for 2% -> 1% of each run, Pallas kernels for 0% -> 0%
where the time goes in v12:
time: 42 us; the launch traced here: 41.5 us
  waiting for transfers between devices  12.4 us (30%)
  Pallas kernels  10.5 us (25%)
  starting transfers between devices  10.2 us (24%)
  matrix products  3.8 us (9%)
  between operations  1.61 us (4%)
  other arithmetic  1.48 us (4%)
  local copies, waits for them, and re-layouts  1.46 us (3%)
    pallas_call x1, Pallas kernels, factor_and_basis(): pl.pallas_call(functools.partial(_chol_kernel, panel=panel), out_shape=(j...  10.5 us
    ppermute x3, waiting for transfers between devices, all_sum_and_route(): got = lax.ppermute(packet, AXES, perm)  7.22 us
    ppermute x3, starting transfers between devices, all_sum_and_route(): got = lax.ppermute(packet, AXES, perm)  5.33 us
    ppermute x2, waiting for transfers between devices, all_sum_and_route(): x = x + lax.ppermute(x, AXES, perm)  5.21 us
    ppermute x2, starting transfers between devices, all_sum_and_route(): x = x + lax.ppermute(x, AXES, perm)  4.89 us
    dot_general x2, matrix products, sketch_block(): jnp.dot(block, omega, preferred_element_type=jnp.float32)  2.87 us
  transfers between devices with their start and end apart: 5, of which 5 were waited for; matrix products, arithmetic and copies ran while one was open for 1% of the time, Pallas kernels for 0%

profile of v12, /device:TPU:0, one launch (start us, length us, event | category | flops | bytes accessed | tf_op | source)
XLA Modules:
  0.0 41.5 jit_solution(16339680576339689773)
XLA Ops:
  1.5 1.1 %convolution_convert_fusion.2 = bf16[32,192]{1,0:T(8,128)(2,1)S(1)} fusion(bf16[32,512]{1,0:T(8,128)(2,1)} %param.6, bf16[512,192]{0,1:T(8,128)(2,1)} %param.9), kind=kOutput, calls=%fused_computation.4 | convolution fusion | flops 6297600 | bytes 241664 | tf_op jit(solution)/shard_map/dot_general | solution.py:17
  2.6 1.8 %convolution_convert_fusion.ys_ref = bf16[2560,192]{1,0:T(8,128)(2,1)S(1)} fusion(bf16[2560,512]{1,0:T(8,128)(2,1)S(1)} %copy-done, bf16[512,192]{0,1:T(8,128)(2,1)} %param.9), kind=kOutput, calls=%fused_computation | convolution fusion | flops 503808000 | bytes 3801088 | tf_op jit(solution)/shard_map/dot_general | solution.py:17
  4.4 0.3 fusion.4
  4.7 0.5 %fusion = f32[192,192]{1,0:T(8,128)S(1)} fusion(f32[192,192]{1,0:T(8,128)S(1)} %fusion.4, bf16[2560,192]{1,0:T(8,128)(2,1)S(1)} %convolution_convert_fusion.ys_ref), kind=kOutput, calls=%fused_computation.2 | convolution fusion | flops 188817408 | bytes 1277952 | tf_op jit(solution)/shard_map/dot_general | solution.py:200
  5.2 0.2 copy-done.1
  5.4 0.1 fusion.13
  5.5 3.1 %collective-permute-start = (f32[193,96]{1,0:T(8,128)S(1)}, f32[193,96]{1,0:T(8,128)S(1)}, u32[]{:S(2)}, u32[]{:S(2)}) collective-permute-start(f32[193,96]{1,0:T(8,128)S(1)} %pad_maximum_fusion.3), channel_id=1, source_target_pairs={{0,16},{1,17},{2,18},{3,19},{4,20},{5,21},{6,22},{7,23},{8,24},{9,... | collective-permute-start | bytes 222344 | tf_op jit(solution)/shard_map/ppermute | solution.py:51
  8.6 0.1 fusion.8
  8.7 0.1 reduce_window_sum.11
  8.7 0.2 select_reduce_fusion.1
  8.9 0.1 convolution_convert_fusion.1
  9.1 2.4 %collective-permute-done = f32[193,96]{1,0:T(8,128)S(1)} collective-permute-done((f32[193,96]{1,0:T(8,128)S(1)}, f32[193,96]{1,0:T(8,128)S(1)}, u32[]{:S(2)}, u32[]{:S(2)}) %collective-permute-start) | collective-permute-done | bytes 74144 | tf_op jit(solution)/shard_map/ppermute | solution.py:51
  11.5 1.8 %collective-permute-start.1 = (f32[193,96]{1,0:T(8,128)S(1)}, f32[193,96]{1,0:T(8,128)S(1)}, u32[]{:S(2)}, u32[]{:S(2)}) collective-permute-start(f32[193,96]{1,0:T(8,128)S(1)} %fusion.12), channel_id=1, source_target_pairs={{0,8},{1,9},{2,10},{3,11},{4,12},{5,13},{6,14},{7,15},{8,0},{9,1},... | collective-permute-start | bytes 222344 | tf_op jit(solution)/shard_map/ppermute | solution.py:51
  13.3 0.1 reshape.123
  13.4 2.8 %collective-permute-done.1 = f32[193,96]{1,0:T(8,128)S(1)} collective-permute-done((f32[193,96]{1,0:T(8,128)S(1)}, f32[193,96]{1,0:T(8,128)S(1)}, u32[]{:S(2)}, u32[]{:S(2)}) %collective-permute-start.1) | collective-permute-done | bytes 74144 | tf_op jit(solution)/shard_map/ppermute | solution.py:51
  16.3 2.9 %collective-permute-start.2 = (f32[241,96]{1,0:T(8,128)S(1)}, f32[241,96]{1,0:T(8,128)S(1)}, u32[]{:S(2)}, u32[]{:S(2)}) collective-permute-start(f32[241,96]{1,0:T(8,128)S(1)} %pad_maximum_fusion), channel_id=1, source_target_pairs={{0,4},{1,5},{2,6},{3,7},{4,0},{5,1},{6,2},{7,3},{8,12},{9,13},{10,... | collective-permute-start | bytes 277640 | tf_op jit(solution)/shard_map/ppermute | solution.py:58
  19.2 3.0 %collective-permute-done.2 = f32[241,96]{1,0:T(8,128)S(1)} collective-permute-done((f32[241,96]{1,0:T(8,128)S(1)}, f32[241,96]{1,0:T(8,128)S(1)}, u32[]{:S(2)}, u32[]{:S(2)}) %collective-permute-start.2) | collective-permute-done | bytes 92576 | tf_op jit(solution)/shard_map/ppermute | solution.py:58
  22.2 0.1 convert_element_type.86
  22.3 0.1 reshape.124
  22.4 2.3 %collective-permute-start.3 = (f32[241,96]{1,0:T(8,128)S(1)}, f32[241,96]{1,0:T(8,128)S(1)}, u32[]{:S(2)}, u32[]{:S(2)}) collective-permute-start(f32[241,96]{1,0:T(8,128)S(1)} %pad_maximum_fusion.1), channel_id=1, source_target_pairs={{0,2},{1,3},{2,0},{3,1},{4,6},{5,7},{6,4},{7,5},{8,10},{9,11},{10,... | collective-permute-start | bytes 277640 | tf_op jit(solution)/shard_map/ppermute | solution.py:58
  24.8 2.9 %collective-permute-done.3 = f32[241,96]{1,0:T(8,128)S(1)} collective-permute-done((f32[241,96]{1,0:T(8,128)S(1)}, f32[241,96]{1,0:T(8,128)S(1)}, u32[]{:S(2)}, u32[]{:S(2)}) %collective-permute-start.3) | collective-permute-done | bytes 92576 | tf_op jit(solution)/shard_map/ppermute | solution.py:58
  27.7 0.1 convert_element_type.89
  27.8 0.1 fusion.2
  27.9 0.1 reshape.125
  28.0 0.1 collective-permute-start.4
  28.1 1.3 %collective-permute-done.4 = f32[241,96]{1,0:T(8,128)S(1)} collective-permute-done((f32[241,96]{1,0:T(8,128)S(1)}, f32[241,96]{1,0:T(8,128)S(1)}, u32[]{:S(2)}, u32[]{:S(2)}) %collective-permute-start.4) | collective-permute-done | bytes 92576 | tf_op jit(solution)/shard_map/ppermute | solution.py:58
  29.5 0.1 convert_element_type.96
  29.5 0.1 broadcast_select_fusion.1
  29.6 0.1 pad_maximum_fusion.5
  29.7 0.6 %reshape_reshape.12.yr_ref = bf16[48,192]{1,0:T(8,128)(2,1)} reshape(bf16[4,2,1,6,192]{4,3,1,0,2:T(8,128)(2,1)S(1)} %copy.28) | data formatting | bytes 36864 | tf_op jit(solution)/shard_map/reshape;reshape | solution.py:213
  30.3 0.7 %slice_add_fusion.g_ref = f32[193,96]{1,0:T(8,128)} fusion(f32[193,96]{1,0:T(8,128)S(1)} %slice_add_fusion.1, f32[241,96]{1,0:T(8,128)S(1)} %collective-permute-done.4), kind=kLoop, calls=%fused_computation.8 | loop fusion | flops 18528 | bytes 222336 | tf_op jit(solution)/shard_map/add | solution.py:59
  31.0 10.5 %shard_map.76 = (f32[192,192]{1,0:T(8,128)}, bf16[192,2560]{1,0:T(8,128)(2,1)}, bf16[48,192]{1,0:T(8,128)(2,1)}) custom-call(f32[193,96]{1,0:T(8,128)} %slice_add_fusion.g_ref, bf16[2560,192]{1,0:T(8,128)(2,1)} %copy-done.1, bf16[48,192]{1,0:T(8,128)(2,1)} %reshape_reshape.12.yr_ref), custom_call_target="tpu_custom_call" | custom-call | tf_op jit(solution)/shard_map/pallas_call | solution.py:165
  (26 shorter events, 0.3 us)
Async XLA Ops:
  0.6 1.9 %copy-start = (bf16[2560,512]{1,0:T(8,128)(2,1)S(1)}, bf16[2560,512]{1,0:T(8,128)(2,1)}, u32[]{:S(2)}) copy-start(bf16[2560,512]{1,0:T(8,128)(2,1)} %param.5) | copy-start | bytes 7864324
  4.4 1.1 %copy-start.1 = (bf16[2560,192]{1,0:T(8,128)(2,1)}, bf16[2560,192]{1,0:T(8,128)(2,1)S(1)}, u32[]{:S(2)}) copy-start(bf16[2560,192]{1,0:T(8,128)(2,1)S(1)} %convolution_convert_fusion.ys_ref) | copy-start | bytes 2949124
  4.7 4.0 %copy-start.2 = (s32[32,1]{0,1:T(1,128)S(1)}, s32[32,1]{0,1:T(1,128)}, u32[]{:S(2)}) copy-start(s32[32,1]{0,1:T(1,128)} %param.7) | copy-start | bytes 388
  5.5 5.9 %collective-permute-start = (f32[193,96]{1,0:T(8,128)S(1)}, f32[193,96]{1,0:T(8,128)S(1)}, u32[]{:S(2)}, u32[]{:S(2)}) collective-permute-start(f32[193,96]{1,0:T(8,128)S(1)} %pad_maximum_fusion.3), channel_id=1, source_target_pairs={{0,16},{1,17},{2,18},{3,19},{4,20},{5,21},{6,22},{7,23},{8,24},{9,... | collective-permute-start | bytes 222344 | tf_op jit(solution)/shard_map/ppermute | solution.py:51
  11.5 4.7 %collective-permute-start.1 = (f32[193,96]{1,0:T(8,128)S(1)}, f32[193,96]{1,0:T(8,128)S(1)}, u32[]{:S(2)}, u32[]{:S(2)}) collective-permute-start(f32[193,96]{1,0:T(8,128)S(1)} %fusion.12), channel_id=1, source_target_pairs={{0,8},{1,9},{2,10},{3,11},{4,12},{5,13},{6,14},{7,15},{8,0},{9,1},... | collective-permute-start | bytes 222344 | tf_op jit(solution)/shard_map/ppermute | solution.py:51
  16.3 5.9 %collective-permute-start.2 = (f32[241,96]{1,0:T(8,128)S(1)}, f32[241,96]{1,0:T(8,128)S(1)}, u32[]{:S(2)}, u32[]{:S(2)}) collective-permute-start(f32[241,96]{1,0:T(8,128)S(1)} %pad_maximum_fusion), channel_id=1, source_target_pairs={{0,4},{1,5},{2,6},{3,7},{4,0},{5,1},{6,2},{7,3},{8,12},{9,13},{10,... | collective-permute-start | bytes 277640 | tf_op jit(solution)/shard_map/ppermute | solution.py:58
  22.4 5.2 %collective-permute-start.3 = (f32[241,96]{1,0:T(8,128)S(1)}, f32[241,96]{1,0:T(8,128)S(1)}, u32[]{:S(2)}, u32[]{:S(2)}) collective-permute-start(f32[241,96]{1,0:T(8,128)S(1)} %pad_maximum_fusion.1), channel_id=1, source_target_pairs={{0,2},{1,3},{2,0},{3,1},{4,6},{5,7},{6,4},{7,5},{8,10},{9,11},{10,... | collective-permute-start | bytes 277640 | tf_op jit(solution)/shard_map/ppermute | solution.py:58
  28.0 1.4 %collective-permute-start.4 = (f32[241,96]{1,0:T(8,128)S(1)}, f32[241,96]{1,0:T(8,128)S(1)}, u32[]{:S(2)}, u32[]{:S(2)}) collective-permute-start(f32[241,96]{1,0:T(8,128)S(1)} %pad_maximum_fusion.2), channel_id=1, source_target_pairs={{0,1},{1,0},{2,3},{3,2},{4,5},{5,4},{6,7},{7,6},{8,9},{9,8},{10,11... | collective-permute-start | bytes 277640 | tf_op jit(solution)/shard_map/ppermute | solution.py:58

commit v13 on v12

--- a/solution.py
+++ b/solution.py
@@ -45,10 +45,15 @@
     row_bits = n_rows.bit_length() - 1
     me = lax.axis_index(AXES)
     width = x.shape[1]
+    last = jnp.zeros_like(x)
     for b in reversed(range(bits)):
         perm = [(i, i ^ (1 << b)) for i in range(n)]
         if b >= row_bits:
-            x = x + lax.ppermute(x, AXES, perm)
+            got = lax.ppermute(x, AXES, perm)
+            if b == 0:
+                last = got
+            else:
+                x = x + got
             continue
         parts = held.reshape((n_rows >> (b + 1), 2, 1 << b) + held.shape[1:])
         mine = (me >> b) & 1
@@ -56,22 +61,25 @@
         away = jnp.where(mine == 0, parts[:, 1], parts[:, 0])
         packet = jnp.concatenate([x, away.astype(jnp.float32).reshape(-1, width)], axis=0)
         got = lax.ppermute(packet, AXES, perm)
-        x = x + got[: x.shape[0]]
+        if b == 0:
+            last = got[: x.shape[0]]
+        else:
+            x = x + got[: x.shape[0]]
         came = got[x.shape[0] :].reshape(away.shape).astype(held.dtype)
         lo = jnp.where(mine == 0, keep, came)
         hi = jnp.where(mine == 0, came, keep)
         held = jnp.stack([lo, hi], axis=1).reshape(held.shape)
-    return x, held
-
-
-def _chol_kernel(g_ref, ys_ref, yr_ref, u_ref, bs_ref, br_ref, b_ref, *, panel):
+    return (x, last), held
+
+
+def _chol_kernel(g_ref, g2_ref, ys_ref, yr_ref, u_ref, bs_ref, br_ref, b_ref, *, panel):
     k = g_ref.shape[1] * 2
     w = 2 * k
     kp = ((k + 127) // 128) * 128
     rows = lax.broadcasted_iota(jnp.int32, (k, k), 0)
     cols = lax.broadcasted_iota(jnp.int32, (k, k), 1)
     h = k // 2
-    packed = g_ref[...]
+    packed = g_ref[...] + g2_ref[...]
     lower_b, mixed, diag_c = packed[:h], packed[h : 2 * h], packed[2 * h : 2 * h + 1]
     i = lax.broadcasted_iota(jnp.int32, (h, h), 0)
     j = lax.broadcasted_iota(jnp.int32, (h, h), 1)
@@ -150,10 +158,10 @@
 
 
 def factor_and_basis(packed, y_stat, y_rot):
-    k = packed.shape[1] * 2
+    k = packed[0].shape[1] * 2
     panel = next((p for p in (96, 64, 48, 32, 16, 8) if k % p == 0), None)
     if panel is None:
-        lower = jnp.linalg.cholesky(unpack_sym(packed))
+        lower = jnp.linalg.cholesky(unpack_sym(packed[0] + packed[1]))
         eye = jnp.eye(k, dtype=jnp.float32)
         inverse = lax.linalg.triangular_solve(lower, eye, left_side=True, lower=True)
         basis = [
@@ -169,10 +177,10 @@
             jax.ShapeDtypeStruct(y_stat.shape[::-1], jnp.bfloat16),
             jax.ShapeDtypeStruct(y_rot.shape, jnp.bfloat16),
         ),
-        in_specs=[vmem, vmem, vmem],
+        in_specs=[vmem, vmem, vmem, vmem],
         out_specs=(vmem, vmem, vmem),
         scratch_shapes=[pltpu.VMEM((k, 2 * k), jnp.float32)],
-    )(packed, y_stat, y_rot)
+    )(*packed, y_stat, y_rot)
     return upper, basis_stat_t.T, basis_rot
 
 
@@ -207,7 +215,7 @@
     n = n_grp * n_rows
     if n & (n - 1) or n_rows & (n_rows - 1) or (CAP * k) % packed.shape[1]:
         arrived = lax.all_to_all(outgoing, "rows", split_axis=0, concat_axis=0, tiled=True)
-        packed = lax.psum(packed, AXES)
+        packed = (lax.psum(packed, AXES), jnp.zeros_like(packed))
     else:
         packed, arrived = all_sum_and_route(packed, outgoing, n, n_rows)
     arrived = arrived.reshape(n_rows * CAP, -1)

time: 42 us -> 42.1 us (level)
  other arithmetic: 1.48 us -> 0.83 us
  local copies, waits for them, and re-layouts: 1.46 us -> 2.11 us
    add x3 -> x2, other arithmetic: 0.68 us -> 0.03 us  [all_sum_and_route(): x = x + got[:x.shape[0]]]
    slice x0 -> x1, local copies, waits for them, and re-layouts: none -> 0.64 us  [all_sum_and_route(): last = got[:x.shape[0]]]
where the time goes in v13:
time: 42.1 us; the launch traced here: 41.6 us
  waiting for transfers between devices  12.4 us (29%)
  Pallas kernels  10.6 us (25%)
  starting transfers between devices  10.2 us (24%)
  matrix products  3.8 us (9%)
  local copies, waits for them, and re-layouts  2.11 us (5%)
  between operations  1.62 us (4%)
  other arithmetic  0.83 us (2%)
    pallas_call x1, Pallas kernels, factor_and_basis(): pl.pallas_call(functools.partial(_chol_kernel, panel=panel), out_shape=(j...  10.6 us
    ppermute x3, waiting for transfers between devices, all_sum_and_route(): got = lax.ppermute(packet, AXES, perm)  7.22 us
    ppermute x3, starting transfers between devices, all_sum_and_route(): got = lax.ppermute(packet, AXES, perm)  5.33 us
    ppermute x2, waiting for transfers between devices, all_sum_and_route(): got = lax.ppermute(x, AXES, perm)  5.21 us
    ppermute x2, starting transfers between devices, all_sum_and_route(): got = lax.ppermute(x, AXES, perm)  4.89 us
    dot_general x2, matrix products, sketch_block(): jnp.dot(block, omega, preferred_element_type=jnp.float32)  2.87 us
  transfers between devices with their start and end apart: 5, of which 5 were waited for; matrix products, arithmetic and copies ran while one was open for 1% of the time, Pallas kernels for 0%

profile of v13, /device:TPU:0, one launch (start us, length us, event | category | flops | bytes accessed | tf_op | source)
XLA Modules:
  0.0 41.6 jit_solution(10414516673172396532)
XLA Ops:
  1.5 1.1 %convolution_convert_fusion.2 = bf16[32,192]{1,0:T(8,128)(2,1)S(1)} fusion(bf16[32,512]{1,0:T(8,128)(2,1)} %param.6, bf16[512,192]{0,1:T(8,128)(2,1)} %param.9), kind=kOutput, calls=%fused_computation.4 | convolution fusion | flops 6297600 | bytes 241664 | tf_op jit(solution)/shard_map/dot_general | solution.py:17
  2.6 1.8 %convolution_convert_fusion.ys_ref = bf16[2560,192]{1,0:T(8,128)(2,1)S(1)} fusion(bf16[2560,512]{1,0:T(8,128)(2,1)S(1)} %copy-done, bf16[512,192]{0,1:T(8,128)(2,1)} %param.9), kind=kOutput, calls=%fused_computation | convolution fusion | flops 503808000 | bytes 3801088 | tf_op jit(solution)/shard_map/dot_general | solution.py:17
  4.4 0.3 fusion.4
  4.7 0.5 %fusion = f32[192,192]{1,0:T(8,128)S(1)} fusion(f32[192,192]{1,0:T(8,128)S(1)} %fusion.4, bf16[2560,192]{1,0:T(8,128)(2,1)S(1)} %convolution_convert_fusion.ys_ref), kind=kOutput, calls=%fused_computation.2 | convolution fusion | flops 188817408 | bytes 1277952 | tf_op jit(solution)/shard_map/dot_general | solution.py:208
  5.2 0.2 copy-done.1
  5.4 0.1 fusion.13
  5.5 3.1 %collective-permute-start = (f32[193,96]{1,0:T(8,128)S(1)}, f32[193,96]{1,0:T(8,128)S(1)}, u32[]{:S(2)}, u32[]{:S(2)}) collective-permute-start(f32[193,96]{1,0:T(8,128)S(1)} %pad_maximum_fusion.3), channel_id=1, source_target_pairs={{0,16},{1,17},{2,18},{3,19},{4,20},{5,21},{6,22},{7,23},{8,24},{9,... | collective-permute-start | bytes 222344 | tf_op jit(solution)/shard_map/ppermute | solution.py:52
  8.6 0.1 fusion.8
  8.7 0.1 reduce_window_sum.11
  8.7 0.2 select_reduce_fusion.1
  8.9 0.1 convolution_convert_fusion.1
  9.1 2.4 %collective-permute-done = f32[193,96]{1,0:T(8,128)S(1)} collective-permute-done((f32[193,96]{1,0:T(8,128)S(1)}, f32[193,96]{1,0:T(8,128)S(1)}, u32[]{:S(2)}, u32[]{:S(2)}) %collective-permute-start) | collective-permute-done | bytes 74144 | tf_op jit(solution)/shard_map/ppermute | solution.py:52
  11.5 1.8 %collective-permute-start.1 = (f32[193,96]{1,0:T(8,128)S(1)}, f32[193,96]{1,0:T(8,128)S(1)}, u32[]{:S(2)}, u32[]{:S(2)}) collective-permute-start(f32[193,96]{1,0:T(8,128)S(1)} %fusion.12), channel_id=1, source_target_pairs={{0,8},{1,9},{2,10},{3,11},{4,12},{5,13},{6,14},{7,15},{8,0},{9,1},... | collective-permute-start | bytes 222344 | tf_op jit(solution)/shard_map/ppermute | solution.py:52
  13.3 0.1 reshape.123
  13.4 2.8 %collective-permute-done.1 = f32[193,96]{1,0:T(8,128)S(1)} collective-permute-done((f32[193,96]{1,0:T(8,128)S(1)}, f32[193,96]{1,0:T(8,128)S(1)}, u32[]{:S(2)}, u32[]{:S(2)}) %collective-permute-start.1) | collective-permute-done | bytes 74144 | tf_op jit(solution)/shard_map/ppermute | solution.py:52
  16.3 2.9 %collective-permute-start.2 = (f32[241,96]{1,0:T(8,128)S(1)}, f32[241,96]{1,0:T(8,128)S(1)}, u32[]{:S(2)}, u32[]{:S(2)}) collective-permute-start(f32[241,96]{1,0:T(8,128)S(1)} %pad_maximum_fusion), channel_id=1, source_target_pairs={{0,4},{1,5},{2,6},{3,7},{4,0},{5,1},{6,2},{7,3},{8,12},{9,13},{10,... | collective-permute-start | bytes 277640 | tf_op jit(solution)/shard_map/ppermute | solution.py:63
  19.2 3.0 %collective-permute-done.2 = f32[241,96]{1,0:T(8,128)S(1)} collective-permute-done((f32[241,96]{1,0:T(8,128)S(1)}, f32[241,96]{1,0:T(8,128)S(1)}, u32[]{:S(2)}, u32[]{:S(2)}) %collective-permute-start.2) | collective-permute-done | bytes 92576 | tf_op jit(solution)/shard_map/ppermute | solution.py:63
  22.2 0.1 convert_element_type.86
  22.3 0.1 reshape.124
  22.4 2.3 %collective-permute-start.3 = (f32[241,96]{1,0:T(8,128)S(1)}, f32[241,96]{1,0:T(8,128)S(1)}, u32[]{:S(2)}, u32[]{:S(2)}) collective-permute-start(f32[241,96]{1,0:T(8,128)S(1)} %pad_maximum_fusion.1), channel_id=1, source_target_pairs={{0,2},{1,3},{2,0},{3,1},{4,6},{5,7},{6,4},{7,5},{8,10},{9,11},{10,... | collective-permute-start | bytes 277640 | tf_op jit(solution)/shard_map/ppermute | solution.py:63
  24.8 2.9 %collective-permute-done.3 = f32[241,96]{1,0:T(8,128)S(1)} collective-permute-done((f32[241,96]{1,0:T(8,128)S(1)}, f32[241,96]{1,0:T(8,128)S(1)}, u32[]{:S(2)}, u32[]{:S(2)}) %collective-permute-start.3) | collective-permute-done | bytes 92576 | tf_op jit(solution)/shard_map/ppermute | solution.py:63
  27.7 0.1 convert_element_type.89
  27.8 0.1 fusion.2
  27.9 0.1 reshape.125
  28.0 0.1 collective-permute-start.4
  28.1 1.3 %collective-permute-done.4 = f32[241,96]{1,0:T(8,128)S(1)} collective-permute-done((f32[241,96]{1,0:T(8,128)S(1)}, f32[241,96]{1,0:T(8,128)S(1)}, u32[]{:S(2)}, u32[]{:S(2)}) %collective-permute-start.4) | collective-permute-done | bytes 92576 | tf_op jit(solution)/shard_map/ppermute | solution.py:63
  29.5 0.1 convert_element_type.96
  29.6 0.1 broadcast_select_fusion.1
  29.6 0.1 pad_maximum_fusion.5
  29.7 0.6 %reshape_reshape.12.yr_ref = bf16[48,192]{1,0:T(8,128)(2,1)} reshape(bf16[4,2,1,6,192]{4,3,1,0,2:T(8,128)(2,1)S(1)} %copy.28) | data formatting | bytes 36864 | tf_op jit(solution)/shard_map/reshape;reshape | solution.py:221
  30.4 0.6 %slice.82.g2_ref = f32[193,96]{1,0:T(8,128)} slice(f32[241,96]{1,0:T(8,128)S(1)} %collective-permute-done.4), slice={[0:193], [0:96]} | slice | bytes 148224 | tf_op jit(solution)/shard_map/slice | solution.py:65
  31.0 10.6 %shard_map.76 = (f32[192,192]{1,0:T(8,128)}, bf16[192,2560]{1,0:T(8,128)(2,1)}, bf16[48,192]{1,0:T(8,128)(2,1)}) custom-call(f32[193,96]{1,0:T(8,128)} %copy-done.2, f32[193,96]{1,0:T(8,128)} %slice.82.g2_ref, bf16[2560,192]{1,0:T(8,128)(2,1)} %copy-done.1, bf16[48,192]{1,0:T(8,128)(2,1)} %reshape_reshape.12.yr_ref), custom_call_target="tpu_custom_call" | custom-call | tf_op jit(solution)/shard_map/pallas_call | solution.py:173
  (28 shorter events, 0.3 us)
Async XLA Ops:
  0.6 1.9 %copy-start = (bf16[2560,512]{1,0:T(8,128)(2,1)S(1)}, bf16[2560,512]{1,0:T(8,128)(2,1)}, u32[]{:S(2)}) copy-start(bf16[2560,512]{1,0:T(8,128)(2,1)} %param.5) | copy-start | bytes 7864324
  4.4 1.1 %copy-start.1 = (bf16[2560,192]{1,0:T(8,128)(2,1)}, bf16[2560,192]{1,0:T(8,128)(2,1)S(1)}, u32[]{:S(2)}) copy-start(bf16[2560,192]{1,0:T(8,128)(2,1)S(1)} %convolution_convert_fusion.ys_ref) | copy-start | bytes 2949124
  4.7 4.0 %copy-start.3 = (s32[32,1]{0,1:T(1,128)S(1)}, s32[32,1]{0,1:T(1,128)}, u32[]{:S(2)}) copy-start(s32[32,1]{0,1:T(1,128)} %param.7) | copy-start | bytes 388
  5.5 5.9 %collective-permute-start = (f32[193,96]{1,0:T(8,128)S(1)}, f32[193,96]{1,0:T(8,128)S(1)}, u32[]{:S(2)}, u32[]{:S(2)}) collective-permute-start(f32[193,96]{1,0:T(8,128)S(1)} %pad_maximum_fusion.3), channel_id=1, source_target_pairs={{0,16},{1,17},{2,18},{3,19},{4,20},{5,21},{6,22},{7,23},{8,24},{9,... | collective-permute-start | bytes 222344 | tf_op jit(solution)/shard_map/ppermute | solution.py:52
  11.5 4.7 %collective-permute-start.1 = (f32[193,96]{1,0:T(8,128)S(1)}, f32[193,96]{1,0:T(8,128)S(1)}, u32[]{:S(2)}, u32[]{:S(2)}) collective-permute-start(f32[193,96]{1,0:T(8,128)S(1)} %fusion.12), channel_id=1, source_target_pairs={{0,8},{1,9},{2,10},{3,11},{4,12},{5,13},{6,14},{7,15},{8,0},{9,1},... | collective-permute-start | bytes 222344 | tf_op jit(solution)/shard_map/ppermute | solution.py:52
  16.3 5.9 %collective-permute-start.2 = (f32[241,96]{1,0:T(8,128)S(1)}, f32[241,96]{1,0:T(8,128)S(1)}, u32[]{:S(2)}, u32[]{:S(2)}) collective-permute-start(f32[241,96]{1,0:T(8,128)S(1)} %pad_maximum_fusion), channel_id=1, source_target_pairs={{0,4},{1,5},{2,6},{3,7},{4,0},{5,1},{6,2},{7,3},{8,12},{9,13},{10,... | collective-permute-start | bytes 277640 | tf_op jit(solution)/shard_map/ppermute | solution.py:63
  22.4 5.2 %collective-permute-start.3 = (f32[241,96]{1,0:T(8,128)S(1)}, f32[241,96]{1,0:T(8,128)S(1)}, u32[]{:S(2)}, u32[]{:S(2)}) collective-permute-start(f32[241,96]{1,0:T(8,128)S(1)} %pad_maximum_fusion.1), channel_id=1, source_target_pairs={{0,2},{1,3},{2,0},{3,1},{4,6},{5,7},{6,4},{7,5},{8,10},{9,11},{10,... | collective-permute-start | bytes 277640 | tf_op jit(solution)/shard_map/ppermute | solution.py:63
  28.0 3.0 %copy-start.2 = (f32[193,96]{1,0:T(8,128)}, f32[193,96]{1,0:T(8,128)S(1)}, u32[]{:S(2)}) copy-start(f32[193,96]{1,0:T(8,128)S(1)} %slice_add_fusion.g_ref) | copy-start | bytes 222340
  28.0 1.4 %collective-permute-start.4 = (f32[241,96]{1,0:T(8,128)S(1)}, f32[241,96]{1,0:T(8,128)S(1)}, u32[]{:S(2)}, u32[]{:S(2)}) collective-permute-start(f32[241,96]{1,0:T(8,128)S(1)} %pad_maximum_fusion.2), channel_id=1, source_target_pairs={{0,1},{1,0},{2,3},{3,2},{4,5},{5,4},{6,7},{7,6},{8,9},{9,8},{10,11... | collective-permute-start | bytes 277640 | tf_op jit(solution)/shard_map/ppermute | solution.py:63

commit v14 on v12

--- a/solution.py
+++ b/solution.py
@@ -134,6 +134,15 @@
         rest = rest - term.astype(jnp.float32)
     dims = (((1,), (1,)), ((), ()))
     for y_ref, o_ref, flip in ((ys_ref, bs_ref, True), (yr_ref, br_ref, False)):
+        if len(y_ref.shape) == 3:
+            cap = y_ref.shape[1]
+            for s in range(y_ref.shape[0]):
+                acc = None
+                for part in parts:
+                    t = lax.dot_general(y_ref[s], part, dims, preferred_element_type=jnp.float32)
+                    acc = t if acc is None else acc + t
+                o_ref[s * cap : (s + 1) * cap, :] = acc.astype(o_ref.dtype)
+            continue
         n = y_ref.shape[0]
         step = 512 if n % 512 == 0 else n
         for i in range(0, n, step):
@@ -158,7 +167,7 @@
         inverse = lax.linalg.triangular_solve(lower, eye, left_side=True, lower=True)
         basis = [
             jnp.dot(y.astype(jnp.float32), inverse.T, precision=HIGHEST).astype(jnp.bfloat16)
-            for y in (y_stat, y_rot)
+            for y in (y_stat, y_rot.reshape(-1, y_rot.shape[-1]))
         ]
         return lower.T, basis[0], basis[1]
     vmem = pl.BlockSpec(memory_space=pltpu.VMEM)
@@ -167,7 +176,7 @@
         out_shape=(
             jax.ShapeDtypeStruct((k, k), jnp.float32),
             jax.ShapeDtypeStruct(y_stat.shape[::-1], jnp.bfloat16),
-            jax.ShapeDtypeStruct(y_rot.shape, jnp.bfloat16),
+            jax.ShapeDtypeStruct((y_rot.shape[0] * y_rot.shape[1], y_rot.shape[2]), jnp.bfloat16),
         ),
         in_specs=[vmem, vmem, vmem],
         out_specs=(vmem, vmem, vmem),
@@ -210,7 +219,8 @@
         packed = lax.psum(packed, AXES)
     else:
         packed, arrived = all_sum_and_route(packed, outgoing, n, n_rows)
-    arrived = arrived.reshape(n_rows * CAP, -1)
+    if n_rows > 16:
+        arrived = arrived.reshape(1, n_rows * CAP, -1)
     upper, basis_stat, basis_rot = factor_and_basis(packed, sketch_stat, arrived)
     return (basis_stat, basis_rot, upper)
 

time: 42 us -> 42.1 us (level)
    another operation x1 -> x0, local copies, waits for them, and re-layouts: 0.63 us -> none  [per_device(): arrived = arrived.reshape(n_rows * CAP, -1)]
    another operation x2, local copies, waits for them, and re-layouts: 0.03 us -> 0.64 us  [all_sum_and_route(): held = jnp.stack([lo, hi], axis=1).reshape(held.shape)]
where the time goes in v14:
time: 42.1 us; the launch traced here: 41.6 us
  waiting for transfers between devices  12.4 us (29%)
  Pallas kernels  10.6 us (25%)
  starting transfers between devices  10.2 us (24%)
  matrix products  3.8 us (9%)
  between operations  1.6 us (4%)
  other arithmetic  1.48 us (4%)
  local copies, waits for them, and re-layouts  1.44 us (3%)
    pallas_call x1, Pallas kernels, factor_and_basis(): pl.pallas_call(functools.partial(_chol_kernel, panel=panel), out_shape=(j...  10.6 us
    ppermute x3, waiting for transfers between devices, all_sum_and_route(): got = lax.ppermute(packet, AXES, perm)  7.22 us
    ppermute x3, starting transfers between devices, all_sum_and_route(): got = lax.ppermute(packet, AXES, perm)  5.33 us
    ppermute x2, waiting for transfers between devices, all_sum_and_route(): x = x + lax.ppermute(x, AXES, perm)  5.21 us
    ppermute x2, starting transfers between devices, all_sum_and_route(): x = x + lax.ppermute(x, AXES, perm)  4.89 us
    dot_general x2, matrix products, sketch_block(): jnp.dot(block, omega, preferred_element_type=jnp.float32)  2.87 us
  transfers between devices with their start and end apart: 5, of which 5 were waited for; matrix products, arithmetic and copies ran while one was open for 1% of the time, Pallas kernels for 0%

profile of v14, /device:TPU:0, one launch (start us, length us, event | category | flops | bytes accessed | tf_op | source)
XLA Modules:
  0.0 41.6 jit_solution(17520266894135854378)
XLA Ops:
  1.5 1.1 %convolution_convert_fusion.2 = bf16[32,192]{1,0:T(8,128)(2,1)S(1)} fusion(bf16[32,512]{1,0:T(8,128)(2,1)} %param.6, bf16[512,192]{0,1:T(8,128)(2,1)} %param.9), kind=kOutput, calls=%fused_computation.4 | convolution fusion | flops 6297600 | bytes 241664 | tf_op jit(solution)/shard_map/dot_general | solution.py:17
  2.6 1.8 %convolution_convert_fusion.ys_ref = bf16[2560,192]{1,0:T(8,128)(2,1)S(1)} fusion(bf16[2560,512]{1,0:T(8,128)(2,1)S(1)} %copy-done, bf16[512,192]{0,1:T(8,128)(2,1)} %param.9), kind=kOutput, calls=%fused_computation | convolution fusion | flops 503808000 | bytes 3801088 | tf_op jit(solution)/shard_map/dot_general | solution.py:17
  4.4 0.3 fusion.4
  4.7 0.5 %fusion = f32[192,192]{1,0:T(8,128)S(1)} fusion(f32[192,192]{1,0:T(8,128)S(1)} %fusion.4, bf16[2560,192]{1,0:T(8,128)(2,1)S(1)} %convolution_convert_fusion.ys_ref), kind=kOutput, calls=%fused_computation.2 | convolution fusion | flops 188817408 | bytes 1277952 | tf_op jit(solution)/shard_map/dot_general | solution.py:209
  5.2 0.2 copy-done.1
  5.4 0.1 fusion.13
  5.5 3.1 %collective-permute-start = (f32[193,96]{1,0:T(8,128)S(1)}, f32[193,96]{1,0:T(8,128)S(1)}, u32[]{:S(2)}, u32[]{:S(2)}) collective-permute-start(f32[193,96]{1,0:T(8,128)S(1)} %pad_maximum_fusion.3), channel_id=1, source_target_pairs={{0,16},{1,17},{2,18},{3,19},{4,20},{5,21},{6,22},{7,23},{8,24},{9,... | collective-permute-start | bytes 222344 | tf_op jit(solution)/shard_map/ppermute | solution.py:51
  8.6 0.1 fusion.8
  8.7 0.1 reduce_window_sum.11
  8.7 0.2 select_reduce_fusion.1
  8.9 0.1 convolution_convert_fusion.1
  9.1 2.4 %collective-permute-done = f32[193,96]{1,0:T(8,128)S(1)} collective-permute-done((f32[193,96]{1,0:T(8,128)S(1)}, f32[193,96]{1,0:T(8,128)S(1)}, u32[]{:S(2)}, u32[]{:S(2)}) %collective-permute-start) | collective-permute-done | bytes 74144 | tf_op jit(solution)/shard_map/ppermute | solution.py:51
  11.5 1.8 %collective-permute-start.1 = (f32[193,96]{1,0:T(8,128)S(1)}, f32[193,96]{1,0:T(8,128)S(1)}, u32[]{:S(2)}, u32[]{:S(2)}) collective-permute-start(f32[193,96]{1,0:T(8,128)S(1)} %fusion.12), channel_id=1, source_target_pairs={{0,8},{1,9},{2,10},{3,11},{4,12},{5,13},{6,14},{7,15},{8,0},{9,1},... | collective-permute-start | bytes 222344 | tf_op jit(solution)/shard_map/ppermute | solution.py:51
  13.3 0.1 reshape.127
  13.4 2.8 %collective-permute-done.1 = f32[193,96]{1,0:T(8,128)S(1)} collective-permute-done((f32[193,96]{1,0:T(8,128)S(1)}, f32[193,96]{1,0:T(8,128)S(1)}, u32[]{:S(2)}, u32[]{:S(2)}) %collective-permute-start.1) | collective-permute-done | bytes 74144 | tf_op jit(solution)/shard_map/ppermute | solution.py:51
  16.3 2.9 %collective-permute-start.2 = (f32[241,96]{1,0:T(8,128)S(1)}, f32[241,96]{1,0:T(8,128)S(1)}, u32[]{:S(2)}, u32[]{:S(2)}) collective-permute-start(f32[241,96]{1,0:T(8,128)S(1)} %pad_maximum_fusion), channel_id=1, source_target_pairs={{0,4},{1,5},{2,6},{3,7},{4,0},{5,1},{6,2},{7,3},{8,12},{9,13},{10,... | collective-permute-start | bytes 277640 | tf_op jit(solution)/shard_map/ppermute | solution.py:58
  19.2 3.0 %collective-permute-done.2 = f32[241,96]{1,0:T(8,128)S(1)} collective-permute-done((f32[241,96]{1,0:T(8,128)S(1)}, f32[241,96]{1,0:T(8,128)S(1)}, u32[]{:S(2)}, u32[]{:S(2)}) %collective-permute-start.2) | collective-permute-done | bytes 92576 | tf_op jit(solution)/shard_map/ppermute | solution.py:58
  22.2 0.1 convert_element_type.86
  22.3 0.1 reshape.128
  22.4 2.3 %collective-permute-start.3 = (f32[241,96]{1,0:T(8,128)S(1)}, f32[241,96]{1,0:T(8,128)S(1)}, u32[]{:S(2)}, u32[]{:S(2)}) collective-permute-start(f32[241,96]{1,0:T(8,128)S(1)} %pad_maximum_fusion.1), channel_id=1, source_target_pairs={{0,2},{1,3},{2,0},{3,1},{4,6},{5,7},{6,4},{7,5},{8,10},{9,11},{10,... | collective-permute-start | bytes 277640 | tf_op jit(solution)/shard_map/ppermute | solution.py:58
  24.8 2.9 %collective-permute-done.3 = f32[241,96]{1,0:T(8,128)S(1)} collective-permute-done((f32[241,96]{1,0:T(8,128)S(1)}, f32[241,96]{1,0:T(8,128)S(1)}, u32[]{:S(2)}, u32[]{:S(2)}) %collective-permute-start.3) | collective-permute-done | bytes 92576 | tf_op jit(solution)/shard_map/ppermute | solution.py:58
  27.7 0.1 convert_element_type.89
  27.8 0.1 fusion.2
  27.9 0.1 reshape.129
  28.0 0.1 collective-permute-start.4
  28.1 1.3 %collective-permute-done.4 = f32[241,96]{1,0:T(8,128)S(1)} collective-permute-done((f32[241,96]{1,0:T(8,128)S(1)}, f32[241,96]{1,0:T(8,128)S(1)}, u32[]{:S(2)}, u32[]{:S(2)}) %collective-permute-start.4) | collective-permute-done | bytes 92576 | tf_op jit(solution)/shard_map/ppermute | solution.py:58
  29.5 0.1 convert_element_type.96
  29.5 0.1 broadcast_select_fusion.1
  29.6 0.1 pad_maximum_fusion.5
  29.7 0.6 %copy.28 = bf16[4,2,1,6,192]{4,3,1,0,2:T(8,128)(2,1)} copy(bf16[4,2,1,6,192]{4,1,3,0,2:T(2,128)(2,1)S(1)} %pad_maximum_fusion.5) | data formatting | bytes 36864 | tf_op jit(solution)/shard_map/stack | solution.py:63
  30.3 0.7 %slice_add_fusion.g_ref = f32[193,96]{1,0:T(8,128)} fusion(f32[193,96]{1,0:T(8,128)S(1)} %slice_add_fusion.1, f32[241,96]{1,0:T(8,128)S(1)} %collective-permute-done.4), kind=kLoop, calls=%fused_computation.8 | loop fusion | flops 18528 | bytes 222336 | tf_op jit(solution)/shard_map/add | solution.py:59
  31.0 10.6 %shard_map.76 = (f32[192,192]{1,0:T(8,128)}, bf16[192,2560]{1,0:T(8,128)(2,1)}, bf16[48,192]{1,0:T(8,128)(2,1)}) custom-call(f32[193,96]{1,0:T(8,128)} %slice_add_fusion.g_ref, bf16[2560,192]{1,0:T(8,128)(2,1)} %copy-done.1, bf16[8,6,192]{2,1,0:T(8,128)(2,1)} %bitcast.30), custom_call_target="tpu_custom_call" | custom-call | tf_op jit(solution)/shard_map/pallas_call | solution.py:174
  (25 shorter events, 0.3 us)
Async XLA Ops:
  0.6 1.9 %copy-start = (bf16[2560,512]{1,0:T(8,128)(2,1)S(1)}, bf16[2560,512]{1,0:T(8,128)(2,1)}, u32[]{:S(2)}) copy-start(bf16[2560,512]{1,0:T(8,128)(2,1)} %param.5) | copy-start | bytes 7864324
  4.4 1.1 %copy-start.1 = (bf16[2560,192]{1,0:T(8,128)(2,1)}, bf16[2560,192]{1,0:T(8,128)(2,1)S(1)}, u32[]{:S(2)}) copy-start(bf16[2560,192]{1,0:T(8,128)(2,1)S(1)} %convolution_convert_fusion.ys_ref) | copy-start | bytes 2949124
  4.7 4.0 %copy-start.2 = (s32[32,1]{0,1:T(1,128)S(1)}, s32[32,1]{0,1:T(1,128)}, u32[]{:S(2)}) copy-start(s32[32,1]{0,1:T(1,128)} %param.7) | copy-start | bytes 388
  5.5 5.9 %collective-permute-start = (f32[193,96]{1,0:T(8,128)S(1)}, f32[193,96]{1,0:T(8,128)S(1)}, u32[]{:S(2)}, u32[]{:S(2)}) collective-permute-start(f32[193,96]{1,0:T(8,128)S(1)} %pad_maximum_fusion.3), channel_id=1, source_target_pairs={{0,16},{1,17},{2,18},{3,19},{4,20},{5,21},{6,22},{7,23},{8,24},{9,... | collective-permute-start | bytes 222344 | tf_op jit(solution)/shard_map/ppermute | solution.py:51
  11.5 4.7 %collective-permute-start.1 = (f32[193,96]{1,0:T(8,128)S(1)}, f32[193,96]{1,0:T(8,128)S(1)}, u32[]{:S(2)}, u32[]{:S(2)}) collective-permute-start(f32[193,96]{1,0:T(8,128)S(1)} %fusion.12), channel_id=1, source_target_pairs={{0,8},{1,9},{2,10},{3,11},{4,12},{5,13},{6,14},{7,15},{8,0},{9,1},... | collective-permute-start | bytes 222344 | tf_op jit(solution)/shard_map/ppermute | solution.py:51
  16.3 5.9 %collective-permute-start.2 = (f32[241,96]{1,0:T(8,128)S(1)}, f32[241,96]{1,0:T(8,128)S(1)}, u32[]{:S(2)}, u32[]{:S(2)}) collective-permute-start(f32[241,96]{1,0:T(8,128)S(1)} %pad_maximum_fusion), channel_id=1, source_target_pairs={{0,4},{1,5},{2,6},{3,7},{4,0},{5,1},{6,2},{7,3},{8,12},{9,13},{10,... | collective-permute-start | bytes 277640 | tf_op jit(solution)/shard_map/ppermute | solution.py:58
  22.4 5.2 %collective-permute-start.3 = (f32[241,96]{1,0:T(8,128)S(1)}, f32[241,96]{1,0:T(8,128)S(1)}, u32[]{:S(2)}, u32[]{:S(2)}) collective-permute-start(f32[241,96]{1,0:T(8,128)S(1)} %pad_maximum_fusion.1), channel_id=1, source_target_pairs={{0,2},{1,3},{2,0},{3,1},{4,6},{5,7},{6,4},{7,5},{8,10},{9,11},{10,... | collective-permute-start | bytes 277640 | tf_op jit(solution)/shard_map/ppermute | solution.py:58
  28.0 1.4 %collective-permute-start.4 = (f32[241,96]{1,0:T(8,128)S(1)}, f32[241,96]{1,0:T(8,128)S(1)}, u32[]{:S(2)}, u32[]{:S(2)}) collective-permute-start(f32[241,96]{1,0:T(8,128)S(1)} %pad_maximum_fusion.2), channel_id=1, source_target_pairs={{0,1},{1,0},{2,3},{3,2},{4,5},{5,4},{6,7},{7,6},{8,9},{9,8},{10,11... | collective-permute-start | bytes 277640 | tf_op jit(solution)/shard_map/ppermute | solution.py:58

commit v15 on v12

--- a/solution.py
+++ b/solution.py
@@ -121,7 +121,7 @@
         if end < k:
             part = jnp.where((lane >= end) & (lane < k), pan, 0.0)[:, :kp]
             upd = lax.dot_general(
-                part, pan, (((0,), (0,)), ((), ())), precision=HIGHEST,
+                part, pan, (((0,), (0,)), ((), ())), precision=lax.Precision.HIGH,
                 preferred_element_type=jnp.float32,
             )
             b_ref[end:, :] = b_ref[end:, :] - upd[end:k]

time: 42 us -> 41.6 us (level)
  no operation moved by 1% of the time
where the time goes in v15:
time: 41.6 us; the launch traced here: 41.1 us
  waiting for transfers between devices  12.4 us (30%)
  starting transfers between devices  10.2 us (25%)
  Pallas kernels  10.1 us (24%)
  matrix products  3.8 us (9%)
  between operations  1.61 us (4%)
  other arithmetic  1.48 us (4%)
  local copies, waits for them, and re-layouts  1.46 us (4%)
    pallas_call x1, Pallas kernels, factor_and_basis(): pl.pallas_call(functools.partial(_chol_kernel, panel=panel), out_shape=(j...  10.1 us
    ppermute x3, waiting for transfers between devices, all_sum_and_route(): got = lax.ppermute(packet, AXES, perm)  7.22 us
    ppermute x3, starting transfers between devices, all_sum_and_route(): got = lax.ppermute(packet, AXES, perm)  5.33 us
    ppermute x2, waiting for transfers between devices, all_sum_and_route(): x = x + lax.ppermute(x, AXES, perm)  5.21 us
    ppermute x2, starting transfers between devices, all_sum_and_route(): x = x + lax.ppermute(x, AXES, perm)  4.89 us
    dot_general x2, matrix products, sketch_block(): jnp.dot(block, omega, preferred_element_type=jnp.float32)  2.87 us
  transfers between devices with their start and end apart: 5, of which 5 were waited for; matrix products, arithmetic and copies ran while one was open for 1% of the time, Pallas kernels for 0%

profile of v15, /device:TPU:0, one launch (start us, length us, event | category | flops | bytes accessed | tf_op | source)
XLA Modules:
  0.0 41.1 jit_solution(13654618155433093293)
XLA Ops:
  1.5 1.1 %convolution_convert_fusion.2 = bf16[32,192]{1,0:T(8,128)(2,1)S(1)} fusion(bf16[32,512]{1,0:T(8,128)(2,1)} %param.6, bf16[512,192]{0,1:T(8,128)(2,1)} %param.9), kind=kOutput, calls=%fused_computation.4 | convolution fusion | flops 6297600 | bytes 241664 | tf_op jit(solution)/shard_map/dot_general | solution.py:17
  2.6 1.8 %convolution_convert_fusion.ys_ref = bf16[2560,192]{1,0:T(8,128)(2,1)S(1)} fusion(bf16[2560,512]{1,0:T(8,128)(2,1)S(1)} %copy-done, bf16[512,192]{0,1:T(8,128)(2,1)} %param.9), kind=kOutput, calls=%fused_computation | convolution fusion | flops 503808000 | bytes 3801088 | tf_op jit(solution)/shard_map/dot_general | solution.py:17
  4.4 0.3 fusion.4
  4.7 0.5 %fusion = f32[192,192]{1,0:T(8,128)S(1)} fusion(f32[192,192]{1,0:T(8,128)S(1)} %fusion.4, bf16[2560,192]{1,0:T(8,128)(2,1)S(1)} %convolution_convert_fusion.ys_ref), kind=kOutput, calls=%fused_computation.2 | convolution fusion | flops 188817408 | bytes 1277952 | tf_op jit(solution)/shard_map/dot_general | solution.py:200
  5.2 0.2 copy-done.1
  5.4 0.1 fusion.13
  5.5 3.1 %collective-permute-start = (f32[193,96]{1,0:T(8,128)S(1)}, f32[193,96]{1,0:T(8,128)S(1)}, u32[]{:S(2)}, u32[]{:S(2)}) collective-permute-start(f32[193,96]{1,0:T(8,128)S(1)} %pad_maximum_fusion.3), channel_id=1, source_target_pairs={{0,16},{1,17},{2,18},{3,19},{4,20},{5,21},{6,22},{7,23},{8,24},{9,... | collective-permute-start | bytes 222344 | tf_op jit(solution)/shard_map/ppermute | solution.py:51
  8.6 0.1 fusion.8
  8.7 0.1 reduce_window_sum.11
  8.7 0.2 select_reduce_fusion.1
  8.9 0.1 convolution_convert_fusion.1
  9.1 2.4 %collective-permute-done = f32[193,96]{1,0:T(8,128)S(1)} collective-permute-done((f32[193,96]{1,0:T(8,128)S(1)}, f32[193,96]{1,0:T(8,128)S(1)}, u32[]{:S(2)}, u32[]{:S(2)}) %collective-permute-start) | collective-permute-done | bytes 74144 | tf_op jit(solution)/shard_map/ppermute | solution.py:51
  11.5 1.8 %collective-permute-start.1 = (f32[193,96]{1,0:T(8,128)S(1)}, f32[193,96]{1,0:T(8,128)S(1)}, u32[]{:S(2)}, u32[]{:S(2)}) collective-permute-start(f32[193,96]{1,0:T(8,128)S(1)} %fusion.12), channel_id=1, source_target_pairs={{0,8},{1,9},{2,10},{3,11},{4,12},{5,13},{6,14},{7,15},{8,0},{9,1},... | collective-permute-start | bytes 222344 | tf_op jit(solution)/shard_map/ppermute | solution.py:51
  13.3 0.1 reshape.123
  13.4 2.8 %collective-permute-done.1 = f32[193,96]{1,0:T(8,128)S(1)} collective-permute-done((f32[193,96]{1,0:T(8,128)S(1)}, f32[193,96]{1,0:T(8,128)S(1)}, u32[]{:S(2)}, u32[]{:S(2)}) %collective-permute-start.1) | collective-permute-done | bytes 74144 | tf_op jit(solution)/shard_map/ppermute | solution.py:51
  16.3 2.9 %collective-permute-start.2 = (f32[241,96]{1,0:T(8,128)S(1)}, f32[241,96]{1,0:T(8,128)S(1)}, u32[]{:S(2)}, u32[]{:S(2)}) collective-permute-start(f32[241,96]{1,0:T(8,128)S(1)} %pad_maximum_fusion), channel_id=1, source_target_pairs={{0,4},{1,5},{2,6},{3,7},{4,0},{5,1},{6,2},{7,3},{8,12},{9,13},{10,... | collective-permute-start | bytes 277640 | tf_op jit(solution)/shard_map/ppermute | solution.py:58
  19.2 3.0 %collective-permute-done.2 = f32[241,96]{1,0:T(8,128)S(1)} collective-permute-done((f32[241,96]{1,0:T(8,128)S(1)}, f32[241,96]{1,0:T(8,128)S(1)}, u32[]{:S(2)}, u32[]{:S(2)}) %collective-permute-start.2) | collective-permute-done | bytes 92576 | tf_op jit(solution)/shard_map/ppermute | solution.py:58
  22.2 0.1 convert_element_type.86
  22.3 0.1 reshape.124
  22.4 2.3 %collective-permute-start.3 = (f32[241,96]{1,0:T(8,128)S(1)}, f32[241,96]{1,0:T(8,128)S(1)}, u32[]{:S(2)}, u32[]{:S(2)}) collective-permute-start(f32[241,96]{1,0:T(8,128)S(1)} %pad_maximum_fusion.1), channel_id=1, source_target_pairs={{0,2},{1,3},{2,0},{3,1},{4,6},{5,7},{6,4},{7,5},{8,10},{9,11},{10,... | collective-permute-start | bytes 277640 | tf_op jit(solution)/shard_map/ppermute | solution.py:58
  24.8 2.9 %collective-permute-done.3 = f32[241,96]{1,0:T(8,128)S(1)} collective-permute-done((f32[241,96]{1,0:T(8,128)S(1)}, f32[241,96]{1,0:T(8,128)S(1)}, u32[]{:S(2)}, u32[]{:S(2)}) %collective-permute-start.3) | collective-permute-done | bytes 92576 | tf_op jit(solution)/shard_map/ppermute | solution.py:58
  27.7 0.1 convert_element_type.89
  27.8 0.1 fusion.2
  27.9 0.1 reshape.125
  28.0 0.1 collective-permute-start.4
  28.1 1.3 %collective-permute-done.4 = f32[241,96]{1,0:T(8,128)S(1)} collective-permute-done((f32[241,96]{1,0:T(8,128)S(1)}, f32[241,96]{1,0:T(8,128)S(1)}, u32[]{:S(2)}, u32[]{:S(2)}) %collective-permute-start.4) | collective-permute-done | bytes 92576 | tf_op jit(solution)/shard_map/ppermute | solution.py:58
  29.5 0.1 convert_element_type.96
  29.5 0.1 broadcast_select_fusion.1
  29.6 0.1 pad_maximum_fusion.5
  29.7 0.6 %reshape_reshape.12.yr_ref = bf16[48,192]{1,0:T(8,128)(2,1)} reshape(bf16[4,2,1,6,192]{4,3,1,0,2:T(8,128)(2,1)S(1)} %copy.28) | data formatting | bytes 36864 | tf_op jit(solution)/shard_map/reshape;reshape | solution.py:213
  30.3 0.7 %slice_add_fusion.g_ref = f32[193,96]{1,0:T(8,128)} fusion(f32[193,96]{1,0:T(8,128)S(1)} %slice_add_fusion.1, f32[241,96]{1,0:T(8,128)S(1)} %collective-permute-done.4), kind=kLoop, calls=%fused_computation.8 | loop fusion | flops 18528 | bytes 222336 | tf_op jit(solution)/shard_map/add | solution.py:59
  31.0 10.1 %shard_map.76 = (f32[192,192]{1,0:T(8,128)}, bf16[192,2560]{1,0:T(8,128)(2,1)}, bf16[48,192]{1,0:T(8,128)(2,1)}) custom-call(f32[193,96]{1,0:T(8,128)} %slice_add_fusion.g_ref, bf16[2560,192]{1,0:T(8,128)(2,1)} %copy-done.1, bf16[48,192]{1,0:T(8,128)(2,1)} %reshape_reshape.12.yr_ref), custom_call_target="tpu_custom_call" | custom-call | tf_op jit(solution)/shard_map/pallas_call | solution.py:165
  (26 shorter events, 0.3 us)
Async XLA Ops:
  0.6 1.9 %copy-start = (bf16[2560,512]{1,0:T(8,128)(2,1)S(1)}, bf16[2560,512]{1,0:T(8,128)(2,1)}, u32[]{:S(2)}) copy-start(bf16[2560,512]{1,0:T(8,128)(2,1)} %param.5) | copy-start | bytes 7864324
  4.4 1.1 %copy-start.1 = (bf16[2560,192]{1,0:T(8,128)(2,1)}, bf16[2560,192]{1,0:T(8,128)(2,1)S(1)}, u32[]{:S(2)}) copy-start(bf16[2560,192]{1,0:T(8,128)(2,1)S(1)} %convolution_convert_fusion.ys_ref) | copy-start | bytes 2949124
  4.7 4.0 %copy-start.2 = (s32[32,1]{0,1:T(1,128)S(1)}, s32[32,1]{0,1:T(1,128)}, u32[]{:S(2)}) copy-start(s32[32,1]{0,1:T(1,128)} %param.7) | copy-start | bytes 388
  5.5 5.9 %collective-permute-start = (f32[193,96]{1,0:T(8,128)S(1)}, f32[193,96]{1,0:T(8,128)S(1)}, u32[]{:S(2)}, u32[]{:S(2)}) collective-permute-start(f32[193,96]{1,0:T(8,128)S(1)} %pad_maximum_fusion.3), channel_id=1, source_target_pairs={{0,16},{1,17},{2,18},{3,19},{4,20},{5,21},{6,22},{7,23},{8,24},{9,... | collective-permute-start | bytes 222344 | tf_op jit(solution)/shard_map/ppermute | solution.py:51
  11.5 4.7 %collective-permute-start.1 = (f32[193,96]{1,0:T(8,128)S(1)}, f32[193,96]{1,0:T(8,128)S(1)}, u32[]{:S(2)}, u32[]{:S(2)}) collective-permute-start(f32[193,96]{1,0:T(8,128)S(1)} %fusion.12), channel_id=1, source_target_pairs={{0,8},{1,9},{2,10},{3,11},{4,12},{5,13},{6,14},{7,15},{8,0},{9,1},... | collective-permute-start | bytes 222344 | tf_op jit(solution)/shard_map/ppermute | solution.py:51
  16.3 5.9 %collective-permute-start.2 = (f32[241,96]{1,0:T(8,128)S(1)}, f32[241,96]{1,0:T(8,128)S(1)}, u32[]{:S(2)}, u32[]{:S(2)}) collective-permute-start(f32[241,96]{1,0:T(8,128)S(1)} %pad_maximum_fusion), channel_id=1, source_target_pairs={{0,4},{1,5},{2,6},{3,7},{4,0},{5,1},{6,2},{7,3},{8,12},{9,13},{10,... | collective-permute-start | bytes 277640 | tf_op jit(solution)/shard_map/ppermute | solution.py:58
  22.4 5.2 %collective-permute-start.3 = (f32[241,96]{1,0:T(8,128)S(1)}, f32[241,96]{1,0:T(8,128)S(1)}, u32[]{:S(2)}, u32[]{:S(2)}) collective-permute-start(f32[241,96]{1,0:T(8,128)S(1)} %pad_maximum_fusion.1), channel_id=1, source_target_pairs={{0,2},{1,3},{2,0},{3,1},{4,6},{5,7},{6,4},{7,5},{8,10},{9,11},{10,... | collective-permute-start | bytes 277640 | tf_op jit(solution)/shard_map/ppermute | solution.py:58
  28.0 1.4 %collective-permute-start.4 = (f32[241,96]{1,0:T(8,128)S(1)}, f32[241,96]{1,0:T(8,128)S(1)}, u32[]{:S(2)}, u32[]{:S(2)}) collective-permute-start(f32[241,96]{1,0:T(8,128)S(1)} %pad_maximum_fusion.2), channel_id=1, source_target_pairs={{0,1},{1,0},{2,3},{3,2},{4,5},{5,4},{6,7},{7,6},{8,9},{9,8},{10,11... | collective-permute-start | bytes 277640 | tf_op jit(solution)/shard_map/ppermute | solution.py:58
